TPU v7x, 1024 devices: a whole 4x4x32 slice. The times are simulated.
1024 devices in a mesh: ctx: 64 (over z_lo, y, core), head: 16 (over x, z_hi).
Axes of the slice: x: 4, y: 4, z: 32 (z_hi: 4, z_lo: 8; z = z_hi * 8 + z_lo), core: 2. Of those that a mesh axis runs over, the one named last changes fastest.
Arguments:
- query_matrix: bfloat16 [32768, 4096], P(('ctx', 'head')), may hold values from -40 to 40
- key_matrix: bfloat16 [32768, 2048], P(('ctx', 'head')), may hold values from -40 to 40
- value_matrix: bfloat16 [32768, 2048], P(('ctx', 'head')), may hold values from -6 to 6
- output_gradient: bfloat16 [32768, 4096], P(('ctx', 'head')), may hold values from -6 to 6
- query_gain: float32 [128], replicated, may hold values from 1 to 3.5
- key_gain: float32 [128], replicated, may hold values from 1 to 3.5
- doc_ids: int32 [32768], replicated, may hold values from 0 to 63, never falling along the last dimension, each value on 1 to 1024 neighbouring positions
Outputs:
- attended: bfloat16 [32768, 4096], P(('ctx', 'head'))
- query_gradient: bfloat16 [32768, 4096], P(('ctx', 'head'))
- key_gradient: bfloat16 [32768, 2048], P(('ctx', 'head'))
- value_gradient: bfloat16 [32768, 2048], P(('ctx', 'head'))
Inputs may be any that keep to these rules, and one draw needn't show every extreme that they name: `doc_ids`: document ids never fall along the sequence; each document holds 1 to 1024 tokens, and one holds exactly 1024.
All inputs are finite; a program needn't handle non-finite values.
Results may differ from a plain program's by a relative error of at most 0.019.
Values may be sent and summed in bfloat16 or wider, within the bound.
No kernel may reach another device: no remote copies, remote signals or barrier semaphores. Data moves between devices by JAX's collectives and lax.ppermute only.
A program may use at most 32 MiB of HBM per device.

v0:
```python
import jax
import jax.numpy as jnp
from jax import lax
from jax.sharding import PartitionSpec as P

HEAD_WIDTH = 128
REACH = 2


CAP_VALUE = 50.0
QUERY_SCALE = 144.0 ** (-0.5)
EPSILON = 1e-06


def passed_along(block, axis, distance):
    devices = range(lax.axis_size(axis))
    route = [(i - distance, i) for i in devices if i - distance in devices]
    return lax.ppermute(block, axis, route)


def for_sending(value):

    def short(part):
        return part.astype(jnp.bfloat16) if part.dtype == jnp.float32 else part

    return jax.tree.map(short, value)


def normalize(value_entries, gain_vector, factor):
    inverse = lax.rsqrt(jnp.mean(value_entries * value_entries, axis=-1, keepdims=True) + EPSILON)
    return (inverse, (value_entries * inverse * gain_vector * factor).astype(jnp.bfloat16))


def norm_grad(value_entries, inverse, gain_vector, factor, upstream):
    scaled = upstream * gain_vector * factor
    inner_mean = jnp.mean(scaled * value_entries, axis=-1, keepdims=True)
    return inverse * (scaled - value_entries * inverse * inverse * inner_mean)


def capped(query_block, key_block, query_docs, key_docs, query_pos, key_pos):
    raw_scores = jnp.einsum(
        "qhge,khe->hgqk", query_block, key_block, preferred_element_type=jnp.float32
    )
    scores = CAP_VALUE * jnp.tanh(raw_scores / CAP_VALUE)
    allowed = (query_docs[:, None] == key_docs[None, :]) & (key_pos[None, :] <= query_pos[:, None])
    return (scores, allowed)


def on_device(
    query_matrix, key_matrix, value_matrix, output_gradient, query_gain, key_gain, doc_ids
):
    query_loc, key_loc, value_loc, grad_loc = (
        lax.all_to_all(query_matrix, "head", split_axis=1, concat_axis=0, tiled=True),
        lax.all_to_all(key_matrix, "head", split_axis=1, concat_axis=0, tiled=True),
        lax.all_to_all(value_matrix, "head", split_axis=1, concat_axis=0, tiled=True),
        lax.all_to_all(output_gradient, "head", split_axis=1, concat_axis=0, tiled=True),
    )
    row_count = query_loc.shape[0]
    kv_heads = key_loc.shape[1] // HEAD_WIDTH
    group_width = query_loc.shape[1] // key_loc.shape[1]
    query_entries = query_loc.astype(jnp.float32).reshape(
        row_count, kv_heads, group_width, HEAD_WIDTH
    )
    key_entries = key_loc.astype(jnp.float32).reshape(row_count, kv_heads, HEAD_WIDTH)
    query_inv, query_norm = normalize(query_entries, query_gain, QUERY_SCALE)
    key_inv, key_norm_factor = normalize(key_entries, key_gain, 1.0)
    value_entries = value_loc.reshape(row_count, kv_heads, HEAD_WIDTH)
    gradient_rows = grad_loc.reshape(row_count, kv_heads, group_width, HEAD_WIDTH)
    ctx_place = lax.axis_index("ctx")
    row_start = ctx_place * row_count
    query_docs = lax.dynamic_slice_in_dim(doc_ids, row_start, row_count, 0)
    query_pos = row_start + jnp.arange(row_count, dtype=jnp.int32)
    first_doc = query_docs[0]
    remote = [
        passed_along((key_norm_factor, value_entries), "ctx", offset)
        for offset in range(1, REACH + 1)
    ]
    sources = [(key_norm_factor, value_entries)] + remote
    block_infos = []
    for offset in range(REACH + 1):
        owner = ctx_place - offset
        key_docs = lax.dynamic_slice_in_dim(
            doc_ids, jnp.maximum(owner, 0) * row_count, row_count, 0
        )
        key_pos = owner * row_count + jnp.arange(row_count, dtype=jnp.int32)
        needed = (owner >= 0) & ((key_docs[row_count - 1] == first_doc) | (offset == 0))
        block_infos.append((key_docs, key_pos, needed))
    mixed_sum = jnp.zeros((row_count, kv_heads, group_width, HEAD_WIDTH), jnp.float32)
    weight_sum = jnp.zeros((kv_heads, group_width, row_count), jnp.float32)
    for offset in range(REACH + 1):
        key_block, value_block = sources[offset]
        key_docs, key_pos, needed = block_infos[offset]

        def attend(running):
            scores, allowed = capped(
                query_norm, key_block, query_docs, key_docs, query_pos, key_pos
            )
            weights = jnp.where(allowed, jnp.exp(scores), 0.0)
            mixed_part = jnp.einsum(
                "hgqk,khe->qhge",
                weights.astype(jnp.bfloat16),
                value_block,
                preferred_element_type=jnp.float32,
            )
            return (running[0] + mixed_part, running[1] + jnp.sum(weights, axis=-1))

        mixed_sum, weight_sum = lax.cond(
            needed, attend, lambda running: running, (mixed_sum, weight_sum)
        )
    attended = (mixed_sum / jnp.transpose(weight_sum, (2, 0, 1))[..., None]).astype(jnp.bfloat16)
    log_total = jnp.log(weight_sum)
    row_inner = jnp.transpose(
        jnp.sum(gradient_rows.astype(jnp.float32) * attended.astype(jnp.float32), axis=-1),
        (1, 2, 0),
    )
    query_total_sum = jnp.zeros((row_count, kv_heads, group_width, HEAD_WIDTH), jnp.float32)
    partials = []
    for offset in range(REACH + 1):
        key_block, value_block = sources[offset]
        key_docs, key_pos, needed = block_infos[offset]

        def differentiate():
            scores, allowed = capped(
                query_norm, key_block, query_docs, key_docs, query_pos, key_pos
            )
            prob_block = jnp.where(allowed, jnp.exp(scores - log_total[..., None]), 0.0)
            dprob = jnp.einsum(
                "qhge,khe->hgqk", gradient_rows, value_block, preferred_element_type=jnp.float32
            )
            dscore = (
                prob_block * (dprob - row_inner[..., None]) * (1.0 - (scores / CAP_VALUE) ** 2)
            ).astype(jnp.bfloat16)
            prob_low = prob_block.astype(jnp.bfloat16)
            query_part = jnp.einsum(
                "hgqk,khe->qhge", dscore, key_block, preferred_element_type=jnp.float32
            )
            key_part = jnp.einsum(
                "hgqk,qhge->khe", dscore, query_norm, preferred_element_type=jnp.float32
            )
            value_part = jnp.einsum(
                "hgqk,qhge->khe", prob_low, gradient_rows, preferred_element_type=jnp.float32
            )
            return (query_part, key_part, value_part)

        def nothing():
            return (
                jnp.zeros((row_count, kv_heads, group_width, HEAD_WIDTH), jnp.float32),
                jnp.zeros((row_count, kv_heads, HEAD_WIDTH), jnp.float32),
                jnp.zeros((row_count, kv_heads, HEAD_WIDTH), jnp.float32),
            )

        query_part, key_part, value_part = lax.cond(needed, differentiate, nothing)
        query_total_sum = query_total_sum + query_part
        partials.append((key_part, value_part))
    key_total, value_total = partials[0]
    for offset in range(1, REACH + 1):
        arrived = passed_along(for_sending(partials[offset]), "ctx", -offset)
        key_total = key_total + arrived[0]
        value_total = value_total + arrived[1]
    query_gradient = norm_grad(
        query_entries, query_inv, query_gain, QUERY_SCALE, query_total_sum
    ).astype(jnp.bfloat16)
    key_gradient = norm_grad(key_entries, key_inv, key_gain, 1.0, key_total).astype(jnp.bfloat16)
    value_gradient = value_total.astype(jnp.bfloat16)
    return (
        lax.all_to_all(
            attended.reshape(row_count, -1), "head", split_axis=0, concat_axis=1, tiled=True
        ),
        lax.all_to_all(
            query_gradient.reshape(row_count, -1), "head", split_axis=0, concat_axis=1, tiled=True
        ),
        lax.all_to_all(
            key_gradient.reshape(row_count, -1), "head", split_axis=0, concat_axis=1, tiled=True
        ),
        lax.all_to_all(
            value_gradient.reshape(row_count, -1), "head", split_axis=0, concat_axis=1, tiled=True
        ),
    )


def solution(mesh):
    placed = (
        P(("ctx", "head"), None),
        P(("ctx", "head"), None),
        P(("ctx", "head"), None),
        P(("ctx", "head"), None),
        P(),
        P(),
        P(),
    )
    return jax.shard_map(
        on_device,
        mesh=mesh,
        in_specs=placed,
        out_specs=(
            P(("ctx", "head"), None),
            P(("ctx", "head"), None),
            P(("ctx", "head"), None),
            P(("ctx", "head"), None),
        ),
        check_vma=False,
    )
```

profile of v0, /device:TPU:33, one launch (start us, length us, event | category | flops | bytes accessed | tf_op | source)
XLA Modules:
  0.0 384.9 jit_solution(2424762256180016709)
XLA Ops:
  2.2 29.7 %all-to-all-start = ((bf16[32,16,128]{2,0,1:T(8,128)(2,1)}), bf16[32,16,128]{2,0,1:T(8,128)(2,1)S(1)}, u32[]{:S(2)}, u32[]{:S(2)}) async-start(bf16[32,16,128]{2,0,1:T(8,128)(2,1)} %copy_bitcast_fusion.5), calls=%async_computation | async-start | bytes 262144 | tf_op jit(solution)/shard_map/all_to_all | solution.py:54
  32.0 1.6 copy_bitcast_fusion.4
  33.5 31.1 %all-to-all-done = bf16[32,16,128]{2,0,1:T(8,128)(2,1)S(1)} async-done(((bf16[32,16,128]{2,0,1:T(8,128)(2,1)}), bf16[32,16,128]{2,0,1:T(8,128)(2,1)S(1)}, u32[]{:S(2)}, u32[]{:S(2)}) %all-to-all-start) | async-done | bytes 131104 | tf_op jit(solution)/shard_map/all_to_all | solution.py:54
  64.6 4.2 %all-to-all-start.2 = ((bf16[32,16,128]{2,0,1:T(8,128)(2,1)}), bf16[32,16,128]{2,0,1:T(8,128)(2,1)}, u32[]{:S(2)}, u32[]{:S(2)}) async-start(bf16[32,16,128]{2,0,1:T(8,128)(2,1)} %copy_bitcast_fusion.4), calls=%async_computation.2 | async-start | bytes 262144 | tf_op jit(solution)/shard_map/all_to_all | solution.py:55
  68.8 1.7 copy.232
  70.5 30.3 %all-to-all-done.2 = bf16[32,16,128]{2,0,1:T(8,128)(2,1)} async-done(((bf16[32,16,128]{2,0,1:T(8,128)(2,1)}), bf16[32,16,128]{2,0,1:T(8,128)(2,1)}, u32[]{:S(2)}, u32[]{:S(2)}) %all-to-all-start.2) | async-done | bytes 131104 | tf_op jit(solution)/shard_map/all_to_all | solution.py:55
  100.8 3.5 all-to-all-start.1
  105.1 39.6 %all-to-all-done.1 = bf16[32,16,256]{2,0,1:T(8,128)(2,1)S(1)} async-done(((bf16[32,16,256]{2,0,1:T(8,128)(2,1)}), bf16[32,16,256]{2,0,1:T(8,128)(2,1)S(1)}, u32[]{:S(2)}, u32[]{:S(2)}) %all-to-all-start.1) | async-done | bytes 262176 | tf_op jit(solution)/shard_map/all_to_all | solution.py:53
  144.7 3.5 all-to-all-start.4
  153.5 3.2 collective-permute-start.3
  156.7 3.9 %collective-permute-start.1 = (bf16[512,1,128]{2,0,1:T(8,128)(2,1)}, bf16[512,1,128]{2,0,1:T(8,128)(2,1)S(1)}, u32[]{:S(2)}, u32[]{:S(2)}) collective-permute-start(bf16[512,1,128]{2,0,1:T(8,128)(2,1)} %bitcast.124), channel_id=1, source_target_pairs={{0,16},{16,32},{32,48},{48,64},{64,80},{80,96},{96,112},{112,128},... | collective-permute-start | bytes 393224 | tf_op jit(solution)/shard_map/ppermute | solution.py:18
  161.0 2.9 collective-permute-start.2
  164.0 2.2 collective-permute-start
  167.2 17.7 %all-to-all-done.4 = bf16[32,16,256]{2,0,1:T(8,128)(2,1)S(1)} async-done(((bf16[32,16,256]{2,0,1:T(8,128)(2,1)}), bf16[32,16,256]{2,0,1:T(8,128)(2,1)S(1)}, u32[]{:S(2)}, u32[]{:S(2)}) %all-to-all-start.4) | async-done | bytes 262176 | tf_op jit(solution)/shard_map/all_to_all | solution.py:56
  185.6 2.5 conditional.6
  186.8 1.4 convolution_bitcast_fusion
  188.2 1.7 conditional.7
  190.0 3.5 conditional.8
  190.3 1.8 fusion.109
  192.1 1.4 fusion.13
  194.3 3.5 multiply_reduce_fusion.1
  197.8 5.4 %conditional.10 = (bf16[512,1,128]{2,0,1:T(8,128)(2,1)S(1)}, bf16[512,1,128]{2,0,1:T(8,128)(2,1)S(1)}, f32[512,1,2,128]{3,2,0,1:T(2,128)S(1)}) conditional(s32[]{:T(128)} %convert_element_type.171, () %tuple.68, (s32[512]{0:T(512)S(1)}, s32[512]{0:T(512)S(1)}, s32[512]{0:T(512)S(1)}, s32[512]{0:T(512)S(1)}, bf16[512,1,128]{2,0,1:T(8,128)(2,1)S(1)}, ...), branch_computations={%region_14.15_spmd, %region_15.16_spmd} | conditional | flops 679739392 | bytes 13529112 | solution.py:152
  198.6 1.4 convolution_bitcast_fusion.7
  200.0 1.8 fusion.53
  203.2 1.9 collective-permute-start.4
  205.2 9.5 %conditional.11 = (bf16[512,1,128]{2,0,1:T(8,128)(2,1)}, bf16[512,1,128]{2,0,1:T(8,128)(2,1)}, f32[512,1,2,128]{3,2,0,1:T(2,128)S(1)}) conditional(s32[]{:T(128)} %convert_element_type.170, () %tuple.70, (s32[512]{0:T(512)S(1)}, s32[512]{0:T(512)}, s32[512]{0:T(512)}, s32[512]{0:T(512)S(1)}, bf16[512,1,128]{2,0,1:T(8,128)(2,1)}, ...), branch_computations={%region_16.17_spmd, %region_17.18_spmd} | conditional | flops 679739392 | bytes 13529112 | solution.py:152
  207.6 2.1 convolution_bitcast_fusion.10
  209.7 2.1 fusion.81
  212.8 1.4 convolution_bitcast_fusion.9
  214.6 1.9 collective-permute-start.5
  216.6 7.1 %conditional.9 = (f32[512,1,128]{2,0,1:T(8,128)S(1)}, f32[512,1,128]{2,0,1:T(8,128)S(1)}, f32[512,1,2,128]{3,2,0,1:T(2,128)}) conditional(s32[]{:T(128)} %convert_element_type.172, () %tuple.66, (s32[512]{0:T(512)S(1)}, s32[512]{0:T(512)S(1)}, s32[512]{0:T(512)S(1)}, bf16[512,1,128]{2,0,1:T(8,128)(2,1)S(1)}, ...), branch_computations={%region_12.13_spmd, %region_13.14_spmd} | conditional | flops 679739392 | bytes 13805620 | solution.py:152
  218.0 1.4 convolution_bitcast_fusion.4
  219.4 2.1 fusion.25
  224.8 1.8 multiply_convert_fusion.2
  226.6 8.6 %all-to-all-start.6 = ((bf16[16,32,128]{2,1,0:T(8,128)(2,1)}), bf16[16,32,128]{2,1,0:T(8,128)(2,1)S(1)}, u32[]{:S(2)}, u32[]{:S(2)}) async-start(bf16[16,32,128]{2,1,0:T(8,128)(2,1)} %bitcast.135), calls=%async_computation.6 | async-start | bytes 262144 | tf_op jit(solution)/shard_map/all_to_all | solution.py:172
  235.2 1.9 collective-permute-start.6
  237.1 1.9 collective-permute-start.7
  239.0 2.7 collective-permute-done.6
  241.7 2.9 collective-permute-done.7
  245.3 14.9 %all-to-all-done.6 = bf16[16,32,128]{2,1,0:T(8,128)(2,1)S(1)} async-done(((bf16[16,32,128]{2,1,0:T(8,128)(2,1)}), bf16[16,32,128]{2,1,0:T(8,128)(2,1)S(1)}, u32[]{:S(2)}, u32[]{:S(2)}) %all-to-all-start.6) | async-done | bytes 131104 | tf_op jit(solution)/shard_map/all_to_all | solution.py:172
  260.2 7.8 %all-to-all-start.7 = ((bf16[16,32,128]{2,1,0:T(8,128)(2,1)}), bf16[16,32,128]{2,1,0:T(8,128)(2,1)S(1)}, u32[]{:S(2)}, u32[]{:S(2)}) async-start(bf16[16,32,128]{2,1,0:T(8,128)(2,1)} %bitcast.137), calls=%async_computation.7 | async-start | bytes 262144 | tf_op jit(solution)/shard_map/all_to_all | solution.py:175
  268.9 31.5 %all-to-all-done.7 = bf16[16,32,128]{2,1,0:T(8,128)(2,1)S(1)} async-done(((bf16[16,32,128]{2,1,0:T(8,128)(2,1)}), bf16[16,32,128]{2,1,0:T(8,128)(2,1)S(1)}, u32[]{:S(2)}, u32[]{:S(2)}) %all-to-all-start.7) | async-done | bytes 131104 | tf_op jit(solution)/shard_map/all_to_all | solution.py:175
  300.5 3.5 all-to-all-start.3
  304.0 1.8 multiply_reduce_fusion
  305.9 1.8 multiply_convert_fusion
  308.6 36.7 %all-to-all-done.3 = bf16[16,32,256]{2,1,0:T(8,128)(2,1)S(1)} async-done(((bf16[16,32,256]{2,1,0:T(8,128)(2,1)}), bf16[16,32,256]{2,1,0:T(8,128)(2,1)S(1)}, u32[]{:S(2)}, u32[]{:S(2)}) %all-to-all-start.3) | async-done | bytes 262176 | tf_op jit(solution)/shard_map/all_to_all | solution.py:166
  345.2 3.5 all-to-all-start.5
  350.8 33.4 %all-to-all-done.5 = bf16[16,32,256]{2,1,0:T(8,128)(2,1)S(1)} async-done(((bf16[16,32,256]{2,1,0:T(8,128)(2,1)}), bf16[16,32,256]{2,1,0:T(8,128)(2,1)S(1)}, u32[]{:S(2)}, u32[]{:S(2)}) %all-to-all-start.5) | async-done | bytes 262176 | tf_op jit(solution)/shard_map/all_to_all | solution.py:169
  (79 shorter events, 26.9 us)
Async XLA Ops:
  0.6 0.9 copy-start
  0.6 103.7 %copy-start.2 = (bf16[32,4096]{1,0:T(8,128)(2,1)S(1)}, bf16[32,4096]{1,0:T(8,128)(2,1)}, u32[]{:S(2)}) copy-start(bf16[32,4096]{1,0:T(8,128)(2,1)} %param.22) | copy-start | bytes 786436
  0.7 160.2 %copy-start.5 = (f32[128]{0:T(128)S(1)}, f32[128]{0:T(128)}, u32[]{:S(2)}) copy-start(f32[128]{0:T(128)} %param.24) | copy-start | bytes 1540
  2.2 62.4 %all-to-all-start = ((bf16[32,16,128]{2,0,1:T(8,128)(2,1)}), bf16[32,16,128]{2,0,1:T(8,128)(2,1)S(1)}, u32[]{:S(2)}, u32[]{:S(2)}) async-start(bf16[32,16,128]{2,0,1:T(8,128)(2,1)} %copy_bitcast_fusion.5), calls=%async_computation | async-start | bytes 262144 | tf_op jit(solution)/shard_map/all_to_all | solution.py:54
  64.6 36.2 %all-to-all-start.2 = ((bf16[32,16,128]{2,0,1:T(8,128)(2,1)}), bf16[32,16,128]{2,0,1:T(8,128)(2,1)}, u32[]{:S(2)}, u32[]{:S(2)}) async-start(bf16[32,16,128]{2,0,1:T(8,128)(2,1)} %copy_bitcast_fusion.4), calls=%async_computation.2 | async-start | bytes 262144 | tf_op jit(solution)/shard_map/all_to_all | solution.py:55
  100.8 43.9 %all-to-all-start.1 = ((bf16[32,16,256]{2,0,1:T(8,128)(2,1)}), bf16[32,16,256]{2,0,1:T(8,128)(2,1)S(1)}, u32[]{:S(2)}, u32[]{:S(2)}) async-start(bf16[32,16,256]{2,0,1:T(8,128)(2,1)} %bitcast.419), calls=%async_computation.1 | async-start | bytes 524288 | tf_op jit(solution)/shard_map/all_to_all | solution.py:53
  144.7 40.1 %all-to-all-start.4 = ((bf16[32,16,256]{2,0,1:T(8,128)(2,1)}), bf16[32,16,256]{2,0,1:T(8,128)(2,1)S(1)}, u32[]{:S(2)}, u32[]{:S(2)}) async-start(bf16[32,16,256]{2,0,1:T(8,128)(2,1)} %bitcast.418), calls=%async_computation.4 | async-start | bytes 524288 | tf_op jit(solution)/shard_map/all_to_all | solution.py:56
  149.1 40.8 %copy-start.3 = (s32[512]{0:T(512)}, s32[512]{0:T(512)S(1)}, u32[]{:S(2)}) copy-start(s32[512]{0:T(512)S(1)} %get-tuple-element.445) | copy-start | bytes 6148
  153.4 36.5 %copy-start.4 = (s32[512]{0:T(512)}, s32[512]{0:T(512)S(1)}, u32[]{:S(2)}) copy-start(s32[512]{0:T(512)S(1)} %iota_add_fusion) | copy-start | bytes 6148
  153.5 36.5 %collective-permute-start.3 = (bf16[512,1,128]{2,0,1:T(8,128)(2,1)}, bf16[512,1,128]{2,0,1:T(8,128)(2,1)}, u32[]{:S(2)}, u32[]{:S(2)}) collective-permute-start(bf16[512,1,128]{2,0,1:T(8,128)(2,1)} %bitcast.124), channel_id=1, source_target_pairs={{0,32},{16,48},{32,64},{48,80},{64,96},{80,112},{96,128},{112,144}... | collective-permute-start | bytes 393224 | tf_op jit(solution)/shard_map/ppermute | solution.py:18
  156.7 31.5 %collective-permute-start.1 = (bf16[512,1,128]{2,0,1:T(8,128)(2,1)}, bf16[512,1,128]{2,0,1:T(8,128)(2,1)S(1)}, u32[]{:S(2)}, u32[]{:S(2)}) collective-permute-start(bf16[512,1,128]{2,0,1:T(8,128)(2,1)} %bitcast.124), channel_id=1, source_target_pairs={{0,16},{16,32},{32,48},{48,64},{64,80},{80,96},{96,112},{112,128},... | collective-permute-start | bytes 393224 | tf_op jit(solution)/shard_map/ppermute | solution.py:18
  160.9 24.0 %copy-start.7 = (f32[128]{0:T(128)S(1)}, f32[128]{0:T(128)}, u32[]{:S(2)}) copy-start(f32[128]{0:T(128)} %param.23) | copy-start | bytes 1540
  161.0 28.9 %collective-permute-start.2 = (bf16[512,1,128]{2,0,1:T(8,128)(2,1)S(1)}, bf16[512,1,128]{2,0,1:T(8,128)(2,1)}, u32[]{:S(2)}, u32[]{:S(2)}) collective-permute-start(bf16[512,1,128]{2,0,1:T(8,128)(2,1)S(1)} %multiply_convert_fusion.3), channel_id=1, source_target_pairs={{0,32},{16,48},{32,64},{48,80},{64,96},{80,112},{96,128},{112,144}... | collective-permute-start | bytes 393224 | tf_op jit(solution)/shard_map/ppermute | solution.py:18
  164.0 24.2 %collective-permute-start = (bf16[512,1,128]{2,0,1:T(8,128)(2,1)S(1)}, bf16[512,1,128]{2,0,1:T(8,128)(2,1)S(1)}, u32[]{:S(2)}, u32[]{:S(2)}) collective-permute-start(bf16[512,1,128]{2,0,1:T(8,128)(2,1)S(1)} %multiply_convert_fusion.3), channel_id=1, source_target_pairs={{0,16},{16,32},{32,48},{48,64},{64,80},{80,96},{96,112},{112,128},... | collective-permute-start | bytes 393224 | tf_op jit(solution)/shard_map/ppermute | solution.py:18
  203.2 20.4 %collective-permute-start.4 = (bf16[512,1,128]{2,0,1:T(8,128)(2,1)S(1)}, bf16[512,1,128]{2,0,1:T(8,128)(2,1)S(1)}, u32[]{:S(2)}, u32[]{:S(2)}) collective-permute-start(bf16[512,1,128]{2,0,1:T(8,128)(2,1)S(1)} %get-tuple-element.208), channel_id=1, source_target_pairs={{16,0},{32,16},{48,32},{64,48},{80,64},{96,80},{112,96},{128,112},... | collective-permute-start | bytes 393224 | tf_op jit(solution)/shard_map/ppermute | solution.py:18
  214.6 9.0 %collective-permute-start.5 = (bf16[512,1,128]{2,0,1:T(8,128)(2,1)}, bf16[512,1,128]{2,0,1:T(8,128)(2,1)}, u32[]{:S(2)}, u32[]{:S(2)}) collective-permute-start(bf16[512,1,128]{2,0,1:T(8,128)(2,1)} %get-tuple-element.209), channel_id=1, source_target_pairs={{32,0},{48,16},{64,32},{80,48},{96,64},{112,80},{128,96},{144,112}... | collective-permute-start | bytes 393224 | tf_op jit(solution)/shard_map/ppermute | solution.py:18
  218.0 1.4 copy-start.6
  223.6 44.4 %copy-start.1 = (bf16[512,1,2,128]{3,2,0,1:T(2,128)(2,1)S(1)}, bf16[512,1,2,128]{3,2,0,1:T(2,128)(2,1)}, u32[]{:S(2)}) copy-start(bf16[512,1,2,128]{3,2,0,1:T(2,128)(2,1)} %get-tuple-element.436) | copy-start | bytes 786436
  226.6 33.7 %all-to-all-start.6 = ((bf16[16,32,128]{2,1,0:T(8,128)(2,1)}), bf16[16,32,128]{2,1,0:T(8,128)(2,1)S(1)}, u32[]{:S(2)}, u32[]{:S(2)}) async-start(bf16[16,32,128]{2,1,0:T(8,128)(2,1)} %bitcast.135), calls=%async_computation.6 | async-start | bytes 262144 | tf_op jit(solution)/shard_map/all_to_all | solution.py:172
  235.2 6.6 %collective-permute-start.6 = (bf16[512,1,128]{2,0,1:T(8,128)(2,1)S(1)}, bf16[512,1,128]{2,0,1:T(8,128)(2,1)S(1)}, u32[]{:S(2)}, u32[]{:S(2)}) collective-permute-start(bf16[512,1,128]{2,0,1:T(8,128)(2,1)S(1)} %get-tuple-element.211), channel_id=1, source_target_pairs={{16,0},{32,16},{48,32},{64,48},{80,64},{96,80},{112,96},{128,112},... | collective-permute-start | bytes 393224 | tf_op jit(solution)/shard_map/ppermute | solution.py:18
  237.1 7.5 %collective-permute-start.7 = (bf16[512,1,128]{2,0,1:T(8,128)(2,1)}, bf16[512,1,128]{2,0,1:T(8,128)(2,1)S(1)}, u32[]{:S(2)}, u32[]{:S(2)}) collective-permute-start(bf16[512,1,128]{2,0,1:T(8,128)(2,1)} %get-tuple-element.212), channel_id=1, source_target_pairs={{32,0},{48,16},{64,32},{80,48},{96,64},{112,80},{128,96},{144,112}... | collective-permute-start | bytes 393224 | tf_op jit(solution)/shard_map/ppermute | solution.py:18
  260.2 40.2 %all-to-all-start.7 = ((bf16[16,32,128]{2,1,0:T(8,128)(2,1)}), bf16[16,32,128]{2,1,0:T(8,128)(2,1)S(1)}, u32[]{:S(2)}, u32[]{:S(2)}) async-start(bf16[16,32,128]{2,1,0:T(8,128)(2,1)} %bitcast.137), calls=%async_computation.7 | async-start | bytes 262144 | tf_op jit(solution)/shard_map/all_to_all | solution.py:175
  300.5 44.7 %all-to-all-start.3 = ((bf16[16,32,256]{2,1,0:T(8,128)(2,1)}), bf16[16,32,256]{2,1,0:T(8,128)(2,1)S(1)}, u32[]{:S(2)}, u32[]{:S(2)}) async-start(bf16[16,32,256]{2,1,0:T(8,128)(2,1)} %all_to_all.107), calls=%async_computation.3 | async-start | bytes 524288 | tf_op jit(solution)/shard_map/all_to_all | solution.py:166
  345.2 38.9 %all-to-all-start.5 = ((bf16[16,32,256]{2,1,0:T(8,128)(2,1)}), bf16[16,32,256]{2,1,0:T(8,128)(2,1)S(1)}, u32[]{:S(2)}, u32[]{:S(2)}) async-start(bf16[16,32,256]{2,1,0:T(8,128)(2,1)} %all_to_all.114), calls=%async_computation.5 | async-start | bytes 524288 | tf_op jit(solution)/shard_map/all_to_all | solution.py:169
where the time goes:
time: 386 us; the launch traced here: 385 us
  waiting for transfers between devices  241 us (62%)
  starting transfers between devices  84.3 us (22%)
  matrix products  24.2 us (6%)
  local copies, waits for them, and re-layouts  16.8 us (4%)
  other arithmetic  14.9 us (4%)
    all_to_all x1, waiting for transfers between devices, on_device(): lax.all_to_all(query_matrix, 'head', split_axis=1, concat_axis=0, tiled=T...  39.6 us
    all_to_all x1, waiting for transfers between devices, on_device(): lax.all_to_all(attended.reshape(row_count, -1), 'head', split_axis=0, con...  36.7 us
    all_to_all x1, waiting for transfers between devices, on_device(): lax.all_to_all(query_gradient.reshape(row_count, -1), 'head', split_axis=...  33.4 us
    all_to_all x1, waiting for transfers between devices, on_device(): lax.all_to_all(value_gradient.reshape(row_count, -1), 'head', split_axis=...  31.5 us
    all_to_all x1, waiting for transfers between devices, on_device(): lax.all_to_all(key_matrix, 'head', split_axis=1, concat_axis=0, tiled=True)  31.1 us
    all_to_all x1, waiting for transfers between devices, on_device(): lax.all_to_all(value_matrix, 'head', split_axis=1, concat_axis=0, tiled=T...  30.3 us
    all_to_all x1, starting transfers between devices, on_device(): lax.all_to_all(key_matrix, 'head', split_axis=1, concat_axis=0, tiled=True)  29.7 us
    ppermute x8, starting transfers between devices, passed_along(): return lax.ppermute(block, axis, route)  19.9 us
  transfers between devices with their start and end apart: 16, of which 10 were waited for; matrix products, arithmetic and copies ran while one was open for 9% of the time, Pallas kernels for 0%

commit v1 on v0

--- a/solution.py
+++ b/solution.py
@@ -49,12 +49,22 @@
 def on_device(
     query_matrix, key_matrix, value_matrix, output_gradient, query_gain, key_gain, doc_ids
 ):
-    query_loc, key_loc, value_loc, grad_loc = (
-        lax.all_to_all(query_matrix, "head", split_axis=1, concat_axis=0, tiled=True),
-        lax.all_to_all(key_matrix, "head", split_axis=1, concat_axis=0, tiled=True),
-        lax.all_to_all(value_matrix, "head", split_axis=1, concat_axis=0, tiled=True),
-        lax.all_to_all(output_gradient, "head", split_axis=1, concat_axis=0, tiled=True),
-    )
+    token_rows, head_devices = query_matrix.shape[0], lax.axis_size("head")
+    packed = jnp.concatenate(
+        [
+            part.reshape(token_rows, head_devices, -1)
+            for part in (query_matrix, key_matrix, value_matrix, output_gradient)
+        ],
+        axis=-1,
+    )
+    arrived = lax.all_to_all(packed, "head", split_axis=1, concat_axis=0, tiled=True)
+    arrived = arrived.reshape(token_rows * head_devices, -1)
+    widths = [query_matrix.shape[1] // head_devices, key_matrix.shape[1] // head_devices]
+    cuts = [widths[0], widths[0] + widths[1], widths[0] + 2 * widths[1]]
+    query_loc = arrived[:, : cuts[0]]
+    key_loc = arrived[:, cuts[0] : cuts[1]]
+    value_loc = arrived[:, cuts[1] : cuts[2]]
+    grad_loc = arrived[:, cuts[2] :]
     row_count = query_loc.shape[0]
     kv_heads = key_loc.shape[1] // HEAD_WIDTH
     group_width = query_loc.shape[1] // key_loc.shape[1]
@@ -162,19 +172,21 @@
     ).astype(jnp.bfloat16)
     key_gradient = norm_grad(key_entries, key_inv, key_gain, 1.0, key_total).astype(jnp.bfloat16)
     value_gradient = value_total.astype(jnp.bfloat16)
+    leaving = jnp.concatenate(
+        [
+            part.reshape(row_count, -1)
+            for part in (attended, query_gradient, key_gradient, value_gradient)
+        ],
+        axis=-1,
+    )
+    home = lax.all_to_all(
+        leaving.reshape(row_count, 1, -1), "head", split_axis=0, concat_axis=1, tiled=True
+    )
     return (
-        lax.all_to_all(
-            attended.reshape(row_count, -1), "head", split_axis=0, concat_axis=1, tiled=True
-        ),
-        lax.all_to_all(
-            query_gradient.reshape(row_count, -1), "head", split_axis=0, concat_axis=1, tiled=True
-        ),
-        lax.all_to_all(
-            key_gradient.reshape(row_count, -1), "head", split_axis=0, concat_axis=1, tiled=True
-        ),
-        lax.all_to_all(
-            value_gradient.reshape(row_count, -1), "head", split_axis=0, concat_axis=1, tiled=True
-        ),
+        home[:, :, : cuts[0]].reshape(token_rows, -1),
+        home[:, :, cuts[0] : 2 * cuts[0]].reshape(token_rows, -1),
+        home[:, :, 2 * cuts[0] : 2 * cuts[0] + widths[1]].reshape(token_rows, -1),
+        home[:, :, 2 * cuts[0] + widths[1] :].reshape(token_rows, -1),
     )
 
 

time: 386 us -> 288 us (0.75)
  the two profiles are of different devices: /device:TPU:33 before, /device:TPU:57 now
where the time goes in v1:
time: 288 us; the launch traced here: 287 us
  blocking collectives  91.4 us (32%)
  waiting for transfers between devices  82.1 us (29%)
  starting transfers between devices  61.6 us (21%)
  local copies, waits for them, and re-layouts  19 us (7%)
  matrix products  17.6 us (6%)
  other arithmetic  10.8 us (4%)
  between operations  3.77 us (1%)
    all_to_all x1, blocking collectives, on_device(): lax.all_to_all(leaving.reshape(row_count, 1, -1), 'head', split_axis=0, c...  91.4 us
    all_to_all x1, waiting for transfers between devices, on_device(): lax.all_to_all(packed, 'head', split_axis=1, concat_axis=0, tiled=True)  82.1 us
    ppermute x8, starting transfers between devices, passed_along(): return lax.ppermute(block, axis, route)  31.9 us
    all_to_all x1, starting transfers between devices, on_device(): lax.all_to_all(packed, 'head', split_axis=1, concat_axis=0, tiled=True)  29.7 us
    unnamed x30, local copies, waits for them, and re-layouts  6 us
  transfers between devices with their start and end apart: 9, of which 1 were waited for; matrix products, arithmetic and copies ran while one was open for 11% of the time, Pallas kernels for 0%

profile of v1, /device:TPU:57, one launch (start us, length us, event | category | flops | bytes accessed | tf_op | source)
XLA Modules:
  0.0 286.6 jit_solution(12536334654834603190)
XLA Ops:
  0.6 0.9 copy.253
  1.6 0.9 copy.254
  2.5 1.0 copy.252
  3.5 1.0 copy.255
  4.6 1.1 copy.206
  5.7 29.7 %all-to-all-start = ((bf16[32,16,768]{2,0,1:T(8,128)(2,1)}), bf16[32,16,768]{2,0,1:T(8,128)(2,1)S(1)}, u32[]{:S(2)}, u32[]{:S(2)}) async-start(bf16[32,16,768]{2,0,1:T(8,128)(2,1)} %copy.206), calls=%async_computation | async-start | bytes 1572864 | tf_op jit(solution)/shard_map/all_to_all | solution.py:60
  35.5 0.9 fusion.113
  40.7 82.1 %all-to-all-done = bf16[32,16,768]{2,0,1:T(8,128)(2,1)S(1)} async-done(((bf16[32,16,768]{2,0,1:T(8,128)(2,1)}), bf16[32,16,768]{2,0,1:T(8,128)(2,1)S(1)}, u32[]{:S(2)}, u32[]{:S(2)}) %all-to-all-start) | async-done | bytes 786464 | tf_op jit(solution)/shard_map/all_to_all | solution.py:60
  123.6 1.9 collective-permute-start.3
  125.5 1.9 collective-permute-start.1
  127.6 1.9 collective-permute-start.2
  129.5 1.9 collective-permute-start
  132.7 0.9 copy.213
  133.8 2.5 conditional.6
  134.1 0.9 fusion.109
  135.0 1.4 convolution_bitcast_fusion
  136.4 3.5 %conditional.7 = ((f32[512,1,2,128]{3,0,2,1:T(8,128)S(1)}, f32[1,2,512]{2,1,0:T(2,128)S(1)})) conditional(s32[]{:T(128)} %convert_element_type.111, (f32[512,1,2,128]{3,0,2,1:T(8,128)S(1)}, f32[1,2,512]{2,1,0:T(2,128)S(1)}) %conditional.6, (s32[512]{0:T(512)S(1)}, s32[512]{0:T(512)S(1)}, s32[512]{0:T(512)S(1)}, s32[512]{0:T(512)S(1)}, ...), branch_computations={%region_5.6_spmd, %region_6.8_spmd} | conditional | flops 271974400 | bytes 4218904 | solution.py:117
  136.7 1.8 fusion.110
  138.5 1.4 fusion.5
  140.2 0.7 copy-done
  140.9 0.8 multiply_reduce_fusion.1
  141.7 0.7 conditional.11
  142.5 0.8 copy.226
  143.2 5.4 %collective-permute-start.7 = (bf16[512,1,128]{0,2,1:T(8,128)(2,1)}, bf16[512,1,128]{0,2,1:T(8,128)(2,1)}, u32[]{:S(2)}, u32[]{:S(2)}) collective-permute-start(bf16[512,1,128]{0,2,1:T(8,128)(2,1)} %copy.226), channel_id=1, source_target_pairs={{32,0},{48,16},{64,32},{80,48},{96,64},{112,80},{128,96},{144,112}... | collective-permute-start | bytes 393224 | tf_op jit(solution)/shard_map/ppermute | solution.py:18
  148.7 3.6 %collective-permute-start.5 = (bf16[512,1,128]{2,0,1:T(8,128)(2,1)}, bf16[512,1,128]{2,0,1:T(8,128)(2,1)}, u32[]{:S(2)}, u32[]{:S(2)}) collective-permute-start(bf16[512,1,128]{2,0,1:T(8,128)(2,1)} %get-tuple-element.209), channel_id=1, source_target_pairs={{32,0},{48,16},{64,32},{80,48},{96,64},{112,80},{128,96},{144,112}... | collective-permute-start | bytes 393224 | tf_op jit(solution)/shard_map/ppermute | solution.py:18
  152.4 7.9 %conditional.10 = (bf16[512,1,128]{2,0,1:T(8,128)(2,1)}, bf16[512,1,128]{2,0,1:T(8,128)(2,1)}, f32[512,1,2,128]{0,3,2,1:T(8,128)S(1)}) conditional(s32[]{:T(128)} %convert_element_type.111, () %tuple.68, (s32[512]{0:T(512)S(1)}, s32[512]{0:T(512)S(1)}, s32[512]{0:T(512)S(1)}, s32[512]{0:T(512)S(1)}, bf16[512,1,128]{2,0,1:T(8,128)(2,1)}, ...), branch_computations={%region_14.15_spmd, %region_15.16_spmd} | conditional | flops 679739392 | bytes 13520920 | solution.py:162
  152.8 1.3 fusion.57
  154.2 1.4 convolution_bitcast_fusion.7
  155.5 2.0 fusion.48
  157.6 1.1 convolution_bitcast_fusion.8
  158.7 1.4 convolution_bitcast_fusion.6
  160.3 1.7 copy.224
  161.9 8.4 %collective-permute-start.6 = (bf16[512,1,128]{0,2,1:T(8,128)(2,1)}, bf16[512,1,128]{0,2,1:T(8,128)(2,1)}, u32[]{:S(2)}, u32[]{:S(2)}) collective-permute-start(bf16[512,1,128]{0,2,1:T(8,128)(2,1)} %copy.224), channel_id=1, source_target_pairs={{16,0},{32,16},{48,32},{64,48},{80,64},{96,80},{112,96},{128,112},... | collective-permute-start | bytes 393224 | tf_op jit(solution)/shard_map/ppermute | solution.py:18
  170.3 6.7 %collective-permute-start.4 = (bf16[512,1,128]{2,0,1:T(8,128)(2,1)}, bf16[512,1,128]{2,0,1:T(8,128)(2,1)}, u32[]{:S(2)}, u32[]{:S(2)}) collective-permute-start(bf16[512,1,128]{2,0,1:T(8,128)(2,1)} %get-tuple-element.208), channel_id=1, source_target_pairs={{16,0},{32,16},{48,32},{64,48},{80,64},{96,80},{112,96},{128,112},... | collective-permute-start | bytes 393224 | tf_op jit(solution)/shard_map/ppermute | solution.py:18
  177.0 6.9 %conditional.9 = (f32[512,1,128]{2,0,1:T(8,128)S(1)}, f32[512,1,2,128]{0,3,2,1:T(8,128)}, f32[512,1,128]{0,2,1:T(8,128)}) conditional(s32[]{:T(128)} %convert_element_type.112, () %tuple.66, (s32[512]{0:T(512)S(1)}, s32[512]{0:T(512)}, s32[512]{0:T(512)S(1)}, bf16[512,1,128]{2,0,1:T(8,128)(2,1)S(1)}, bf16[512,1,2,128]{0,3,2,1:T(8,128)(2,1)S(1)}, ...), branch_computations={%region_12.13_spmd, %region_13.14_spmd} | conditional | flops 679739392 | bytes 13813840 | solution.py:162
  177.1 0.9 compare_and_fusion.3
  178.5 1.5 convolution_bitcast_fusion.4
  180.0 2.0 fusion.22
  183.0 1.0 copy.240
  184.0 1.3 multiply_reduce_fusion
  185.4 1.1 fusion.105
  186.6 1.2 fusion.107
  188.0 1.1 fusion.106
  189.7 1.2 reduce.9
  191.4 91.4 %all_to_all.33 = bf16[16,2,12288]{2,1,0:T(2,128)(2,1)S(1)} all-to-all(bf16[16,2,12288]{2,1,0:T(2,128)(2,1)S(1)} %reshape.442), channel_id=1, replica_groups=mesh['ctx'=64,'head'=16] {'head'}, dimensions={0} | all-to-all | bytes 1572864 | tf_op jit(solution)/shard_map/all_to_all | solution.py:182
  282.8 0.7 reshape.443
  283.8 0.7 copy.249
  285.8 0.7 copy.248
  (76 shorter events, 10.4 us)
Async XLA Ops:
  4.6 122.8 %copy-start.5 = (f32[128]{0:T(128)S(1)}, f32[128]{0:T(128)}, u32[]{:S(2)}) copy-start(f32[128]{0:T(128)} %param.24) | copy-start | bytes 1540
  5.7 117.0 %all-to-all-start = ((bf16[32,16,768]{2,0,1:T(8,128)(2,1)}), bf16[32,16,768]{2,0,1:T(8,128)(2,1)S(1)}, u32[]{:S(2)}, u32[]{:S(2)}) async-start(bf16[32,16,768]{2,0,1:T(8,128)(2,1)} %copy.206), calls=%async_computation | async-start | bytes 1572864 | tf_op jit(solution)/shard_map/all_to_all | solution.py:60
  36.4 97.5 %copy-start.4 = (s32[512]{0:T(512)}, s32[512]{0:T(512)S(1)}, u32[]{:S(2)}) copy-start(s32[512]{0:T(512)S(1)} %get-tuple-element.585) | copy-start | bytes 6148
  123.6 16.4 %collective-permute-start.3 = (bf16[512,1,128]{2,0,1:T(8,128)(2,1)}, bf16[512,1,128]{2,0,1:T(8,128)(2,1)}, u32[]{:S(2)}, u32[]{:S(2)}) collective-permute-start(bf16[512,1,128]{2,0,1:T(8,128)(2,1)} %slice_bitcast_fusion.4), channel_id=1, source_target_pairs={{0,32},{16,48},{32,64},{48,80},{64,96},{80,112},{96,128},{112,144}... | collective-permute-start | bytes 393224 | tf_op jit(solution)/shard_map/ppermute | solution.py:18
  125.5 10.9 %collective-permute-start.1 = (bf16[512,1,128]{2,0,1:T(8,128)(2,1)}, bf16[512,1,128]{2,0,1:T(8,128)(2,1)}, u32[]{:S(2)}, u32[]{:S(2)}) collective-permute-start(bf16[512,1,128]{2,0,1:T(8,128)(2,1)} %slice_bitcast_fusion.4), channel_id=1, source_target_pairs={{0,16},{16,32},{32,48},{48,64},{64,80},{80,96},{96,112},{112,128},... | collective-permute-start | bytes 393224 | tf_op jit(solution)/shard_map/ppermute | solution.py:18
  127.4 5.2 %copy-start.2 = (f32[512]{0:T(512)}, f32[512]{0:T(512)S(1)}, u32[]{:S(2)}) copy-start(f32[512]{0:T(512)S(1)} %add_rsqrt_fusion.1) | copy-start | bytes 6148
  127.6 12.4 %collective-permute-start.2 = (bf16[512,1,128]{2,0,1:T(8,128)(2,1)S(1)}, bf16[512,1,128]{2,0,1:T(8,128)(2,1)}, u32[]{:S(2)}, u32[]{:S(2)}) collective-permute-start(bf16[512,1,128]{2,0,1:T(8,128)(2,1)S(1)} %fusion.108), channel_id=1, source_target_pairs={{0,32},{16,48},{32,64},{48,80},{64,96},{80,112},{96,128},{112,144}... | collective-permute-start | bytes 393224 | tf_op jit(solution)/shard_map/ppermute | solution.py:18
  129.5 6.9 %collective-permute-start = (bf16[512,1,128]{2,0,1:T(8,128)(2,1)S(1)}, bf16[512,1,128]{2,0,1:T(8,128)(2,1)}, u32[]{:S(2)}, u32[]{:S(2)}) collective-permute-start(bf16[512,1,128]{2,0,1:T(8,128)(2,1)S(1)} %fusion.108), channel_id=1, source_target_pairs={{0,16},{16,32},{32,48},{48,64},{64,80},{80,96},{96,112},{112,128},... | collective-permute-start | bytes 393224 | tf_op jit(solution)/shard_map/ppermute | solution.py:18
  131.5 2.2 copy-start.11
  140.0 1.0 copy-start
  140.2 12.1 %copy-start.9 = (f32[1,2,512]{2,1,0:T(2,128)}, f32[1,2,512]{2,1,0:T(2,128)S(1)}, u32[]{:S(2)}) copy-start(f32[1,2,512]{2,1,0:T(2,128)S(1)} %log.16) | copy-start | bytes 12292
  141.7 10.6 %copy-start.7 = (f32[512,2]{0,1:T(2,128)}, f32[512,2]{0,1:T(2,128)S(1)}, u32[]{:S(2)}) copy-start(f32[512,2]{0,1:T(2,128)S(1)} %get-tuple-element.571) | copy-start | bytes 12292
  143.2 44.7 %collective-permute-start.7 = (bf16[512,1,128]{0,2,1:T(8,128)(2,1)}, bf16[512,1,128]{0,2,1:T(8,128)(2,1)}, u32[]{:S(2)}, u32[]{:S(2)}) collective-permute-start(bf16[512,1,128]{0,2,1:T(8,128)(2,1)} %copy.226), channel_id=1, source_target_pairs={{32,0},{48,16},{64,32},{80,48},{96,64},{112,80},{128,96},{144,112}... | collective-permute-start | bytes 393224 | tf_op jit(solution)/shard_map/ppermute | solution.py:18
  148.7 36.7 %collective-permute-start.5 = (bf16[512,1,128]{2,0,1:T(8,128)(2,1)}, bf16[512,1,128]{2,0,1:T(8,128)(2,1)}, u32[]{:S(2)}, u32[]{:S(2)}) collective-permute-start(bf16[512,1,128]{2,0,1:T(8,128)(2,1)} %get-tuple-element.209), channel_id=1, source_target_pairs={{32,0},{48,16},{64,32},{80,48},{96,64},{112,80},{128,96},{144,112}... | collective-permute-start | bytes 393224 | tf_op jit(solution)/shard_map/ppermute | solution.py:18
  161.9 26.0 %collective-permute-start.6 = (bf16[512,1,128]{0,2,1:T(8,128)(2,1)}, bf16[512,1,128]{0,2,1:T(8,128)(2,1)}, u32[]{:S(2)}, u32[]{:S(2)}) collective-permute-start(bf16[512,1,128]{0,2,1:T(8,128)(2,1)} %copy.224), channel_id=1, source_target_pairs={{16,0},{32,16},{48,32},{64,48},{80,64},{96,80},{112,96},{128,112},... | collective-permute-start | bytes 393224 | tf_op jit(solution)/shard_map/ppermute | solution.py:18
  170.3 15.1 %collective-permute-start.4 = (bf16[512,1,128]{2,0,1:T(8,128)(2,1)}, bf16[512,1,128]{2,0,1:T(8,128)(2,1)}, u32[]{:S(2)}, u32[]{:S(2)}) collective-permute-start(bf16[512,1,128]{2,0,1:T(8,128)(2,1)} %get-tuple-element.208), channel_id=1, source_target_pairs={{16,0},{32,16},{48,32},{64,48},{80,64},{96,80},{112,96},{128,112},... | collective-permute-start | bytes 393224 | tf_op jit(solution)/shard_map/ppermute | solution.py:18
  177.1 1.4 copy-start.10
  178.5 1.6 copy-start.8
  184.0 1.4 copy-start.6
  184.0 2.6 copy-start.3
  185.2 3.8 %copy-start.1 = (bf16[512,1,2,128]{0,3,2,1:T(8,128)(2,1)S(1)}, bf16[512,1,2,128]{0,3,2,1:T(8,128)(2,1)}, u32[]{:S(2)}) copy-start(bf16[512,1,2,128]{0,3,2,1:T(8,128)(2,1)} %get-tuple-element.572) | copy-start | bytes 786436

commit v2 on v1

--- a/solution.py
+++ b/solution.py
@@ -80,93 +80,61 @@
     row_start = ctx_place * row_count
     query_docs = lax.dynamic_slice_in_dim(doc_ids, row_start, row_count, 0)
     query_pos = row_start + jnp.arange(row_count, dtype=jnp.int32)
-    first_doc = query_docs[0]
-    remote = [
-        passed_along((key_norm_factor, value_entries), "ctx", offset)
-        for offset in range(1, REACH + 1)
+    own_pair = jnp.concatenate([key_norm_factor, value_entries], axis=-1)
+    pairs = [own_pair] + [
+        passed_along(own_pair, "ctx", offset) for offset in range(1, REACH + 1)
     ]
-    sources = [(key_norm_factor, value_entries)] + remote
-    block_infos = []
-    for offset in range(REACH + 1):
-        owner = ctx_place - offset
-        key_docs = lax.dynamic_slice_in_dim(
-            doc_ids, jnp.maximum(owner, 0) * row_count, row_count, 0
-        )
-        key_pos = owner * row_count + jnp.arange(row_count, dtype=jnp.int32)
-        needed = (owner >= 0) & ((key_docs[row_count - 1] == first_doc) | (offset == 0))
-        block_infos.append((key_docs, key_pos, needed))
-    mixed_sum = jnp.zeros((row_count, kv_heads, group_width, HEAD_WIDTH), jnp.float32)
-    weight_sum = jnp.zeros((kv_heads, group_width, row_count), jnp.float32)
-    for offset in range(REACH + 1):
-        key_block, value_block = sources[offset]
-        key_docs, key_pos, needed = block_infos[offset]
-
-        def attend(running):
-            scores, allowed = capped(
-                query_norm, key_block, query_docs, key_docs, query_pos, key_pos
-            )
-            weights = jnp.where(allowed, jnp.exp(scores), 0.0)
-            mixed_part = jnp.einsum(
-                "hgqk,khe->qhge",
-                weights.astype(jnp.bfloat16),
-                value_block,
-                preferred_element_type=jnp.float32,
-            )
-            return (running[0] + mixed_part, running[1] + jnp.sum(weights, axis=-1))
-
-        mixed_sum, weight_sum = lax.cond(
-            needed, attend, lambda running: running, (mixed_sum, weight_sum)
-        )
+    window = jnp.concatenate(pairs[::-1], axis=0)
+    key_window = window[..., :HEAD_WIDTH]
+    value_window = window[..., HEAD_WIDTH:]
+    window_rows = (REACH + 1) * row_count
+    key_pos = row_start - REACH * row_count + jnp.arange(window_rows, dtype=jnp.int32)
+    padded_docs = jnp.concatenate(
+        [jnp.full((REACH * row_count,), -1, jnp.int32), doc_ids.astype(jnp.int32)]
+    )
+    key_docs = lax.dynamic_slice_in_dim(padded_docs, row_start, window_rows, 0)
+    scores, allowed = capped(query_norm, key_window, query_docs, key_docs, query_pos, key_pos)
+    weights = jnp.where(allowed, jnp.exp(scores), 0.0)
+    weight_sum = jnp.sum(weights, axis=-1)
+    mixed_sum = jnp.einsum(
+        "hgqk,khe->qhge",
+        weights.astype(jnp.bfloat16),
+        value_window,
+        preferred_element_type=jnp.float32,
+    )
     attended = (mixed_sum / jnp.transpose(weight_sum, (2, 0, 1))[..., None]).astype(jnp.bfloat16)
     log_total = jnp.log(weight_sum)
     row_inner = jnp.transpose(
         jnp.sum(gradient_rows.astype(jnp.float32) * attended.astype(jnp.float32), axis=-1),
         (1, 2, 0),
     )
-    query_total_sum = jnp.zeros((row_count, kv_heads, group_width, HEAD_WIDTH), jnp.float32)
-    partials = []
-    for offset in range(REACH + 1):
-        key_block, value_block = sources[offset]
-        key_docs, key_pos, needed = block_infos[offset]
-
-        def differentiate():
-            scores, allowed = capped(
-                query_norm, key_block, query_docs, key_docs, query_pos, key_pos
-            )
-            prob_block = jnp.where(allowed, jnp.exp(scores - log_total[..., None]), 0.0)
-            dprob = jnp.einsum(
-                "qhge,khe->hgqk", gradient_rows, value_block, preferred_element_type=jnp.float32
-            )
-            dscore = (
-                prob_block * (dprob - row_inner[..., None]) * (1.0 - (scores / CAP_VALUE) ** 2)
-            ).astype(jnp.bfloat16)
-            prob_low = prob_block.astype(jnp.bfloat16)
-            query_part = jnp.einsum(
-                "hgqk,khe->qhge", dscore, key_block, preferred_element_type=jnp.float32
-            )
-            key_part = jnp.einsum(
-                "hgqk,qhge->khe", dscore, query_norm, preferred_element_type=jnp.float32
-            )
-            value_part = jnp.einsum(
-                "hgqk,qhge->khe", prob_low, gradient_rows, preferred_element_type=jnp.float32
-            )
-            return (query_part, key_part, value_part)
-
-        def nothing():
-            return (
-                jnp.zeros((row_count, kv_heads, group_width, HEAD_WIDTH), jnp.float32),
-                jnp.zeros((row_count, kv_heads, HEAD_WIDTH), jnp.float32),
-                jnp.zeros((row_count, kv_heads, HEAD_WIDTH), jnp.float32),
-            )
-
-        query_part, key_part, value_part = lax.cond(needed, differentiate, nothing)
-        query_total_sum = query_total_sum + query_part
-        partials.append((key_part, value_part))
-    key_total, value_total = partials[0]
+    prob_block = jnp.where(allowed, jnp.exp(scores - log_total[..., None]), 0.0)
+    dprob = jnp.einsum(
+        "qhge,khe->hgqk", gradient_rows, value_window, preferred_element_type=jnp.float32
+    )
+    dscore = (
+        prob_block * (dprob - row_inner[..., None]) * (1.0 - (scores / CAP_VALUE) ** 2)
+    ).astype(jnp.bfloat16)
+    prob_low = prob_block.astype(jnp.bfloat16)
+    query_total_sum = jnp.einsum(
+        "hgqk,khe->qhge", dscore, key_window, preferred_element_type=jnp.float32
+    )
+    key_part = jnp.einsum(
+        "hgqk,qhge->khe", dscore, query_norm, preferred_element_type=jnp.float32
+    )
+    value_part = jnp.einsum(
+        "hgqk,qhge->khe", prob_low, gradient_rows, preferred_element_type=jnp.float32
+    )
+    key_total = key_part[REACH * row_count :]
+    value_total = value_part[REACH * row_count :]
+    grad_parts = jnp.concatenate([key_part, value_part], axis=-1)
     for offset in range(1, REACH + 1):
-        arrived = passed_along(for_sending(partials[offset]), "ctx", -offset)
-        key_total = key_total + arrived[0]
-        value_total = value_total + arrived[1]
+        first = (REACH - offset) * row_count
+        arrived = passed_along(
+            for_sending(grad_parts[first : first + row_count]), "ctx", -offset
+        )
+        key_total = key_total + arrived[..., :HEAD_WIDTH]
+        value_total = value_total + arrived[..., HEAD_WIDTH:]
     query_gradient = norm_grad(
         query_entries, query_inv, query_gain, QUERY_SCALE, query_total_sum
     ).astype(jnp.bfloat16)

time: 288 us -> 267 us (0.927)
  starting transfers between devices: 61.6 us -> 40.4 us
  waiting for transfers between devices: 82.1 us -> 94.4 us
  local copies, waits for them, and re-layouts: 19 us -> 12.3 us
  matrix products: 17.6 us -> 13.5 us
    ppermute x8 -> x4, starting transfers between devices: 31.9 us -> 10.7 us  [passed_along(): return lax.ppermute(block, axis, route)]
    ppermute x8 -> x4, waiting for transfers between devices: 0.02 us -> 11.2 us  [passed_along(): return lax.ppermute(block, axis, route)]
    unnamed x30 -> x13, local copies, waits for them, and re-layouts: 6 us -> 1.17 us
    cond x9 -> x0, local copies, waits for them, and re-layouts: 3.84 us -> none  [the longest x4 3.64 us: on_device(): query_part, key_part, value_part = lax.cond(needed, differentiate, nothing)]
    dot_general x10 -> x5, matrix products: 13.2 us -> 9.85 us  [the longest x1 3.47 us: on_device(): jnp.einsum('qhge,khe->hgqk', gradient_rows, value_window, preferred_eleme...]
  transfers between devices with their start and end apart: 9 -> 5, of which waited for: 1 -> 4; matrix products, arithmetic and copies ran while one was open for 11% -> 4% of each run, Pallas kernels for 0% -> 0%
where the time goes in v2:
time: 267 us
  waiting for transfers between devices  94.4 us (35%)
  blocking collectives  92.9 us (35%)
  starting transfers between devices  40.4 us (15%)
  matrix products  13.5 us (5%)
  other arithmetic  12.4 us (5%)
  local copies, waits for them, and re-layouts  12.3 us (5%)
    all_to_all x1, blocking collectives, on_device(): lax.all_to_all(leaving.reshape(row_count, 1, -1), 'head', split_axis=0, c...  92.9 us
    all_to_all x1, waiting for transfers between devices, on_device(): lax.all_to_all(packed, 'head', split_axis=1, concat_axis=0, tiled=True)  83.2 us
    all_to_all x1, starting transfers between devices, on_device(): lax.all_to_all(packed, 'head', split_axis=1, concat_axis=0, tiled=True)  29.7 us
    ppermute x4, waiting for transfers between devices, passed_along(): return lax.ppermute(block, axis, route)  11.2 us
    ppermute x4, starting transfers between devices, passed_along(): return lax.ppermute(block, axis, route)  10.7 us
  transfers between devices with their start and end apart: 5, of which 4 were waited for; matrix products, arithmetic and copies ran while one was open for 4% of the time, Pallas kernels for 0%

profile of v2, /device:TPU:57, one launch (start us, length us, event | category | flops | bytes accessed | tf_op | source)
XLA Modules:
  0.0 266.8 jit_solution(16287389016524596563)
XLA Ops:
  0.6 1.1 copy_bitcast_fusion
  1.8 1.0 copy_bitcast_fusion.4
  2.7 1.0 pad_maximum_fusion
  3.7 29.7 %all-to-all-start = ((bf16[32,16,768]{2,0,1:T(8,128)(2,1)}), bf16[32,16,768]{2,0,1:T(8,128)(2,1)S(1)}, u32[]{:S(2)}, u32[]{:S(2)}) async-start(bf16[32,16,768]{2,0,1:T(8,128)(2,1)} %pad_maximum_fusion), calls=%async_computation | async-start | bytes 1572864 | tf_op jit(solution)/shard_map/all_to_all | solution.py:60
  33.5 0.8 dynamic_slice.6
  34.2 0.8 pad_dynamic-slice_fusion
  35.0 0.7 broadcast_bitcast_fusion
  35.7 1.9 compare_and_fusion
  37.5 83.2 %all-to-all-done = bf16[32,16,768]{2,0,1:T(8,128)(2,1)S(1)} async-done(((bf16[32,16,768]{2,0,1:T(8,128)(2,1)}), bf16[32,16,768]{2,0,1:T(8,128)(2,1)S(1)}, u32[]{:S(2)}, u32[]{:S(2)}) %all-to-all-start) | async-done | bytes 786464 | tf_op jit(solution)/shard_map/all_to_all | solution.py:60
  120.7 0.1 fusion.42
  120.9 0.8 fusion.57
  121.7 0.7 pad_maximum_fusion.2
  122.4 1.9 collective-permute-start
  124.4 1.9 collective-permute-start.1
  126.4 0.3 reshape.246
  126.7 1.3 multiply_reduce_fusion.2
  128.0 0.2 copy.184
  128.2 0.2 copy.211
  128.4 1.1 copy.175
  129.6 1.0 copy.208
  130.6 0.2 copy.210
  130.8 0.1 copy.215
  130.9 2.7 collective-permute-done.1
  133.6 1.1 maximum_maximum_fusion
  134.7 3.6 %fusion.6 = (f32[2,512]{1,0:T(2,128)S(1)}, f32[1536,512,2]{1,0,2:T(8,128)S(1)}) fusion(pred[512,1536]{0,1:T(8,128)(4,1)} %compare_and_fusion, bf16[1536,1,256]{2,0,1:T(8,128)(2,1)S(1)} %maximum_maximum_fusion, f32[512,256]{1,0:T(8,128)} %copy.208, f32[256]{0:T(256)S(1)} %broadcast_bitcast_fusion, bf16[512,768]{1,0:T(8,128)(2,1)S(1)} %bitcast.224), kind=kOutput, calls=%fused_computation.11 | convolution fusion | flops 409598976 | bytes 8262656 | tf_op jit(solution)/shard_map/qhge,khe->hgqk/dot_general | solution.py:41
  138.4 2.9 %multiply_reduce_fusion.1 = (f32[512,2]{0,1:T(2,128)S(1)}, bf16[512,1,2,128]{0,3,2,1:T(8,128)(2,1)}) fusion(f32[512,1,2,128]{0,3,2,1:T(8,128)S(1)} %bitcast.232, f32[512,2]{0,1:T(2,128)S(1)} %bitcast.242, f32[1536,512,2]{1,0,2:T(8,128)S(1)} %get-tuple-element.16, pred[512,1536]{0,1:T(8,128)(4,1)S(1)} %copy-done.1, ...), kind=kOutput, calls=%fused_computation.39 | convolution fusion | flops 409598976 | bytes 8265728 | tf_op jit(solution)/shard_map/hgqk,khe->qhge/dot_general | solution.py:99
  141.2 1.8 fusion.17
  143.1 3.5 %fusion.8 = bf16[2,512,1536]{1,2,0:T(8,128)(2,1)S(1)} fusion(bf16[512,2,128]{0,2,1:T(8,128)(2,1)S(1)} %bitcast.235, f32[1536,512,2]{1,0,2:T(8,128)S(1)} %get-tuple-element.16, f32[2,512]{1,0:T(2,128)S(1)} %bitcast.243, f32[2,512]{1,0:T(2,128)S(1)} %log.9, pred[512,1536]{0,1:T(8,128)(4,1)S(1)} %copy-done.1, bf16[1536,1,256]{2,0,1:T(8,128)(2,1)S(1)} %maximum_maximum_fusion), kind=kOutput, calls=%fused_computation.13 | convolution fusion | flops 418381824 | bytes 10887168 | tf_op jit(solution)/shard_map/qhge,khe->hgqk/dot_general | solution.py:112
  146.6 0.6 multiply_reduce_fusion
  147.2 1.1 convolution_bitcast_fusion
  148.3 0.8 maximum_convert_fusion
  149.1 4.5 %collective-permute-start.2 = (bf16[512,1,256]{2,0,1:T(8,128)(2,1)}, bf16[512,1,256]{2,0,1:T(8,128)(2,1)S(1)}, u32[]{:S(2)}, u32[]{:S(2)}) collective-permute-start(bf16[512,1,256]{2,0,1:T(8,128)(2,1)} %get-tuple-element.4), channel_id=1, source_target_pairs={{16,0},{32,16},{48,32},{64,48},{80,64},{96,80},{112,96},{128,112},... | collective-permute-start | bytes 786440 | tf_op jit(solution)/shard_map/ppermute | solution.py:18
  153.6 2.4 collective-permute-start.3
  156.1 0.1 copy.193
  156.3 1.1 copy.192
  157.4 2.5 collective-permute-done.2
  159.9 6.0 %collective-permute-done.3 = bf16[512,1,256]{2,0,1:T(8,128)(2,1)} collective-permute-done((bf16[512,1,256]{2,0,1:T(8,128)(2,1)}, bf16[512,1,256]{2,0,1:T(8,128)(2,1)}, u32[]{:S(2)}, u32[]{:S(2)}) %collective-permute-start.3) | collective-permute-done | bytes 262176 | tf_op jit(solution)/shard_map/ppermute | solution.py:18
  165.9 1.1 fusion.44
  166.9 1.2 fusion.56
  168.3 0.5 broadcast.189
  168.8 1.2 reduce.7
  170.0 0.2 reshape.271
  170.2 92.9 %all_to_all.33 = bf16[16,2,12288]{2,1,0:T(2,128)(2,1)S(1)} all-to-all(bf16[16,2,12288]{2,1,0:T(2,128)(2,1)S(1)} %reshape.271), channel_id=1, replica_groups=mesh['ctx'=64,'head'=16] {'head'}, dimensions={0} | all-to-all | bytes 1572864 | tf_op jit(solution)/shard_map/all_to_all | solution.py:150
  263.1 0.7 reshape.272
  264.1 0.7 copy.221
  264.8 0.7 copy.222
  265.5 0.7 copy.237
  266.2 0.7 copy.238
  (23 shorter events, 0.6 us)
Async XLA Ops:
  0.6 1.1 copy-start
  3.7 117.0 %all-to-all-start = ((bf16[32,16,768]{2,0,1:T(8,128)(2,1)}), bf16[32,16,768]{2,0,1:T(8,128)(2,1)S(1)}, u32[]{:S(2)}, u32[]{:S(2)}) async-start(bf16[32,16,768]{2,0,1:T(8,128)(2,1)} %pad_maximum_fusion), calls=%async_computation | async-start | bytes 1572864 | tf_op jit(solution)/shard_map/all_to_all | solution.py:60
  122.4 8.5 %collective-permute-start = (bf16[512,1,256]{2,0,1:T(8,128)(2,1)}, bf16[512,1,256]{2,0,1:T(8,128)(2,1)}, u32[]{:S(2)}, u32[]{:S(2)}) collective-permute-start(bf16[512,1,256]{2,0,1:T(8,128)(2,1)} %pad_maximum_fusion.2), channel_id=1, source_target_pairs={{0,32},{16,48},{32,64},{48,80},{64,96},{80,112},{96,128},{112,144}... | collective-permute-start | bytes 786440 | tf_op jit(solution)/shard_map/ppermute | solution.py:18
  124.4 9.2 %collective-permute-start.1 = (bf16[512,1,256]{2,0,1:T(8,128)(2,1)}, bf16[512,1,256]{2,0,1:T(8,128)(2,1)}, u32[]{:S(2)}, u32[]{:S(2)}) collective-permute-start(bf16[512,1,256]{2,0,1:T(8,128)(2,1)} %pad_maximum_fusion.2), channel_id=1, source_target_pairs={{0,16},{16,32},{32,48},{48,64},{64,80},{80,96},{96,112},{112,128},... | collective-permute-start | bytes 786440 | tf_op jit(solution)/shard_map/ppermute | solution.py:18
  134.7 3.7 %copy-start.1 = (pred[512,1536]{0,1:T(8,128)(4,1)S(1)}, pred[512,1536]{0,1:T(8,128)(4,1)}, u32[]{:S(2)}) copy-start(pred[512,1536]{0,1:T(8,128)(4,1)} %compare_and_fusion) | copy-start | bytes 2359300
  143.1 3.5 %copy-start.2 = (f32[128]{0:T(128)S(1)}, f32[128]{0:T(128)}, u32[]{:S(2)}) copy-start(f32[128]{0:T(128)} %param.11) | copy-start | bytes 1540
  146.6 19.3 %copy-start.3 = (f32[128]{0:T(128)S(1)}, f32[128]{0:T(128)}, u32[]{:S(2)}) copy-start(f32[128]{0:T(128)} %param.12) | copy-start | bytes 1540
  149.1 10.8 %collective-permute-start.2 = (bf16[512,1,256]{2,0,1:T(8,128)(2,1)}, bf16[512,1,256]{2,0,1:T(8,128)(2,1)S(1)}, u32[]{:S(2)}, u32[]{:S(2)}) collective-permute-start(bf16[512,1,256]{2,0,1:T(8,128)(2,1)} %get-tuple-element.4), channel_id=1, source_target_pairs={{16,0},{32,16},{48,32},{64,48},{80,64},{96,80},{112,96},{128,112},... | collective-permute-start | bytes 786440 | tf_op jit(solution)/shard_map/ppermute | solution.py:18
  153.6 12.2 %collective-permute-start.3 = (bf16[512,1,256]{2,0,1:T(8,128)(2,1)}, bf16[512,1,256]{2,0,1:T(8,128)(2,1)}, u32[]{:S(2)}, u32[]{:S(2)}) collective-permute-start(bf16[512,1,256]{2,0,1:T(8,128)(2,1)} %get-tuple-element.5), channel_id=1, source_target_pairs={{32,0},{48,16},{64,32},{80,48},{96,64},{112,80},{128,96},{144,112}... | collective-permute-start | bytes 786440 | tf_op jit(solution)/shard_map/ppermute | solution.py:18

commit v3 on v2

v3 whole, which is shorter than its diff:
```python
import jax
import jax.numpy as jnp
from jax import lax
from jax.sharding import PartitionSpec as P

HEAD_WIDTH = 128
REACH = 2
Z_PARTS = 4


CAP_VALUE = 50.0
QUERY_SCALE = 144.0 ** (-0.5)
EPSILON = 1e-06


def passed_along(block, axis, distance):
    devices = range(lax.axis_size(axis))
    route = [(i - distance, i) for i in devices if i - distance in devices]
    return lax.ppermute(block, axis, route)


def for_sending(value):

    def short(part):
        return part.astype(jnp.bfloat16) if part.dtype == jnp.float32 else part

    return jax.tree.map(short, value)


def head_place():
    me = lax.axis_index("head")
    return me // Z_PARTS, me % Z_PARTS


def shifted(block, step, along):
    size = lax.axis_size("head")
    x_parts = size // Z_PARTS

    def target(i):
        hx, hz = divmod(i, Z_PARTS)
        if along == "z":
            return hx * Z_PARTS + (hz + step) % Z_PARTS
        return ((hx + step) % x_parts) * Z_PARTS + hz

    return lax.ppermute(block, "head", [(i, target(i)) for i in range(size)])


def mirrored(block, hx, hz):
    block = jnp.roll(jnp.flip(block, 0), hx + 1, 0)
    return jnp.roll(jnp.flip(block, 1), hz + 1, 1)


def to_heads(block):
    x_parts, z_parts = block.shape[1], block.shape[2]
    hx, hz = head_place()
    got = []
    for k in range(z_parts):
        piece = lax.dynamic_index_in_dim(block, (hz + k) % z_parts, 2, keepdims=False)
        got.append(piece if k == 0 else shifted(piece, k, "z"))
    stage = jnp.stack(got, 0)
    got = []
    for k in range(x_parts):
        piece = lax.dynamic_index_in_dim(stage, (hx + k) % x_parts, 2, keepdims=False)
        got.append(piece if k == 0 else shifted(piece, k, "x"))
    ordered = mirrored(jnp.stack(got, 0), hx, hz)
    return ordered.reshape(x_parts * z_parts * block.shape[0], block.shape[-1])


def from_heads(rows, token_rows):
    x_parts = lax.axis_size("head") // Z_PARTS
    hx, hz = head_place()
    block = mirrored(rows.reshape(x_parts, Z_PARTS, token_rows, -1), hx, hz)
    back = jnp.stack(
        [block[0]] + [shifted(block[k], x_parts - k, "x") for k in range(1, x_parts)], 0
    )
    home = jnp.stack(
        [back[:, 0]]
        + [shifted(back[:, k], Z_PARTS - k, "z") for k in range(1, Z_PARTS)],
        1,
    )
    home = jnp.roll(jnp.roll(home, hx, 0), hz, 1)
    return jnp.transpose(home, (2, 0, 1, 3)).reshape(token_rows, x_parts * Z_PARTS, -1)


def normalize(value_entries, gain_vector, factor):
    inverse = lax.rsqrt(jnp.mean(value_entries * value_entries, axis=-1, keepdims=True) + EPSILON)
    return (inverse, (value_entries * inverse * gain_vector * factor).astype(jnp.bfloat16))


def norm_grad(value_entries, inverse, gain_vector, factor, upstream):
    scaled = upstream * gain_vector * factor
    inner_mean = jnp.mean(scaled * value_entries, axis=-1, keepdims=True)
    return inverse * (scaled - value_entries * inverse * inverse * inner_mean)


def one_head(query_loc, grad_loc, query_gain, key_window, value_window, allowed):
    query_entries = query_loc.astype(jnp.float32)
    query_inv, query_norm = normalize(query_entries, query_gain, QUERY_SCALE)
    raw_scores = jnp.einsum(
        "qe,ke->qk", query_norm, key_window, preferred_element_type=jnp.float32
    )
    scores = CAP_VALUE * jnp.tanh(raw_scores / CAP_VALUE)
    weights = jnp.where(allowed, jnp.exp(scores), 0.0)
    weight_sum = jnp.sum(weights, axis=-1, keepdims=True)
    mixed_sum = jnp.einsum(
        "qk,ke->qe", weights.astype(jnp.bfloat16), value_window, preferred_element_type=jnp.float32
    )
    attended = (mixed_sum / weight_sum).astype(jnp.bfloat16)
    log_total = jnp.log(weight_sum)
    row_inner = jnp.sum(
        grad_loc.astype(jnp.float32) * attended.astype(jnp.float32), axis=-1, keepdims=True
    )
    prob_block = jnp.where(allowed, jnp.exp(scores - log_total), 0.0)
    dprob = jnp.einsum("qe,ke->qk", grad_loc, value_window, preferred_element_type=jnp.float32)
    dscore = (prob_block * (dprob - row_inner) * (1.0 - (scores / CAP_VALUE) ** 2)).astype(
        jnp.bfloat16
    )
    prob_low = prob_block.astype(jnp.bfloat16)
    query_total_sum = jnp.einsum(
        "qk,ke->qe", dscore, key_window, preferred_element_type=jnp.float32
    )
    key_part = jnp.einsum("qk,qe->ke", dscore, query_norm, preferred_element_type=jnp.float32)
    value_part = jnp.einsum("qk,qe->ke", prob_low, grad_loc, preferred_element_type=jnp.float32)
    query_gradient = norm_grad(
        query_entries, query_inv, query_gain, QUERY_SCALE, query_total_sum
    ).astype(jnp.bfloat16)
    return attended, query_gradient, key_part, value_part


def on_device(
    query_matrix, key_matrix, value_matrix, output_gradient, query_gain, key_gain, doc_ids
):
    token_rows, head_devices = query_matrix.shape[0], lax.axis_size("head")
    x_parts = head_devices // Z_PARTS
    group_width = query_matrix.shape[1] // key_matrix.shape[1]
    queries = query_matrix.reshape(token_rows, head_devices, group_width, HEAD_WIDTH)
    grads = output_gradient.reshape(token_rows, head_devices, group_width, HEAD_WIDTH)
    keys = key_matrix.reshape(token_rows, head_devices, HEAD_WIDTH)
    values = value_matrix.reshape(token_rows, head_devices, HEAD_WIDTH)

    def sent(parts):
        packed = jnp.concatenate(parts, axis=-1)
        return to_heads(packed.reshape(token_rows, x_parts, Z_PARTS, -1))

    first = sent([keys, values, queries[:, :, 0], grads[:, :, 0]])
    later = [
        sent([queries[:, :, g], grads[:, :, g]]) for g in range(1, group_width)
    ]
    row_count = first.shape[0]
    key_entries = first[:, :HEAD_WIDTH].astype(jnp.float32)
    key_inv, key_norm_factor = normalize(key_entries, key_gain, 1.0)
    own_pair = jnp.concatenate([key_norm_factor, first[:, HEAD_WIDTH : 2 * HEAD_WIDTH]], axis=-1)
    pairs = [own_pair] + [
        passed_along(own_pair, "ctx", offset) for offset in range(1, REACH + 1)
    ]
    window = jnp.concatenate(pairs[::-1], axis=0)
    key_window = window[:, :HEAD_WIDTH]
    value_window = window[:, HEAD_WIDTH:]
    ctx_place = lax.axis_index("ctx")
    row_start = ctx_place * row_count
    window_rows = (REACH + 1) * row_count
    query_docs = lax.dynamic_slice_in_dim(doc_ids, row_start, row_count, 0)
    query_pos = row_start + jnp.arange(row_count, dtype=jnp.int32)
    key_pos = row_start - REACH * row_count + jnp.arange(window_rows, dtype=jnp.int32)
    padded_docs = jnp.concatenate(
        [jnp.full((REACH * row_count,), -1, jnp.int32), doc_ids.astype(jnp.int32)]
    )
    key_docs = lax.dynamic_slice_in_dim(padded_docs, row_start, window_rows, 0)
    allowed = (query_docs[:, None] == key_docs[None, :]) & (key_pos[None, :] <= query_pos[:, None])
    sources = [first[:, 2 * HEAD_WIDTH :]] + later
    results = []
    key_total = None
    for g in range(group_width):
        attended, query_gradient, key_part, value_part = one_head(
            sources[g][:, :HEAD_WIDTH],
            sources[g][:, HEAD_WIDTH:],
            query_gain,
            key_window,
            value_window,
            allowed,
        )
        if g + 1 < group_width:
            results.append(from_heads(jnp.concatenate([attended, query_gradient], -1), token_rows))
        else:
            results.append((attended, query_gradient))
        grad_parts = jnp.concatenate([key_part, value_part], axis=-1)
        key_total = grad_parts if key_total is None else key_total + grad_parts
    total = key_total[REACH * row_count :]
    for offset in range(1, REACH + 1):
        start = (REACH - offset) * row_count
        arrived = passed_along(for_sending(key_total[start : start + row_count]), "ctx", -offset)
        total = total + arrived
    key_gradient = norm_grad(
        key_entries, key_inv, key_gain, 1.0, total[:, :HEAD_WIDTH]
    ).astype(jnp.bfloat16)
    value_gradient = total[:, HEAD_WIDTH:].astype(jnp.bfloat16)
    attended, query_gradient = results[-1]
    final = from_heads(
        jnp.concatenate([attended, query_gradient, key_gradient, value_gradient], -1), token_rows
    )
    attended_heads = [r[..., :HEAD_WIDTH] for r in results[:-1]] + [final[..., :HEAD_WIDTH]]
    query_heads = [r[..., HEAD_WIDTH:] for r in results[:-1]] + [
        final[..., HEAD_WIDTH : 2 * HEAD_WIDTH]
    ]
    return (
        jnp.stack(attended_heads, 2).reshape(token_rows, -1),
        jnp.stack(query_heads, 2).reshape(token_rows, -1),
        final[..., 2 * HEAD_WIDTH : 3 * HEAD_WIDTH].reshape(token_rows, -1),
        final[..., 3 * HEAD_WIDTH :].reshape(token_rows, -1),
    )


def solution(mesh):
    placed = (
        P(("ctx", "head"), None),
        P(("ctx", "head"), None),
        P(("ctx", "head"), None),
        P(("ctx", "head"), None),
        P(),
        P(),
        P(),
    )
    return jax.shard_map(
        on_device,
        mesh=mesh,
        in_specs=placed,
        out_specs=(
            P(("ctx", "head"), None),
            P(("ctx", "head"), None),
            P(("ctx", "head"), None),
            P(("ctx", "head"), None),
        ),
        check_vma=False,
    )
```

time: 267 us -> 298 us (1.12)
  the two profiles are of different devices: /device:TPU:57 before, /device:TPU:128 now
where the time goes in v3:
time: 298 us; the launch traced here: 297 us
  starting transfers between devices  169 us (57%)
  waiting for transfers between devices  94.6 us (32%)
  matrix products  13.9 us (5%)
  local copies, waits for them, and re-layouts  13.4 us (4%)
  other arithmetic  4.88 us (2%)
    ppermute x24, starting transfers between devices, shifted(): return lax.ppermute(block, 'head', [(i, target(i)) for i in range(size)])  156 us
    ppermute x24, waiting for transfers between devices, shifted(): return lax.ppermute(block, 'head', [(i, target(i)) for i in range(size)])  82.6 us
    ppermute x4, starting transfers between devices, passed_along(): return lax.ppermute(block, axis, route)  12.9 us
    ppermute x4, waiting for transfers between devices, passed_along(): return lax.ppermute(block, axis, route)  12 us
  transfers between devices with their start and end apart: 28, of which 9 were waited for; matrix products, arithmetic and copies ran while one was open for 2% of the time, Pallas kernels for 0%

profile of v3, /device:TPU:128, one launch (start us, length us, event | category | flops | bytes accessed | tf_op | source)
XLA Modules:
  0.0 297.4 jit_solution(6309373873896733313)
XLA Ops:
  1.8 1.0 concatenate.55
  2.7 1.1 reshape.124
  4.3 1.1 reshape.125
  6.3 1.1 constant_dynamic-slice_fusion.3
  7.5 18.2 %collective-permute-start.2 = (bf16[32,4,512]{2,0,1:T(8,128)(2,1)S(1)}, bf16[32,4,512]{2,0,1:T(8,128)(2,1)S(1)}, u32[]{:S(2)}, u32[]{:S(2)}) collective-permute-start(bf16[32,4,512]{2,0,1:T(8,128)(2,1)S(1)} %bitcast.144), channel_id=1, source_target_pairs={{0,3},{1,0},{2,1},{3,2},{4,7},{5,4},{6,5},{7,6},{8,11},{9,8},{10,9... | collective-permute-start | bytes 393224 | tf_op jit(solution)/shard_map/ppermute | solution.py:45
  25.8 9.6 %collective-permute-start.1 = (bf16[32,4,512]{2,0,1:T(8,128)(2,1)S(1)}, bf16[32,4,512]{2,0,1:T(8,128)(2,1)S(1)}, u32[]{:S(2)}, u32[]{:S(2)}) collective-permute-start(bf16[32,4,512]{2,0,1:T(8,128)(2,1)S(1)} %bitcast.143), channel_id=1, source_target_pairs={{0,2},{1,3},{2,0},{3,1},{4,6},{5,7},{6,4},{7,5},{8,10},{9,11},{10,... | collective-permute-start | bytes 393224 | tf_op jit(solution)/shard_map/ppermute | solution.py:45
  35.6 1.9 collective-permute-start.16
  37.6 21.1 %collective-permute-start.15 = (bf16[32,4,256]{2,0,1:T(8,128)(2,1)S(1)}, bf16[32,4,256]{2,0,1:T(8,128)(2,1)S(1)}, u32[]{:S(2)}, u32[]{:S(2)}) collective-permute-start(bf16[32,4,256]{2,0,1:T(8,128)(2,1)S(1)} %get-tuple-element.56), channel_id=1, source_target_pairs={{0,2},{1,3},{2,0},{3,1},{4,6},{5,7},{6,4},{7,5},{8,10},{9,11},{10,... | collective-permute-start | bytes 196616 | tf_op jit(solution)/shard_map/ppermute | solution.py:45
  58.7 6.1 %collective-permute-start.14 = (bf16[32,4,256]{2,0,1:T(8,128)(2,1)S(1)}, bf16[32,4,256]{2,0,1:T(8,128)(2,1)S(1)}, u32[]{:S(2)}, u32[]{:S(2)}) collective-permute-start(bf16[32,4,256]{2,0,1:T(8,128)(2,1)S(1)} %get-tuple-element.55), channel_id=1, source_target_pairs={{0,1},{1,2},{2,3},{3,0},{4,5},{5,6},{6,7},{7,4},{8,9},{9,10},{10,1... | collective-permute-start | bytes 196616 | tf_op jit(solution)/shard_map/ppermute | solution.py:45
  65.3 19.8 %collective-permute-done.16 = bf16[32,4,256]{2,0,1:T(8,128)(2,1)S(1)} collective-permute-done((bf16[32,4,256]{2,0,1:T(8,128)(2,1)S(1)}, bf16[32,4,256]{2,0,1:T(8,128)(2,1)S(1)}, u32[]{:S(2)}, u32[]{:S(2)}) %collective-permute-start.16) | collective-permute-done | bytes 65568 | tf_op jit(solution)/shard_map/ppermute | solution.py:45
  85.0 5.5 %collective-permute-start = (bf16[32,4,512]{2,0,1:T(8,128)(2,1)S(1)}, bf16[32,4,512]{2,0,1:T(8,128)(2,1)S(1)}, u32[]{:S(2)}, u32[]{:S(2)}) collective-permute-start(bf16[32,4,512]{2,0,1:T(8,128)(2,1)S(1)} %bitcast.145), channel_id=1, source_target_pairs={{0,1},{1,2},{2,3},{3,0},{4,5},{5,6},{6,7},{7,4},{8,9},{9,10},{10,1... | collective-permute-start | bytes 393224 | tf_op jit(solution)/shard_map/ppermute | solution.py:45
  90.6 4.8 %collective-permute-start.19 = (bf16[4,32,256]{2,1,0:T(8,128)(2,1)S(1)}, bf16[4,32,256]{2,1,0:T(8,128)(2,1)S(1)}, u32[]{:S(2)}, u32[]{:S(2)}) collective-permute-start(bf16[4,32,256]{2,1,0:T(8,128)(2,1)S(1)} %get-tuple-element.51), channel_id=1, source_target_pairs={{0,12},{1,13},{2,14},{3,15},{4,0},{5,1},{6,2},{7,3},{8,4},{9,5},{1... | collective-permute-start | bytes 196616 | tf_op jit(solution)/shard_map/ppermute | solution.py:45
  95.4 2.7 collective-permute-start.18
  98.1 2.8 collective-permute-start.17
  100.9 6.8 %collective-permute-done = bf16[32,4,512]{2,0,1:T(8,128)(2,1)S(1)} collective-permute-done((bf16[32,4,512]{2,0,1:T(8,128)(2,1)S(1)}, bf16[32,4,512]{2,0,1:T(8,128)(2,1)S(1)}, u32[]{:S(2)}, u32[]{:S(2)}) %collective-permute-start) | collective-permute-done | bytes 131104 | tf_op jit(solution)/shard_map/ppermute | solution.py:45
  107.9 2.1 collective-permute-start.5
  110.0 2.7 collective-permute-start.4
  112.7 2.9 collective-permute-start.3
  116.4 3.3 %collective-permute-done.4 = bf16[4,32,512]{2,1,0:T(8,128)(2,1)S(1)} collective-permute-done((bf16[4,32,512]{2,1,0:T(8,128)(2,1)S(1)}, bf16[4,32,512]{2,1,0:T(8,128)(2,1)S(1)}, u32[]{:S(2)}, u32[]{:S(2)}) %collective-permute-start.4) | collective-permute-done | bytes 131104 | tf_op jit(solution)/shard_map/ppermute | solution.py:45
  119.7 1.5 collective-permute-done.3
  122.4 1.9 collective-permute-start.7
  124.3 3.6 %collective-permute-start.6 = (bf16[512,256]{0,1:T(8,128)(2,1)S(1)}, bf16[512,256]{0,1:T(8,128)(2,1)S(1)}, u32[]{:S(2)}, u32[]{:S(2)}) collective-permute-start(bf16[512,256]{0,1:T(8,128)(2,1)S(1)} %pad_maximum_fusion.4), channel_id=1, source_target_pairs={{0,32},{16,48},{32,64},{48,80},{64,96},{80,112},{96,128},{112,144}... | collective-permute-start | bytes 786440 | tf_op jit(solution)/shard_map/ppermute | solution.py:19
  128.3 6.3 %collective-permute-done.7 = bf16[512,256]{0,1:T(8,128)(2,1)S(1)} collective-permute-done((bf16[512,256]{0,1:T(8,128)(2,1)S(1)}, bf16[512,256]{0,1:T(8,128)(2,1)S(1)}, u32[]{:S(2)}, u32[]{:S(2)}) %collective-permute-start.7) | collective-permute-done | bytes 262176 | tf_op jit(solution)/shard_map/ppermute | solution.py:19
  134.6 5.6 %collective-permute-done.6 = bf16[512,256]{0,1:T(8,128)(2,1)S(1)} collective-permute-done((bf16[512,256]{0,1:T(8,128)(2,1)S(1)}, bf16[512,256]{0,1:T(8,128)(2,1)S(1)}, u32[]{:S(2)}, u32[]{:S(2)}) %collective-permute-start.6) | collective-permute-done | bytes 262176 | tf_op jit(solution)/shard_map/ppermute | solution.py:19
  141.0 2.3 fusion.12
  143.3 1.1 fusion.20
  144.5 1.7 multiply_reduce_fusion
  146.1 1.9 fusion.6
  149.1 1.1 fusion.18
  150.3 1.0 multiply_reduce_fusion.1
  151.3 1.9 fusion.7
  155.3 5.3 %collective-permute-start.21 = (bf16[512,256]{0,1:T(8,128)(2,1)}, bf16[512,256]{0,1:T(8,128)(2,1)S(1)}, u32[]{:S(2)}, u32[]{:S(2)}) collective-permute-start(bf16[512,256]{0,1:T(8,128)(2,1)} %get-tuple-element.13), channel_id=1, source_target_pairs={{32,0},{48,16},{64,32},{80,48},{96,64},{112,80},{128,96},{144,112}... | collective-permute-start | bytes 786440 | tf_op jit(solution)/shard_map/ppermute | solution.py:19
  160.6 2.1 collective-permute-start.20
  163.2 1.9 collective-permute-start.10
  165.2 3.7 %collective-permute-start.9 = (bf16[4,32,256]{2,1,0:T(8,128)(2,1)S(1)}, bf16[4,32,256]{2,1,0:T(8,128)(2,1)S(1)}, u32[]{:S(2)}, u32[]{:S(2)}) collective-permute-start(bf16[4,32,256]{2,1,0:T(8,128)(2,1)S(1)} %get-tuple-element.45), channel_id=1, source_target_pairs={{0,8},{1,9},{2,10},{3,11},{4,12},{5,13},{6,14},{7,15},{8,0},{9,1},... | collective-permute-start | bytes 196616 | tf_op jit(solution)/shard_map/ppermute | solution.py:45
  168.9 4.2 %collective-permute-start.8 = (bf16[4,32,256]{2,1,0:T(8,128)(2,1)S(1)}, bf16[4,32,256]{2,1,0:T(8,128)(2,1)S(1)}, u32[]{:S(2)}, u32[]{:S(2)}) collective-permute-start(bf16[4,32,256]{2,1,0:T(8,128)(2,1)S(1)} %get-tuple-element.46), channel_id=1, source_target_pairs={{0,12},{1,13},{2,14},{3,15},{4,0},{5,1},{6,2},{7,3},{8,4},{9,5},{1... | collective-permute-start | bytes 196616 | tf_op jit(solution)/shard_map/ppermute | solution.py:45
  173.2 2.1 collective-permute-done.8
  175.4 7.1 %collective-permute-start.11 = (bf16[4,32,256]{2,1,0:T(8,128)(2,1)S(1)}, bf16[4,32,256]{2,1,0:T(8,128)(2,1)S(1)}, u32[]{:S(2)}, u32[]{:S(2)}) collective-permute-start(bf16[4,32,256]{2,1,0:T(8,128)(2,1)S(1)} %get-tuple-element.43), channel_id=1, source_target_pairs={{0,3},{1,0},{2,1},{3,2},{4,7},{5,4},{6,5},{7,6},{8,11},{9,8},{10,9... | collective-permute-start | bytes 196616 | tf_op jit(solution)/shard_map/ppermute | solution.py:45
  182.5 17.6 %collective-permute-start.12 = (bf16[4,32,256]{2,1,0:T(8,128)(2,1)S(1)}, bf16[4,32,256]{2,1,0:T(8,128)(2,1)S(1)}, u32[]{:S(2)}, u32[]{:S(2)}) collective-permute-start(bf16[4,32,256]{2,1,0:T(8,128)(2,1)S(1)} %get-tuple-element.42), channel_id=1, source_target_pairs={{0,2},{1,3},{2,0},{3,1},{4,6},{5,7},{6,4},{7,5},{8,10},{9,11},{10,... | collective-permute-start | bytes 196616 | tf_op jit(solution)/shard_map/ppermute | solution.py:45
  200.1 2.1 collective-permute-start.13
  204.4 3.9 %collective-permute-start.24 = (bf16[4,32,512]{2,1,0:T(8,128)(2,1)S(1)}, bf16[4,32,512]{2,1,0:T(8,128)(2,1)S(1)}, u32[]{:S(2)}, u32[]{:S(2)}) collective-permute-start(bf16[4,32,512]{2,1,0:T(8,128)(2,1)S(1)} %get-tuple-element.25), channel_id=1, source_target_pairs={{0,4},{1,5},{2,6},{3,7},{4,8},{5,9},{6,10},{7,11},{8,12},{9,13},{1... | collective-permute-start | bytes 393224 | tf_op jit(solution)/shard_map/ppermute | solution.py:45
  208.3 4.6 %collective-permute-start.23 = (bf16[4,32,512]{2,1,0:T(8,128)(2,1)S(1)}, bf16[4,32,512]{2,1,0:T(8,128)(2,1)S(1)}, u32[]{:S(2)}, u32[]{:S(2)}) collective-permute-start(bf16[4,32,512]{2,1,0:T(8,128)(2,1)S(1)} %get-tuple-element.23), channel_id=1, source_target_pairs={{0,8},{1,9},{2,10},{3,11},{4,12},{5,13},{6,14},{7,15},{8,0},{9,1},... | collective-permute-start | bytes 393224 | tf_op jit(solution)/shard_map/ppermute | solution.py:45
  212.9 1.9 collective-permute-start.22
  214.8 5.3 %collective-permute-done.13 = bf16[4,32,256]{2,1,0:T(8,128)(2,1)S(1)} collective-permute-done((bf16[4,32,256]{2,1,0:T(8,128)(2,1)S(1)}, bf16[4,32,256]{2,1,0:T(8,128)(2,1)S(1)}, u32[]{:S(2)}, u32[]{:S(2)}) %collective-permute-start.13) | collective-permute-done | bytes 65568 | tf_op jit(solution)/shard_map/ppermute | solution.py:45
  220.8 11.1 %collective-permute-start.25 = (bf16[4,32,512]{2,1,0:T(8,128)(2,1)S(1)}, bf16[4,32,512]{2,1,0:T(8,128)(2,1)S(1)}, u32[]{:S(2)}, u32[]{:S(2)}) collective-permute-start(bf16[4,32,512]{2,1,0:T(8,128)(2,1)S(1)} %get-tuple-element.21), channel_id=1, source_target_pairs={{0,3},{1,0},{2,1},{3,2},{4,7},{5,4},{6,5},{7,6},{8,11},{9,8},{10,9... | collective-permute-start | bytes 393224 | tf_op jit(solution)/shard_map/ppermute | solution.py:45
  231.9 13.0 %collective-permute-start.26 = (bf16[4,32,512]{2,1,0:T(8,128)(2,1)S(1)}, bf16[4,32,512]{2,1,0:T(8,128)(2,1)S(1)}, u32[]{:S(2)}, u32[]{:S(2)}) collective-permute-start(bf16[4,32,512]{2,1,0:T(8,128)(2,1)S(1)} %get-tuple-element.20), channel_id=1, source_target_pairs={{0,2},{1,3},{2,0},{3,1},{4,6},{5,7},{6,4},{7,5},{8,10},{9,11},{10,... | collective-permute-start | bytes 393224 | tf_op jit(solution)/shard_map/ppermute | solution.py:45
  245.0 4.1 %collective-permute-start.27 = (bf16[4,32,512]{2,1,0:T(8,128)(2,1)S(1)}, bf16[4,32,512]{2,1,0:T(8,128)(2,1)S(1)}, u32[]{:S(2)}, u32[]{:S(2)}) collective-permute-start(bf16[4,32,512]{2,1,0:T(8,128)(2,1)S(1)} %get-tuple-element.18), channel_id=1, source_target_pairs={{0,1},{1,2},{2,3},{3,0},{4,5},{5,6},{6,7},{7,4},{8,9},{9,10},{10,1... | collective-permute-start | bytes 393224 | tf_op jit(solution)/shard_map/ppermute | solution.py:45
  249.1 43.6 %collective-permute-done.26 = bf16[4,32,512]{2,1,0:T(8,128)(2,1)S(1)} collective-permute-done((bf16[4,32,512]{2,1,0:T(8,128)(2,1)S(1)}, bf16[4,32,512]{2,1,0:T(8,128)(2,1)S(1)}, u32[]{:S(2)}, u32[]{:S(2)}) %collective-permute-start.26) | collective-permute-done | bytes 131104 | tf_op jit(solution)/shard_map/ppermute | solution.py:45
  (127 shorter events, 16.8 us)
Async XLA Ops:
  5.8 59.3 %copy-start = (s32[32768]{0:T(1024)S(1)}, s32[32768]{0:T(1024)}, u32[]{:S(2)}) copy-start(s32[32768]{0:T(1024)} %param.21) | copy-start | bytes 393220
  7.5 90.6 %collective-permute-start.2 = (bf16[32,4,512]{2,0,1:T(8,128)(2,1)S(1)}, bf16[32,4,512]{2,0,1:T(8,128)(2,1)S(1)}, u32[]{:S(2)}, u32[]{:S(2)}) collective-permute-start(bf16[32,4,512]{2,0,1:T(8,128)(2,1)S(1)} %bitcast.144), channel_id=1, source_target_pairs={{0,3},{1,0},{2,1},{3,2},{4,7},{5,4},{6,5},{7,6},{8,11},{9,8},{10,9... | collective-permute-start | bytes 393224 | tf_op jit(solution)/shard_map/ppermute | solution.py:45
  25.8 75.1 %collective-permute-start.1 = (bf16[32,4,512]{2,0,1:T(8,128)(2,1)S(1)}, bf16[32,4,512]{2,0,1:T(8,128)(2,1)S(1)}, u32[]{:S(2)}, u32[]{:S(2)}) collective-permute-start(bf16[32,4,512]{2,0,1:T(8,128)(2,1)S(1)} %bitcast.143), channel_id=1, source_target_pairs={{0,2},{1,3},{2,0},{3,1},{4,6},{5,7},{6,4},{7,5},{8,10},{9,11},{10,... | collective-permute-start | bytes 393224 | tf_op jit(solution)/shard_map/ppermute | solution.py:45
  35.6 49.4 %collective-permute-start.16 = (bf16[32,4,256]{2,0,1:T(8,128)(2,1)S(1)}, bf16[32,4,256]{2,0,1:T(8,128)(2,1)S(1)}, u32[]{:S(2)}, u32[]{:S(2)}) collective-permute-start(bf16[32,4,256]{2,0,1:T(8,128)(2,1)S(1)} %get-tuple-element.57), channel_id=1, source_target_pairs={{0,3},{1,0},{2,1},{3,2},{4,7},{5,4},{6,5},{7,6},{8,11},{9,8},{10,9... | collective-permute-start | bytes 196616 | tf_op jit(solution)/shard_map/ppermute | solution.py:45
  37.6 52.9 %collective-permute-start.15 = (bf16[32,4,256]{2,0,1:T(8,128)(2,1)S(1)}, bf16[32,4,256]{2,0,1:T(8,128)(2,1)S(1)}, u32[]{:S(2)}, u32[]{:S(2)}) collective-permute-start(bf16[32,4,256]{2,0,1:T(8,128)(2,1)S(1)} %get-tuple-element.56), channel_id=1, source_target_pairs={{0,2},{1,3},{2,0},{3,1},{4,6},{5,7},{6,4},{7,5},{8,10},{9,11},{10,... | collective-permute-start | bytes 196616 | tf_op jit(solution)/shard_map/ppermute | solution.py:45
  58.7 31.9 %collective-permute-start.14 = (bf16[32,4,256]{2,0,1:T(8,128)(2,1)S(1)}, bf16[32,4,256]{2,0,1:T(8,128)(2,1)S(1)}, u32[]{:S(2)}, u32[]{:S(2)}) collective-permute-start(bf16[32,4,256]{2,0,1:T(8,128)(2,1)S(1)} %get-tuple-element.55), channel_id=1, source_target_pairs={{0,1},{1,2},{2,3},{3,0},{4,5},{5,6},{6,7},{7,4},{8,9},{9,10},{10,1... | collective-permute-start | bytes 196616 | tf_op jit(solution)/shard_map/ppermute | solution.py:45
  85.0 22.7 %collective-permute-start = (bf16[32,4,512]{2,0,1:T(8,128)(2,1)S(1)}, bf16[32,4,512]{2,0,1:T(8,128)(2,1)S(1)}, u32[]{:S(2)}, u32[]{:S(2)}) collective-permute-start(bf16[32,4,512]{2,0,1:T(8,128)(2,1)S(1)} %bitcast.145), channel_id=1, source_target_pairs={{0,1},{1,2},{2,3},{3,0},{4,5},{5,6},{6,7},{7,4},{8,9},{9,10},{10,1... | collective-permute-start | bytes 393224 | tf_op jit(solution)/shard_map/ppermute | solution.py:45
  90.6 22.1 %collective-permute-start.19 = (bf16[4,32,256]{2,1,0:T(8,128)(2,1)S(1)}, bf16[4,32,256]{2,1,0:T(8,128)(2,1)S(1)}, u32[]{:S(2)}, u32[]{:S(2)}) collective-permute-start(bf16[4,32,256]{2,1,0:T(8,128)(2,1)S(1)} %get-tuple-element.51), channel_id=1, source_target_pairs={{0,12},{1,13},{2,14},{3,15},{4,0},{5,1},{6,2},{7,3},{8,4},{9,5},{1... | collective-permute-start | bytes 196616 | tf_op jit(solution)/shard_map/ppermute | solution.py:45
  95.4 20.3 %collective-permute-start.18 = (bf16[4,32,256]{2,1,0:T(8,128)(2,1)S(1)}, bf16[4,32,256]{2,1,0:T(8,128)(2,1)S(1)}, u32[]{:S(2)}, u32[]{:S(2)}) collective-permute-start(bf16[4,32,256]{2,1,0:T(8,128)(2,1)S(1)} %get-tuple-element.52), channel_id=1, source_target_pairs={{0,8},{1,9},{2,10},{3,11},{4,12},{5,13},{6,14},{7,15},{8,0},{9,1},... | collective-permute-start | bytes 196616 | tf_op jit(solution)/shard_map/ppermute | solution.py:45
  98.1 17.6 %collective-permute-start.17 = (bf16[4,32,256]{2,1,0:T(8,128)(2,1)S(1)}, bf16[4,32,256]{2,1,0:T(8,128)(2,1)S(1)}, u32[]{:S(2)}, u32[]{:S(2)}) collective-permute-start(bf16[4,32,256]{2,1,0:T(8,128)(2,1)S(1)} %get-tuple-element.53), channel_id=1, source_target_pairs={{0,4},{1,5},{2,6},{3,7},{4,8},{5,9},{6,10},{7,11},{8,12},{9,13},{1... | collective-permute-start | bytes 196616 | tf_op jit(solution)/shard_map/ppermute | solution.py:45
  107.9 8.5 %collective-permute-start.5 = (bf16[4,32,512]{2,1,0:T(8,128)(2,1)S(1)}, bf16[4,32,512]{2,1,0:T(8,128)(2,1)S(1)}, u32[]{:S(2)}, u32[]{:S(2)}) collective-permute-start(bf16[4,32,512]{2,1,0:T(8,128)(2,1)S(1)} %get-tuple-element.31), channel_id=1, source_target_pairs={{0,12},{1,13},{2,14},{3,15},{4,0},{5,1},{6,2},{7,3},{8,4},{9,5},{1... | collective-permute-start | bytes 393224 | tf_op jit(solution)/shard_map/ppermute | solution.py:45
  110.0 9.7 %collective-permute-start.4 = (bf16[4,32,512]{2,1,0:T(8,128)(2,1)S(1)}, bf16[4,32,512]{2,1,0:T(8,128)(2,1)S(1)}, u32[]{:S(2)}, u32[]{:S(2)}) collective-permute-start(bf16[4,32,512]{2,1,0:T(8,128)(2,1)S(1)} %get-tuple-element.32), channel_id=1, source_target_pairs={{0,8},{1,9},{2,10},{3,11},{4,12},{5,13},{6,14},{7,15},{8,0},{9,1},... | collective-permute-start | bytes 393224 | tf_op jit(solution)/shard_map/ppermute | solution.py:45
  112.7 8.5 %collective-permute-start.3 = (bf16[4,32,512]{2,1,0:T(8,128)(2,1)S(1)}, bf16[4,32,512]{2,1,0:T(8,128)(2,1)S(1)}, u32[]{:S(2)}, u32[]{:S(2)}) collective-permute-start(bf16[4,32,512]{2,1,0:T(8,128)(2,1)S(1)} %get-tuple-element.33), channel_id=1, source_target_pairs={{0,4},{1,5},{2,6},{3,7},{4,8},{5,9},{6,10},{7,11},{8,12},{9,13},{1... | collective-permute-start | bytes 393224 | tf_op jit(solution)/shard_map/ppermute | solution.py:45
  121.3 1.0 copy-start.2
  121.7 18.6 %copy-start.1 = (f32[128]{0:T(128)S(1)}, f32[128]{0:T(128)}, u32[]{:S(2)}) copy-start(f32[128]{0:T(128)} %param.19) | copy-start | bytes 1540
  122.4 12.2 %collective-permute-start.7 = (bf16[512,256]{0,1:T(8,128)(2,1)S(1)}, bf16[512,256]{0,1:T(8,128)(2,1)S(1)}, u32[]{:S(2)}, u32[]{:S(2)}) collective-permute-start(bf16[512,256]{0,1:T(8,128)(2,1)S(1)} %pad_maximum_fusion.4), channel_id=1, source_target_pairs={{0,16},{16,32},{32,48},{48,64},{64,80},{80,96},{96,112},{112,128},... | collective-permute-start | bytes 786440 | tf_op jit(solution)/shard_map/ppermute | solution.py:19
  124.3 15.9 %collective-permute-start.6 = (bf16[512,256]{0,1:T(8,128)(2,1)S(1)}, bf16[512,256]{0,1:T(8,128)(2,1)S(1)}, u32[]{:S(2)}, u32[]{:S(2)}) collective-permute-start(bf16[512,256]{0,1:T(8,128)(2,1)S(1)} %pad_maximum_fusion.4), channel_id=1, source_target_pairs={{0,32},{16,48},{32,64},{48,80},{64,96},{80,112},{96,128},{112,144}... | collective-permute-start | bytes 786440 | tf_op jit(solution)/shard_map/ppermute | solution.py:19
  155.3 47.0 %collective-permute-start.21 = (bf16[512,256]{0,1:T(8,128)(2,1)}, bf16[512,256]{0,1:T(8,128)(2,1)S(1)}, u32[]{:S(2)}, u32[]{:S(2)}) collective-permute-start(bf16[512,256]{0,1:T(8,128)(2,1)} %get-tuple-element.13), channel_id=1, source_target_pairs={{32,0},{48,16},{64,32},{80,48},{96,64},{112,80},{128,96},{144,112}... | collective-permute-start | bytes 786440 | tf_op jit(solution)/shard_map/ppermute | solution.py:19
  160.6 41.7 %collective-permute-start.20 = (bf16[512,256]{0,1:T(8,128)(2,1)S(1)}, bf16[512,256]{0,1:T(8,128)(2,1)S(1)}, u32[]{:S(2)}, u32[]{:S(2)}) collective-permute-start(bf16[512,256]{0,1:T(8,128)(2,1)S(1)} %get-tuple-element.12), channel_id=1, source_target_pairs={{16,0},{32,16},{48,32},{64,48},{80,64},{96,80},{112,96},{128,112},... | collective-permute-start | bytes 786440 | tf_op jit(solution)/shard_map/ppermute | solution.py:19
  163.2 9.9 %collective-permute-start.10 = (bf16[4,32,256]{2,1,0:T(8,128)(2,1)S(1)}, bf16[4,32,256]{2,1,0:T(8,128)(2,1)S(1)}, u32[]{:S(2)}, u32[]{:S(2)}) collective-permute-start(bf16[4,32,256]{2,1,0:T(8,128)(2,1)S(1)} %get-tuple-element.47), channel_id=1, source_target_pairs={{0,4},{1,5},{2,6},{3,7},{4,8},{5,9},{6,10},{7,11},{8,12},{9,13},{1... | collective-permute-start | bytes 196616 | tf_op jit(solution)/shard_map/ppermute | solution.py:45
  165.2 8.0 %collective-permute-start.9 = (bf16[4,32,256]{2,1,0:T(8,128)(2,1)S(1)}, bf16[4,32,256]{2,1,0:T(8,128)(2,1)S(1)}, u32[]{:S(2)}, u32[]{:S(2)}) collective-permute-start(bf16[4,32,256]{2,1,0:T(8,128)(2,1)S(1)} %get-tuple-element.45), channel_id=1, source_target_pairs={{0,8},{1,9},{2,10},{3,11},{4,12},{5,13},{6,14},{7,15},{8,0},{9,1},... | collective-permute-start | bytes 196616 | tf_op jit(solution)/shard_map/ppermute | solution.py:45
  168.9 6.4 %collective-permute-start.8 = (bf16[4,32,256]{2,1,0:T(8,128)(2,1)S(1)}, bf16[4,32,256]{2,1,0:T(8,128)(2,1)S(1)}, u32[]{:S(2)}, u32[]{:S(2)}) collective-permute-start(bf16[4,32,256]{2,1,0:T(8,128)(2,1)S(1)} %get-tuple-element.46), channel_id=1, source_target_pairs={{0,12},{1,13},{2,14},{3,15},{4,0},{5,1},{6,2},{7,3},{8,4},{9,5},{1... | collective-permute-start | bytes 196616 | tf_op jit(solution)/shard_map/ppermute | solution.py:45
  175.4 37.5 %collective-permute-start.11 = (bf16[4,32,256]{2,1,0:T(8,128)(2,1)S(1)}, bf16[4,32,256]{2,1,0:T(8,128)(2,1)S(1)}, u32[]{:S(2)}, u32[]{:S(2)}) collective-permute-start(bf16[4,32,256]{2,1,0:T(8,128)(2,1)S(1)} %get-tuple-element.43), channel_id=1, source_target_pairs={{0,3},{1,0},{2,1},{3,2},{4,7},{5,4},{6,5},{7,6},{8,11},{9,8},{10,9... | collective-permute-start | bytes 196616 | tf_op jit(solution)/shard_map/ppermute | solution.py:45
  182.5 32.3 %collective-permute-start.12 = (bf16[4,32,256]{2,1,0:T(8,128)(2,1)S(1)}, bf16[4,32,256]{2,1,0:T(8,128)(2,1)S(1)}, u32[]{:S(2)}, u32[]{:S(2)}) collective-permute-start(bf16[4,32,256]{2,1,0:T(8,128)(2,1)S(1)} %get-tuple-element.42), channel_id=1, source_target_pairs={{0,2},{1,3},{2,0},{3,1},{4,6},{5,7},{6,4},{7,5},{8,10},{9,11},{10,... | collective-permute-start | bytes 196616 | tf_op jit(solution)/shard_map/ppermute | solution.py:45
  200.1 20.1 %collective-permute-start.13 = (bf16[4,32,256]{2,1,0:T(8,128)(2,1)S(1)}, bf16[4,32,256]{2,1,0:T(8,128)(2,1)S(1)}, u32[]{:S(2)}, u32[]{:S(2)}) collective-permute-start(bf16[4,32,256]{2,1,0:T(8,128)(2,1)S(1)} %get-tuple-element.40), channel_id=1, source_target_pairs={{0,1},{1,2},{2,3},{3,0},{4,5},{5,6},{6,7},{7,4},{8,9},{9,10},{10,1... | collective-permute-start | bytes 196616 | tf_op jit(solution)/shard_map/ppermute | solution.py:45
  204.4 16.3 %collective-permute-start.24 = (bf16[4,32,512]{2,1,0:T(8,128)(2,1)S(1)}, bf16[4,32,512]{2,1,0:T(8,128)(2,1)S(1)}, u32[]{:S(2)}, u32[]{:S(2)}) collective-permute-start(bf16[4,32,512]{2,1,0:T(8,128)(2,1)S(1)} %get-tuple-element.25), channel_id=1, source_target_pairs={{0,4},{1,5},{2,6},{3,7},{4,8},{5,9},{6,10},{7,11},{8,12},{9,13},{1... | collective-permute-start | bytes 393224 | tf_op jit(solution)/shard_map/ppermute | solution.py:45
  208.3 12.3 %collective-permute-start.23 = (bf16[4,32,512]{2,1,0:T(8,128)(2,1)S(1)}, bf16[4,32,512]{2,1,0:T(8,128)(2,1)S(1)}, u32[]{:S(2)}, u32[]{:S(2)}) collective-permute-start(bf16[4,32,512]{2,1,0:T(8,128)(2,1)S(1)} %get-tuple-element.23), channel_id=1, source_target_pairs={{0,8},{1,9},{2,10},{3,11},{4,12},{5,13},{6,14},{7,15},{8,0},{9,1},... | collective-permute-start | bytes 393224 | tf_op jit(solution)/shard_map/ppermute | solution.py:45
  212.9 7.7 %collective-permute-start.22 = (bf16[4,32,512]{2,1,0:T(8,128)(2,1)S(1)}, bf16[4,32,512]{2,1,0:T(8,128)(2,1)S(1)}, u32[]{:S(2)}, u32[]{:S(2)}) collective-permute-start(bf16[4,32,512]{2,1,0:T(8,128)(2,1)S(1)} %get-tuple-element.24), channel_id=1, source_target_pairs={{0,12},{1,13},{2,14},{3,15},{4,0},{5,1},{6,2},{7,3},{8,4},{9,5},{1... | collective-permute-start | bytes 393224 | tf_op jit(solution)/shard_map/ppermute | solution.py:45
  220.8 28.3 %collective-permute-start.25 = (bf16[4,32,512]{2,1,0:T(8,128)(2,1)S(1)}, bf16[4,32,512]{2,1,0:T(8,128)(2,1)S(1)}, u32[]{:S(2)}, u32[]{:S(2)}) collective-permute-start(bf16[4,32,512]{2,1,0:T(8,128)(2,1)S(1)} %get-tuple-element.21), channel_id=1, source_target_pairs={{0,3},{1,0},{2,1},{3,2},{4,7},{5,4},{6,5},{7,6},{8,11},{9,8},{10,9... | collective-permute-start | bytes 393224 | tf_op jit(solution)/shard_map/ppermute | solution.py:45
  231.9 60.8 %collective-permute-start.26 = (bf16[4,32,512]{2,1,0:T(8,128)(2,1)S(1)}, bf16[4,32,512]{2,1,0:T(8,128)(2,1)S(1)}, u32[]{:S(2)}, u32[]{:S(2)}) collective-permute-start(bf16[4,32,512]{2,1,0:T(8,128)(2,1)S(1)} %get-tuple-element.20), channel_id=1, source_target_pairs={{0,2},{1,3},{2,0},{3,1},{4,6},{5,7},{6,4},{7,5},{8,10},{9,11},{10,... | collective-permute-start | bytes 393224 | tf_op jit(solution)/shard_map/ppermute | solution.py:45
  245.0 47.8 %collective-permute-start.27 = (bf16[4,32,512]{2,1,0:T(8,128)(2,1)S(1)}, bf16[4,32,512]{2,1,0:T(8,128)(2,1)S(1)}, u32[]{:S(2)}, u32[]{:S(2)}) collective-permute-start(bf16[4,32,512]{2,1,0:T(8,128)(2,1)S(1)} %get-tuple-element.18), channel_id=1, source_target_pairs={{0,1},{1,2},{2,3},{3,0},{4,5},{5,6},{6,7},{7,4},{8,9},{9,10},{10,1... | collective-permute-start | bytes 393224 | tf_op jit(solution)/shard_map/ppermute | solution.py:45

commit v4 on v2

--- a/solution.py
+++ b/solution.py
@@ -140,21 +140,21 @@
     ).astype(jnp.bfloat16)
     key_gradient = norm_grad(key_entries, key_inv, key_gain, 1.0, key_total).astype(jnp.bfloat16)
     value_gradient = value_total.astype(jnp.bfloat16)
+    early = lax.all_to_all(
+        attended.reshape(row_count, 1, -1), "head", split_axis=0, concat_axis=1, tiled=True
+    )
     leaving = jnp.concatenate(
-        [
-            part.reshape(row_count, -1)
-            for part in (attended, query_gradient, key_gradient, value_gradient)
-        ],
+        [part.reshape(row_count, -1) for part in (query_gradient, key_gradient, value_gradient)],
         axis=-1,
     )
     home = lax.all_to_all(
         leaving.reshape(row_count, 1, -1), "head", split_axis=0, concat_axis=1, tiled=True
     )
     return (
+        early.reshape(token_rows, -1),
         home[:, :, : cuts[0]].reshape(token_rows, -1),
-        home[:, :, cuts[0] : 2 * cuts[0]].reshape(token_rows, -1),
-        home[:, :, 2 * cuts[0] : 2 * cuts[0] + widths[1]].reshape(token_rows, -1),
-        home[:, :, 2 * cuts[0] + widths[1] :].reshape(token_rows, -1),
+        home[:, :, cuts[0] : cuts[0] + widths[1]].reshape(token_rows, -1),
+        home[:, :, cuts[0] + widths[1] :].reshape(token_rows, -1),
     )
 
 

time: 267 us -> 281 us (1.052)
  the two profiles are of different devices: /device:TPU:57 before, /device:TPU:33 now
where the time goes in v4:
time: 281 us; the launch traced here: 280 us
  waiting for transfers between devices  170 us (60%)
  starting transfers between devices  63 us (22%)
  matrix products  16.5 us (6%)
  local copies, waits for them, and re-layouts  14.7 us (5%)
  other arithmetic  14.5 us (5%)
    all_to_all x1, waiting for transfers between devices, on_device(): lax.all_to_all(packed, 'head', split_axis=1, concat_axis=0, tiled=True)  83.2 us
    all_to_all x1, waiting for transfers between devices, on_device(): lax.all_to_all(leaving.reshape(row_count, 1, -1), 'head', split_axis=0, c...  64.1 us
    all_to_all x1, starting transfers between devices, on_device(): lax.all_to_all(packed, 'head', split_axis=1, concat_axis=0, tiled=True)  29.7 us
    ppermute x4, starting transfers between devices, passed_along(): return lax.ppermute(block, axis, route)  16.4 us
    ppermute x4, waiting for transfers between devices, passed_along(): return lax.ppermute(block, axis, route)  12.9 us
    all_to_all x1, starting transfers between devices, on_device(): lax.all_to_all(leaving.reshape(row_count, 1, -1), 'head', split_axis=0, c...  12.7 us
    all_to_all x1, waiting for transfers between devices, on_device(): lax.all_to_all(attended.reshape(row_count, 1, -1), 'head', split_axis=0,...  10.2 us
  transfers between devices with their start and end apart: 7, of which 5 were waited for; matrix products, arithmetic and copies ran while one was open for 7% of the time, Pallas kernels for 0%

profile of v4, /device:TPU:33, one launch (start us, length us, event | category | flops | bytes accessed | tf_op | source)
XLA Modules:
  0.0 280.2 jit_solution(2712802095228671974)
XLA Ops:
  0.6 1.1 copy_bitcast_fusion
  1.8 1.0 copy_bitcast_fusion.4
  2.7 1.0 pad_maximum_fusion
  3.7 29.7 %all-to-all-start = ((bf16[32,16,768]{2,0,1:T(8,128)(2,1)}), bf16[32,16,768]{2,0,1:T(8,128)(2,1)S(1)}, u32[]{:S(2)}, u32[]{:S(2)}) async-start(bf16[32,16,768]{2,0,1:T(8,128)(2,1)} %pad_maximum_fusion), calls=%async_computation | async-start | bytes 1572864 | tf_op jit(solution)/shard_map/all_to_all | solution.py:60
  33.4 0.8 dynamic_slice.6
  34.2 0.8 pad_dynamic-slice_fusion
  35.0 0.7 broadcast_bitcast_fusion
  35.7 1.9 compare_and_fusion
  37.5 83.2 %all-to-all-done = bf16[32,16,768]{2,0,1:T(8,128)(2,1)S(1)} async-done(((bf16[32,16,768]{2,0,1:T(8,128)(2,1)}), bf16[32,16,768]{2,0,1:T(8,128)(2,1)S(1)}, u32[]{:S(2)}, u32[]{:S(2)}) %all-to-all-start) | async-done | bytes 786464 | tf_op jit(solution)/shard_map/all_to_all | solution.py:60
  120.9 0.8 fusion.57
  121.8 3.2 %collective-permute-start = (bf16[512,1,256]{2,0,1:T(8,128)(2,1)S(1)}, bf16[512,1,256]{2,0,1:T(8,128)(2,1)}, u32[]{:S(2)}, u32[]{:S(2)}) collective-permute-start(bf16[512,1,256]{2,0,1:T(8,128)(2,1)S(1)} %pad_maximum_fusion.2), channel_id=1, source_target_pairs={{0,32},{16,48},{32,64},{48,80},{64,96},{80,112},{96,128},{112,144}... | collective-permute-start | bytes 786440 | tf_op jit(solution)/shard_map/ppermute | solution.py:18
  125.0 5.6 %collective-permute-start.1 = (bf16[512,1,256]{2,0,1:T(8,128)(2,1)S(1)}, bf16[512,1,256]{2,0,1:T(8,128)(2,1)}, u32[]{:S(2)}, u32[]{:S(2)}) collective-permute-start(bf16[512,1,256]{2,0,1:T(8,128)(2,1)S(1)} %pad_maximum_fusion.2), channel_id=1, source_target_pairs={{0,16},{16,32},{32,48},{48,64},{64,80},{80,96},{96,112},{112,128},... | collective-permute-start | bytes 786440 | tf_op jit(solution)/shard_map/ppermute | solution.py:18
  130.7 0.3 reshape.247
  131.0 0.6 multiply_reduce_fusion.2
  131.6 1.0 copy.187
  132.6 1.0 copy.212
  133.8 0.2 copy.209
  134.0 0.2 copy.211
  134.4 1.2 maximum_maximum_fusion
  135.6 3.7 %fusion.6 = (f32[2,512]{1,0:T(2,128)S(1)}, f32[1536,512,2]{1,0,2:T(8,128)S(1)}) fusion(pred[512,1536]{0,1:T(8,128)(4,1)} %compare_and_fusion, bf16[1536,1,256]{2,0,1:T(8,128)(2,1)S(1)} %maximum_maximum_fusion, f32[512,256]{1,0:T(8,128)S(1)} %copy.209, f32[256]{0:T(256)S(1)} %broadcast_bitcast_fusion, bf16[512,768]{1,0:T(8,128)(2,1)S(1)} %bitcast.230), kind=kOutput, calls=%fused_computation.11 | convolution fusion | flops 409598976 | bytes 8262656 | tf_op jit(solution)/shard_map/qhge,khe->hgqk/dot_general | solution.py:41
  139.3 2.8 %multiply_reduce_fusion.1 = (f32[512,2]{0,1:T(2,128)S(1)}, bf16[512,1,2,128]{0,3,2,1:T(8,128)(2,1)}) fusion(f32[512,1,2,128]{0,3,2,1:T(8,128)S(1)} %bitcast.239, f32[512,2]{0,1:T(2,128)S(1)} %bitcast.249, f32[1536,512,2]{1,0,2:T(8,128)S(1)} %get-tuple-element.14, pred[512,1536]{0,1:T(8,128)(4,1)S(1)} %copy-done.6, ...), kind=kOutput, calls=%fused_computation.39 | convolution fusion | flops 409598976 | bytes 8265728 | tf_op jit(solution)/shard_map/hgqk,khe->qhge/dot_general | solution.py:99
  142.2 2.7 fusion.17
  144.9 4.4 %fusion.8 = bf16[2,512,1536]{1,2,0:T(8,128)(2,1)S(1)} fusion(bf16[512,2,128]{0,2,1:T(8,128)(2,1)} %bitcast.243, f32[1536,512,2]{1,0,2:T(8,128)S(1)} %get-tuple-element.14, f32[2,512]{1,0:T(2,128)S(1)} %bitcast.250, f32[2,512]{1,0:T(2,128)S(1)} %log.9, pred[512,1536]{0,1:T(8,128)(4,1)S(1)} %copy-done.6, bf16[1536,1,256]{2,0,1:T(8,128)(2,1)S(1)} %maximum_maximum_fusion), kind=kOutput, calls=%fused_computation.13 | convolution fusion | flops 418381824 | bytes 10887168 | tf_op jit(solution)/shard_map/qhge,khe->hgqk/dot_general | solution.py:112
  149.3 0.5 broadcast.189
  149.8 1.7 reduce.7
  151.5 0.8 copy.242
  152.4 1.7 reshape.272
  154.1 4.3 %all-to-all-start.1 = ((bf16[16,2,4096]{2,1,0:T(2,128)(2,1)}), bf16[16,2,4096]{2,1,0:T(2,128)(2,1)S(1)}, u32[]{:S(2)}, u32[]{:S(2)}) async-start(bf16[16,2,4096]{2,1,0:T(2,128)(2,1)} %reshape.272), calls=%async_computation.1 | async-start | bytes 524288 | tf_op jit(solution)/shard_map/all_to_all | solution.py:143
  158.4 2.2 convolution_bitcast_fusion
  160.6 2.2 maximum_convert_fusion
  162.8 5.7 %collective-permute-start.2 = (bf16[512,1,256]{2,0,1:T(8,128)(2,1)}, bf16[512,1,256]{2,0,1:T(8,128)(2,1)}, u32[]{:S(2)}, u32[]{:S(2)}) collective-permute-start(bf16[512,1,256]{2,0,1:T(8,128)(2,1)} %get-tuple-element.4), channel_id=1, source_target_pairs={{16,0},{32,16},{48,32},{64,48},{80,64},{96,80},{112,96},{128,112},... | collective-permute-start | bytes 786440 | tf_op jit(solution)/shard_map/ppermute | solution.py:18
  168.5 1.9 collective-permute-start.3
  170.4 0.6 multiply_reduce_fusion
  171.4 0.7 collective-permute-done.2
  172.1 12.1 %collective-permute-done.3 = bf16[512,1,256]{2,0,1:T(8,128)(2,1)} collective-permute-done((bf16[512,1,256]{2,0,1:T(8,128)(2,1)}, bf16[512,1,256]{2,0,1:T(8,128)(2,1)}, u32[]{:S(2)}, u32[]{:S(2)}) %collective-permute-start.3) | collective-permute-done | bytes 262176 | tf_op jit(solution)/shard_map/ppermute | solution.py:18
  184.2 1.3 fusion.44
  185.5 1.6 fusion.56
  187.2 1.0 reduce.8
  188.2 1.2 reshape.274
  189.4 10.2 %all-to-all-done.1 = bf16[16,2,4096]{2,1,0:T(2,128)(2,1)S(1)} async-done(((bf16[16,2,4096]{2,1,0:T(2,128)(2,1)}), bf16[16,2,4096]{2,1,0:T(2,128)(2,1)S(1)}, u32[]{:S(2)}, u32[]{:S(2)}) %all-to-all-start.1) | async-done | bytes 262176 | tf_op jit(solution)/shard_map/all_to_all | solution.py:143
  199.6 12.7 %all-to-all-start.2 = ((bf16[16,2,8192]{2,1,0:T(2,128)(2,1)}), bf16[16,2,8192]{2,1,0:T(2,128)(2,1)S(1)}, u32[]{:S(2)}, u32[]{:S(2)}) async-start(bf16[16,2,8192]{2,1,0:T(2,128)(2,1)} %reshape.274), calls=%async_computation.2 | async-start | bytes 1048576 | tf_op jit(solution)/shard_map/all_to_all | solution.py:150
  212.2 0.3 reshape.273
  212.6 0.7 copy.226
  213.3 64.1 %all-to-all-done.2 = bf16[16,2,8192]{2,1,0:T(2,128)(2,1)S(1)} async-done(((bf16[16,2,8192]{2,1,0:T(2,128)(2,1)}), bf16[16,2,8192]{2,1,0:T(2,128)(2,1)S(1)}, u32[]{:S(2)}, u32[]{:S(2)}) %all-to-all-start.2) | async-done | bytes 524320 | tf_op jit(solution)/shard_map/all_to_all | solution.py:150
  277.4 0.5 reshape.275
  278.1 0.7 copy.223
  278.9 0.7 copy.240
  279.5 0.7 copy.241
  (42 shorter events, 1.2 us)
Async XLA Ops:
  0.6 1.1 copy-start
  3.7 117.0 %all-to-all-start = ((bf16[32,16,768]{2,0,1:T(8,128)(2,1)}), bf16[32,16,768]{2,0,1:T(8,128)(2,1)S(1)}, u32[]{:S(2)}, u32[]{:S(2)}) async-start(bf16[32,16,768]{2,0,1:T(8,128)(2,1)} %pad_maximum_fusion), calls=%async_computation | async-start | bytes 1572864 | tf_op jit(solution)/shard_map/all_to_all | solution.py:60
  120.7 18.5 %copy-start.2 = (bf16[32,16,768]{2,0,1:T(8,128)(2,1)}, bf16[32,16,768]{2,0,1:T(8,128)(2,1)S(1)}, u32[]{:S(2)}) copy-start(bf16[32,16,768]{2,0,1:T(8,128)(2,1)S(1)} %all-to-all-done) | copy-start | bytes 2359300
  121.8 12.6 %collective-permute-start = (bf16[512,1,256]{2,0,1:T(8,128)(2,1)S(1)}, bf16[512,1,256]{2,0,1:T(8,128)(2,1)}, u32[]{:S(2)}, u32[]{:S(2)}) collective-permute-start(bf16[512,1,256]{2,0,1:T(8,128)(2,1)S(1)} %pad_maximum_fusion.2), channel_id=1, source_target_pairs={{0,32},{16,48},{32,64},{48,80},{64,96},{80,112},{96,128},{112,144}... | collective-permute-start | bytes 786440 | tf_op jit(solution)/shard_map/ppermute | solution.py:18
  125.0 9.4 %collective-permute-start.1 = (bf16[512,1,256]{2,0,1:T(8,128)(2,1)S(1)}, bf16[512,1,256]{2,0,1:T(8,128)(2,1)}, u32[]{:S(2)}, u32[]{:S(2)}) collective-permute-start(bf16[512,1,256]{2,0,1:T(8,128)(2,1)S(1)} %pad_maximum_fusion.2), channel_id=1, source_target_pairs={{0,16},{16,32},{32,48},{48,64},{64,80},{80,96},{96,112},{112,128},... | collective-permute-start | bytes 786440 | tf_op jit(solution)/shard_map/ppermute | solution.py:18
  134.3 7.8 %copy-start.7 = (bf16[512,256]{0,1:T(8,128)(2,1)}, bf16[512,256]{0,1:T(8,128)(2,1)S(1)}, u32[]{:S(2)}) copy-start(bf16[512,256]{0,1:T(8,128)(2,1)S(1)} %copy.217) | copy-start | bytes 786436
  135.5 9.3 %copy-start.4 = (bf16[1536,1,256]{2,0,1:T(8,128)(2,1)}, bf16[1536,1,256]{2,0,1:T(8,128)(2,1)S(1)}, u32[]{:S(2)}) copy-start(bf16[1536,1,256]{2,0,1:T(8,128)(2,1)S(1)} %maximum_maximum_fusion) | copy-start | bytes 2359300
  135.6 3.7 %copy-start.6 = (pred[512,1536]{0,1:T(8,128)(4,1)S(1)}, pred[512,1536]{0,1:T(8,128)(4,1)}, u32[]{:S(2)}) copy-start(pred[512,1536]{0,1:T(8,128)(4,1)} %compare_and_fusion) | copy-start | bytes 2359300
  144.9 13.5 %copy-start.8 = (f32[128]{0:T(128)S(1)}, f32[128]{0:T(128)}, u32[]{:S(2)}) copy-start(f32[128]{0:T(128)} %param.11) | copy-start | bytes 1540
  154.1 45.5 %all-to-all-start.1 = ((bf16[16,2,4096]{2,1,0:T(2,128)(2,1)}), bf16[16,2,4096]{2,1,0:T(2,128)(2,1)S(1)}, u32[]{:S(2)}, u32[]{:S(2)}) async-start(bf16[16,2,4096]{2,1,0:T(2,128)(2,1)} %reshape.272), calls=%async_computation.1 | async-start | bytes 524288 | tf_op jit(solution)/shard_map/all_to_all | solution.py:143
  158.4 12.1 %copy-start.3 = (f32[512,1,2,128]{0,3,2,1:T(8,128)S(1)}, f32[512,1,2,128]{0,3,2,1:T(8,128)}, u32[]{:S(2)}) copy-start(f32[512,1,2,128]{0,3,2,1:T(8,128)} %copy.187) | copy-start | bytes 1572868
  158.4 12.1 %copy-start.5 = (bf16[1536,1,256]{2,0,1:T(8,128)(2,1)S(1)}, bf16[1536,1,256]{2,0,1:T(8,128)(2,1)}, u32[]{:S(2)}) copy-start(bf16[1536,1,256]{2,0,1:T(8,128)(2,1)} %copy-done.4) | copy-start | bytes 2359300
  158.4 25.8 %copy-start.9 = (f32[128]{0:T(128)S(1)}, f32[128]{0:T(128)}, u32[]{:S(2)}) copy-start(f32[128]{0:T(128)} %param.12) | copy-start | bytes 1540
  160.6 10.5 %copy-start.1 = (f32[1536,1,128]{2,0,1:T(8,128)}, f32[1536,1,128]{2,0,1:T(8,128)S(1)}, u32[]{:S(2)}) copy-start(f32[1536,1,128]{2,0,1:T(8,128)S(1)} %convolution_bitcast_fusion) | copy-start | bytes 2359300
  162.8 9.3 %collective-permute-start.2 = (bf16[512,1,256]{2,0,1:T(8,128)(2,1)}, bf16[512,1,256]{2,0,1:T(8,128)(2,1)}, u32[]{:S(2)}, u32[]{:S(2)}) collective-permute-start(bf16[512,1,256]{2,0,1:T(8,128)(2,1)} %get-tuple-element.4), channel_id=1, source_target_pairs={{16,0},{32,16},{48,32},{64,48},{80,64},{96,80},{112,96},{128,112},... | collective-permute-start | bytes 786440 | tf_op jit(solution)/shard_map/ppermute | solution.py:18
  168.5 15.7 %collective-permute-start.3 = (bf16[512,1,256]{2,0,1:T(8,128)(2,1)}, bf16[512,1,256]{2,0,1:T(8,128)(2,1)}, u32[]{:S(2)}, u32[]{:S(2)}) collective-permute-start(bf16[512,1,256]{2,0,1:T(8,128)(2,1)} %get-tuple-element.5), channel_id=1, source_target_pairs={{32,0},{48,16},{64,32},{80,48},{96,64},{112,80},{128,96},{144,112}... | collective-permute-start | bytes 786440 | tf_op jit(solution)/shard_map/ppermute | solution.py:18
  199.6 77.9 %all-to-all-start.2 = ((bf16[16,2,8192]{2,1,0:T(2,128)(2,1)}), bf16[16,2,8192]{2,1,0:T(2,128)(2,1)S(1)}, u32[]{:S(2)}, u32[]{:S(2)}) async-start(bf16[16,2,8192]{2,1,0:T(2,128)(2,1)} %reshape.274), calls=%async_computation.2 | async-start | bytes 1048576 | tf_op jit(solution)/shard_map/all_to_all | solution.py:150

commit v5 on v2

--- a/solution.py
+++ b/solution.py
@@ -2,6 +2,8 @@
 import jax.numpy as jnp
 from jax import lax
 from jax.sharding import PartitionSpec as P
+from jax.experimental import pallas as pl
+from jax.experimental.pallas import tpu as pltpu
 
 HEAD_WIDTH = 128
 REACH = 2
@@ -10,6 +12,139 @@
 CAP_VALUE = 50.0
 QUERY_SCALE = 144.0 ** (-0.5)
 EPSILON = 1e-06
+TILE = 128
+INTERPRET = False
+
+
+def attention_kernel(
+    live_ref, query_ref, key_ref, value_ref, grad_ref, query_doc_ref, key_doc_ref,
+    attended_ref, dquery_ref, dkey_ref, dvalue_ref,
+):
+    query_tiles = query_ref.shape[0] // TILE
+    key_tiles = key_ref.shape[0] // TILE
+    reach_rows = key_ref.shape[0] - query_ref.shape[0]
+    dkey_ref[...] = jnp.zeros_like(dkey_ref)
+    dvalue_ref[...] = jnp.zeros_like(dvalue_ref)
+    query_iota = lax.broadcasted_iota(jnp.int32, (TILE, TILE), 0)
+    key_iota = lax.broadcasted_iota(jnp.int32, (TILE, TILE), 1)
+
+    def tile_scores(q_start, k_start, query_tile, query_docs):
+        key_tile = key_ref[pl.ds(k_start, TILE), :]
+        raw = lax.dot_general(
+            query_tile, key_tile, (((1,), (1,)), ((), ())), preferred_element_type=jnp.float32
+        )
+        scores = CAP_VALUE * jnp.tanh(raw / CAP_VALUE)
+        key_docs = key_doc_ref[:, pl.ds(k_start, TILE)]
+        allowed = (query_docs == key_docs) & (
+            k_start + key_iota <= q_start + reach_rows + query_iota
+        )
+        return key_tile, scores, allowed
+
+    for head in range(query_ref.shape[1] // HEAD_WIDTH):
+        columns = pl.ds(head * HEAD_WIDTH, HEAD_WIDTH)
+
+        def query_step(i, carry):
+            q_start = pl.multiple_of(i * TILE, TILE)
+            query_tile = query_ref[pl.ds(q_start, TILE), columns]
+            grad_tile = grad_ref[pl.ds(q_start, TILE), columns]
+            query_docs = query_doc_ref[pl.ds(q_start, TILE), :]
+
+            def forward_step(j, acc):
+                k_start = pl.multiple_of(j * TILE, TILE)
+
+                def work(acc):
+                    _, scores, allowed = tile_scores(q_start, k_start, query_tile, query_docs)
+                    weights = jnp.where(allowed, jnp.exp(scores), 0.0)
+                    value_tile = value_ref[pl.ds(k_start, TILE), :]
+                    mixed = jnp.dot(
+                        weights.astype(jnp.bfloat16), value_tile, preferred_element_type=jnp.float32
+                    )
+                    return (acc[0] + jnp.sum(weights, axis=1, keepdims=True), acc[1] + mixed)
+
+                return lax.cond(live_ref[i, j] > 0, work, lambda acc: acc, acc)
+
+            weight_sum, mixed_sum = lax.fori_loop(
+                0,
+                key_tiles,
+                forward_step,
+                (jnp.zeros((TILE, 1), jnp.float32), jnp.zeros((TILE, HEAD_WIDTH), jnp.float32)),
+            )
+            attended = (mixed_sum / weight_sum).astype(jnp.bfloat16)
+            attended_ref[pl.ds(q_start, TILE), columns] = attended
+            log_total = jnp.log(weight_sum)
+            row_inner = jnp.sum(
+                grad_tile.astype(jnp.float32) * attended.astype(jnp.float32), axis=1, keepdims=True
+            )
+
+            def backward_step(j, dquery):
+                k_start = pl.multiple_of(j * TILE, TILE)
+
+                def work(dquery):
+                    key_tile, scores, allowed = tile_scores(q_start, k_start, query_tile, query_docs)
+                    value_tile = value_ref[pl.ds(k_start, TILE), :]
+                    prob = jnp.where(allowed, jnp.exp(scores - log_total), 0.0)
+                    dprob = lax.dot_general(
+                        grad_tile, value_tile, (((1,), (1,)), ((), ())),
+                        preferred_element_type=jnp.float32,
+                    )
+                    dscore = (
+                        prob * (dprob - row_inner) * (1.0 - (scores / CAP_VALUE) ** 2)
+                    ).astype(jnp.bfloat16)
+                    rows = pl.ds(k_start, TILE)
+                    dkey_ref[rows, :] += lax.dot_general(
+                        dscore, query_tile, (((0,), (0,)), ((), ())),
+                        preferred_element_type=jnp.float32,
+                    )
+                    dvalue_ref[rows, :] += lax.dot_general(
+                        prob.astype(jnp.bfloat16), grad_tile, (((0,), (0,)), ((), ())),
+                        preferred_element_type=jnp.float32,
+                    )
+                    return dquery + jnp.dot(dscore, key_tile, preferred_element_type=jnp.float32)
+
+                return lax.cond(live_ref[i, j] > 0, work, lambda d: d, dquery)
+
+            dquery = lax.fori_loop(
+                0, key_tiles, backward_step, jnp.zeros((TILE, HEAD_WIDTH), jnp.float32)
+            )
+            dquery_ref[pl.ds(q_start, TILE), columns] = dquery
+            return carry
+
+        lax.fori_loop(0, query_tiles, query_step, 0)
+
+
+def fused_attention(query_norm, key_window, value_window, grad_rows, query_docs, key_docs):
+    rows, width = query_norm.shape
+    window_rows = key_window.shape[0]
+    query_span = query_docs.reshape(rows // TILE, TILE)
+    key_span = key_docs.reshape(window_rows // TILE, TILE)
+    reach_tiles = (window_rows - rows) // TILE
+    tile_gap = jnp.arange(window_rows // TILE)[None, :] - jnp.arange(rows // TILE)[:, None]
+    live = (
+        (key_span[None, :, -1] >= query_span[:, None, 0])
+        & (key_span[None, :, 0] <= query_span[:, None, -1])
+        & (tile_gap <= reach_tiles)
+    ).astype(jnp.int32)
+    vmem = pl.BlockSpec(memory_space=pltpu.VMEM)
+    return pl.pallas_call(
+        attention_kernel,
+        out_shape=(
+            jax.ShapeDtypeStruct((rows, width), jnp.bfloat16),
+            jax.ShapeDtypeStruct((rows, width), jnp.float32),
+            jax.ShapeDtypeStruct((window_rows, HEAD_WIDTH), jnp.float32),
+            jax.ShapeDtypeStruct((window_rows, HEAD_WIDTH), jnp.float32),
+        ),
+        in_specs=[pl.BlockSpec(memory_space=pltpu.SMEM)] + [vmem] * 6,
+        out_specs=(vmem, vmem, vmem, vmem),
+        interpret=INTERPRET,
+    )(
+        live,
+        query_norm,
+        key_window,
+        value_window,
+        grad_rows,
+        query_docs.reshape(rows, 1),
+        key_docs.reshape(1, window_rows),
+    )
 
 
 def passed_along(block, axis, distance):
@@ -93,38 +228,18 @@
         [jnp.full((REACH * row_count,), -1, jnp.int32), doc_ids.astype(jnp.int32)]
     )
     key_docs = lax.dynamic_slice_in_dim(padded_docs, row_start, window_rows, 0)
-    scores, allowed = capped(query_norm, key_window, query_docs, key_docs, query_pos, key_pos)
-    weights = jnp.where(allowed, jnp.exp(scores), 0.0)
-    weight_sum = jnp.sum(weights, axis=-1)
-    mixed_sum = jnp.einsum(
-        "hgqk,khe->qhge",
-        weights.astype(jnp.bfloat16),
-        value_window,
-        preferred_element_type=jnp.float32,
-    )
-    attended = (mixed_sum / jnp.transpose(weight_sum, (2, 0, 1))[..., None]).astype(jnp.bfloat16)
-    log_total = jnp.log(weight_sum)
-    row_inner = jnp.transpose(
-        jnp.sum(gradient_rows.astype(jnp.float32) * attended.astype(jnp.float32), axis=-1),
-        (1, 2, 0),
-    )
-    prob_block = jnp.where(allowed, jnp.exp(scores - log_total[..., None]), 0.0)
-    dprob = jnp.einsum(
-        "qhge,khe->hgqk", gradient_rows, value_window, preferred_element_type=jnp.float32
-    )
-    dscore = (
-        prob_block * (dprob - row_inner[..., None]) * (1.0 - (scores / CAP_VALUE) ** 2)
-    ).astype(jnp.bfloat16)
-    prob_low = prob_block.astype(jnp.bfloat16)
-    query_total_sum = jnp.einsum(
-        "hgqk,khe->qhge", dscore, key_window, preferred_element_type=jnp.float32
-    )
-    key_part = jnp.einsum(
-        "hgqk,qhge->khe", dscore, query_norm, preferred_element_type=jnp.float32
-    )
-    value_part = jnp.einsum(
-        "hgqk,qhge->khe", prob_low, gradient_rows, preferred_element_type=jnp.float32
-    )
+    attended, dquery, key_part, value_part = fused_attention(
+        query_norm.reshape(row_count, -1),
+        key_window.reshape(window_rows, HEAD_WIDTH),
+        value_window.reshape(window_rows, HEAD_WIDTH),
+        gradient_rows.reshape(row_count, -1),
+        query_docs.astype(jnp.int32),
+        key_docs,
+    )
+    attended = attended.reshape(row_count, kv_heads, group_width, HEAD_WIDTH)
+    query_total_sum = dquery.reshape(row_count, kv_heads, group_width, HEAD_WIDTH)
+    key_part = key_part.reshape(window_rows, kv_heads, HEAD_WIDTH)
+    value_part = value_part.reshape(window_rows, kv_heads, HEAD_WIDTH)
     key_total = key_part[REACH * row_count :]
     value_total = value_part[REACH * row_count :]
     grad_parts = jnp.concatenate([key_part, value_part], axis=-1)

time: 267 us -> 291 us (1.090)
  the two profiles are of different devices: /device:TPU:57 before, /device:TPU:97 now
where the time goes in v5:
time: 291 us; the launch traced here: 290 us
  blocking collectives  95.1 us (33%)
  waiting for transfers between devices  81 us (28%)
  starting transfers between devices  55.3 us (19%)
  Pallas kernels  38.1 us (13%)
  local copies, waits for them, and re-layouts  13 us (4%)
  other arithmetic  6.8 us (2%)
    all_to_all x1, blocking collectives, on_device(): lax.all_to_all(leaving.reshape(row_count, 1, -1), 'head', split_axis=0, c...  95.1 us
    all_to_all x1, waiting for transfers between devices, on_device(): lax.all_to_all(packed, 'head', split_axis=1, concat_axis=0, tiled=True)  73.7 us
    pallas_call x1, Pallas kernels, fused_attention(): pl.pallas_call(attention_kernel, out_shape=(jax.ShapeDtypeStruct((rows, w...  38.1 us
    all_to_all x1, starting transfers between devices, on_device(): lax.all_to_all(packed, 'head', split_axis=1, concat_axis=0, tiled=True)  28.1 us
    ppermute x4, starting transfers between devices, passed_along(): return lax.ppermute(block, axis, route)  27.2 us
    ppermute x4, waiting for transfers between devices, passed_along(): return lax.ppermute(block, axis, route)  7.31 us
  transfers between devices with their start and end apart: 5, of which 4 were waited for; matrix products, arithmetic and copies ran while one was open for 2% of the time, Pallas kernels for 0%

profile of v5, /device:TPU:97, one launch (start us, length us, event | category | flops | bytes accessed | tf_op | source)
XLA Modules:
  0.0 290.1 jit_solution(7400840860837222356)
XLA Ops:
  0.6 1.1 copy_bitcast_fusion
  1.8 1.0 copy_bitcast_fusion.4
  2.8 1.0 pad_maximum_fusion
  3.7 28.1 %all-to-all-start = ((bf16[32,16,768]{2,0,1:T(8,128)(2,1)}), bf16[32,16,768]{2,0,1:T(8,128)(2,1)S(1)}, u32[]{:S(2)}, u32[]{:S(2)}) async-start(bf16[32,16,768]{2,0,1:T(8,128)(2,1)} %pad_maximum_fusion), calls=%async_computation | async-start | bytes 1572864 | tf_op jit(solution)/shard_map/all_to_all | solution.py:195
  31.8 0.1 dynamic_slice.7
  31.9 0.9 copy.57.query_doc_ref
  32.8 0.1 pad_dynamic-slice_fusion
  32.8 0.6 reshape.215.key_doc_ref
  33.4 0.1 dynamic-slice_bitcast_fusion
  33.5 0.2 slice_reduce_fusion.3
  33.7 0.1 fusion.25
  33.8 0.2 slice_reduce_fusion.1
  34.0 0.7 fusion.23.live_ref
  34.6 73.7 %all-to-all-done = bf16[32,16,768]{2,0,1:T(8,128)(2,1)S(1)} async-done(((bf16[32,16,768]{2,0,1:T(8,128)(2,1)}), bf16[32,16,768]{2,0,1:T(8,128)(2,1)S(1)}, u32[]{:S(2)}, u32[]{:S(2)}) %all-to-all-start) | async-done | bytes 786464 | tf_op jit(solution)/shard_map/all_to_all | solution.py:195
  108.3 0.1 fusion.12
  108.5 0.1 fusion.21
  108.7 3.2 %collective-permute-start = (bf16[512,1,256]{2,0,1:T(8,128)(2,1)S(1)}, bf16[512,1,256]{2,0,1:T(8,128)(2,1)S(1)}, u32[]{:S(2)}, u32[]{:S(2)}) collective-permute-start(bf16[512,1,256]{2,0,1:T(8,128)(2,1)S(1)} %pad_maximum_fusion.2), channel_id=1, source_target_pairs={{0,32},{16,48},{32,64},{48,80},{64,96},{80,112},{96,128},{112,144}... | collective-permute-start | bytes 786440 | tf_op jit(solution)/shard_map/ppermute | solution.py:153
  111.9 16.8 %collective-permute-start.1 = (bf16[512,1,256]{2,0,1:T(8,128)(2,1)S(1)}, bf16[512,1,256]{2,0,1:T(8,128)(2,1)S(1)}, u32[]{:S(2)}, u32[]{:S(2)}) collective-permute-start(bf16[512,1,256]{2,0,1:T(8,128)(2,1)S(1)} %pad_maximum_fusion.2), channel_id=1, source_target_pairs={{0,16},{16,32},{32,48},{48,64},{64,80},{80,96},{96,112},{112,128},... | collective-permute-start | bytes 786440 | tf_op jit(solution)/shard_map/ppermute | solution.py:153
  128.7 0.8 fusion.24
  129.4 0.3 reshape.210
  129.7 0.6 multiply_reduce_fusion.1
  130.4 0.6 mul.196
  131.0 0.8 multiply_convert_fusion.query_ref
  131.8 0.2 collective-permute-done.1
  132.0 1.0 slice_bitcast_fusion
  133.0 38.1 %shard_map.102 = (bf16[512,256]{1,0:T(8,128)(2,1)}, f32[512,256]{1,0:T(8,128)}, f32[1536,128]{1,0:T(8,128)}, f32[1536,128]{1,0:T(8,128)}) custom-call(s32[4,12]{1,0:T(4,128)} %fusion.23.live_ref, bf16[512,256]{1,0:T(8,128)(2,1)} %multiply_convert_fusion.query_ref, bf16[1536,128]{1,0:T(8,128)(2,1)} %get-tuple-element.25.key_ref, ...), custom_call_target="tpu_custom_call" | custom-call | tf_op jit(solution)/shard_map/pallas_call | solution.py:128
  171.1 1.4 reshape.216
  172.5 0.6 multiply_reduce_fusion
  173.2 0.4 copy-done.3
  173.7 5.3 %collective-permute-start.2 = (bf16[512,1,256]{2,0,1:T(8,128)(2,1)S(1)}, bf16[512,1,256]{2,0,1:T(8,128)(2,1)S(1)}, u32[]{:S(2)}, u32[]{:S(2)}) collective-permute-start(bf16[512,1,256]{2,0,1:T(8,128)(2,1)S(1)} %get-tuple-element.16), channel_id=1, source_target_pairs={{16,0},{32,16},{48,32},{64,48},{80,64},{96,80},{112,96},{128,112},... | collective-permute-start | bytes 786440 | tf_op jit(solution)/shard_map/ppermute | solution.py:153
  179.0 1.9 collective-permute-start.3
  180.9 0.6 mul.216
  181.5 0.2 fusion.2
  181.7 0.4 collective-permute-done.2
  182.1 6.7 %collective-permute-done.3 = bf16[512,1,256]{2,0,1:T(8,128)(2,1)S(1)} collective-permute-done((bf16[512,1,256]{2,0,1:T(8,128)(2,1)S(1)}, bf16[512,1,256]{2,0,1:T(8,128)(2,1)S(1)}, u32[]{:S(2)}, u32[]{:S(2)}) %collective-permute-start.3) | collective-permute-done | bytes 262176 | tf_op jit(solution)/shard_map/ppermute | solution.py:153
  188.8 0.2 fusion.14
  189.0 0.3 fusion.20
  189.3 0.1 maximum_bitcast_fusion
  189.3 0.5 broadcast.116
  189.9 1.2 reduce.13
  191.1 0.2 reshape.231
  191.3 95.1 %all_to_all.33 = bf16[16,2,12288]{2,1,0:T(2,128)(2,1)S(1)} all-to-all(bf16[16,2,12288]{2,1,0:T(2,128)(2,1)S(1)} %reshape.231), channel_id=1, replica_groups=mesh['ctx'=64,'head'=16] {'head'}, dimensions={0} | all-to-all | bytes 1572864 | tf_op jit(solution)/shard_map/all_to_all | solution.py:265
  286.3 0.7 reshape.232
  287.1 0.1 copy.63
  287.3 0.7 copy.68
  288.1 0.7 copy.69
  288.8 0.7 copy.83
  289.5 0.7 copy.84
  (27 shorter events, 0.4 us)
Async XLA Ops:
  0.6 1.1 copy-start
  2.7 29.1 %copy-start.4 = (s32[32768]{0:T(1024)S(1)}, s32[32768]{0:T(1024)}, u32[]{:S(2)}) copy-start(s32[32768]{0:T(1024)} %param.13) | copy-start | bytes 393220
  2.8 31.2 %copy-start.7 = (f32[128]{0:T(128)S(1)}, f32[128]{0:T(128)}, u32[]{:S(2)}) copy-start(f32[128]{0:T(128)} %param.11) | copy-start | bytes 1540
  3.7 104.8 %copy-start.6 = (f32[128]{0:T(128)S(1)}, f32[128]{0:T(128)}, u32[]{:S(2)}) copy-start(f32[128]{0:T(128)} %param.12) | copy-start | bytes 1540
  3.7 104.6 %all-to-all-start = ((bf16[32,16,768]{2,0,1:T(8,128)(2,1)}), bf16[32,16,768]{2,0,1:T(8,128)(2,1)S(1)}, u32[]{:S(2)}, u32[]{:S(2)}) async-start(bf16[32,16,768]{2,0,1:T(8,128)(2,1)} %pad_maximum_fusion), calls=%async_computation | async-start | bytes 1572864 | tf_op jit(solution)/shard_map/all_to_all | solution.py:195
  108.7 23.1 %collective-permute-start = (bf16[512,1,256]{2,0,1:T(8,128)(2,1)S(1)}, bf16[512,1,256]{2,0,1:T(8,128)(2,1)S(1)}, u32[]{:S(2)}, u32[]{:S(2)}) collective-permute-start(bf16[512,1,256]{2,0,1:T(8,128)(2,1)S(1)} %pad_maximum_fusion.2), channel_id=1, source_target_pairs={{0,32},{16,48},{32,64},{48,80},{64,96},{80,112},{96,128},{112,144}... | collective-permute-start | bytes 786440 | tf_op jit(solution)/shard_map/ppermute | solution.py:153
  111.9 20.1 %collective-permute-start.1 = (bf16[512,1,256]{2,0,1:T(8,128)(2,1)S(1)}, bf16[512,1,256]{2,0,1:T(8,128)(2,1)S(1)}, u32[]{:S(2)}, u32[]{:S(2)}) collective-permute-start(bf16[512,1,256]{2,0,1:T(8,128)(2,1)S(1)} %pad_maximum_fusion.2), channel_id=1, source_target_pairs={{0,16},{16,32},{32,48},{48,64},{64,80},{80,96},{96,112},{112,128},... | collective-permute-start | bytes 786440 | tf_op jit(solution)/shard_map/ppermute | solution.py:153
  171.1 2.1 copy-start.1
  172.5 1.1 copy-start.3
  173.1 8.4 %copy-start.2 = (f32[512,256]{1,0:T(8,128)S(1)}, f32[512,256]{1,0:T(8,128)}, u32[]{:S(2)}) copy-start(f32[512,256]{1,0:T(8,128)} %get-tuple-element.9) | copy-start | bytes 1572868
  173.7 8.4 %collective-permute-start.2 = (bf16[512,1,256]{2,0,1:T(8,128)(2,1)S(1)}, bf16[512,1,256]{2,0,1:T(8,128)(2,1)S(1)}, u32[]{:S(2)}, u32[]{:S(2)}) collective-permute-start(bf16[512,1,256]{2,0,1:T(8,128)(2,1)S(1)} %get-tuple-element.16), channel_id=1, source_target_pairs={{16,0},{32,16},{48,32},{64,48},{80,64},{96,80},{112,96},{128,112},... | collective-permute-start | bytes 786440 | tf_op jit(solution)/shard_map/ppermute | solution.py:153
  179.0 9.8 %collective-permute-start.3 = (bf16[512,1,256]{2,0,1:T(8,128)(2,1)S(1)}, bf16[512,1,256]{2,0,1:T(8,128)(2,1)S(1)}, u32[]{:S(2)}, u32[]{:S(2)}) collective-permute-start(bf16[512,1,256]{2,0,1:T(8,128)(2,1)S(1)} %get-tuple-element.17), channel_id=1, source_target_pairs={{32,0},{48,16},{64,32},{80,48},{96,64},{112,80},{128,96},{144,112}... | collective-permute-start | bytes 786440 | tf_op jit(solution)/shard_map/ppermute | solution.py:153
  181.7 7.6 %copy-start.5 = (bf16[512,256]{1,0:T(8,128)(2,1)S(1)}, bf16[512,256]{1,0:T(8,128)(2,1)}, u32[]{:S(2)}) copy-start(bf16[512,256]{1,0:T(8,128)(2,1)} %get-tuple-element.8) | copy-start | bytes 786436

commit v6 on v2

--- a/solution.py
+++ b/solution.py
@@ -52,12 +52,12 @@
     token_rows, head_devices = query_matrix.shape[0], lax.axis_size("head")
     packed = jnp.concatenate(
         [
-            part.reshape(token_rows, head_devices, -1)
+            jnp.swapaxes(part.reshape(token_rows, head_devices, -1), 0, 1)
             for part in (query_matrix, key_matrix, value_matrix, output_gradient)
         ],
         axis=-1,
     )
-    arrived = lax.all_to_all(packed, "head", split_axis=1, concat_axis=0, tiled=True)
+    arrived = lax.all_to_all(packed, "head", split_axis=0, concat_axis=0, tiled=True)
     arrived = arrived.reshape(token_rows * head_devices, -1)
     widths = [query_matrix.shape[1] // head_devices, key_matrix.shape[1] // head_devices]
     cuts = [widths[0], widths[0] + widths[1], widths[0] + 2 * widths[1]]
@@ -148,8 +148,9 @@
         axis=-1,
     )
     home = lax.all_to_all(
-        leaving.reshape(row_count, 1, -1), "head", split_axis=0, concat_axis=1, tiled=True
+        leaving.reshape(head_devices, token_rows, -1), "head", split_axis=0, concat_axis=0, tiled=True
     )
+    home = jnp.swapaxes(home, 0, 1)
     return (
         home[:, :, : cuts[0]].reshape(token_rows, -1),
         home[:, :, cuts[0] : 2 * cuts[0]].reshape(token_rows, -1),

time: 267 us -> 265 us (level)
    reshape x5 -> x0, local copies, waits for them, and re-layouts: 3.8 us -> none  [the longest x2 2.07 us: on_device(): part.reshape(token_rows, head_devices, -1)]
where the time goes in v6:
time: 265 us; the launch traced here: 264 us
  waiting for transfers between devices  94 us (35%)
  blocking collectives  92.9 us (35%)
  starting transfers between devices  40.4 us (15%)
  matrix products  13.5 us (5%)
  local copies, waits for them, and re-layouts  11.2 us (4%)
  other arithmetic  11.2 us (4%)
    all_to_all x1, blocking collectives, on_device(): lax.all_to_all(leaving.reshape(head_devices, token_rows, -1), 'head', spl...  92.9 us
    all_to_all x1, waiting for transfers between devices, on_device(): lax.all_to_all(packed, 'head', split_axis=0, concat_axis=0, tiled=True)  83.2 us
    all_to_all x1, starting transfers between devices, on_device(): lax.all_to_all(packed, 'head', split_axis=0, concat_axis=0, tiled=True)  29.7 us
    ppermute x4, waiting for transfers between devices, passed_along(): return lax.ppermute(block, axis, route)  10.7 us
    ppermute x4, starting transfers between devices, passed_along(): return lax.ppermute(block, axis, route)  10.7 us
  transfers between devices with their start and end apart: 5, of which 4 were waited for; matrix products, arithmetic and copies ran while one was open for 4% of the time, Pallas kernels for 0%

profile of v6, /device:TPU:57, one launch (start us, length us, event | category | flops | bytes accessed | tf_op | source)
XLA Modules:
  0.0 264.0 jit_solution(10851055089418015263)
XLA Ops:
  0.6 1.1 bitcast_bitcast_fusion
  1.8 1.0 bitcast_bitcast_fusion.2
  2.7 1.0 pad_maximum_fusion
  3.7 29.7 %all-to-all-start = ((bf16[16,32,768]{2,1,0:T(8,128)(2,1)}), bf16[16,32,768]{2,1,0:T(8,128)(2,1)S(1)}, u32[]{:S(2)}, u32[]{:S(2)}) async-start(bf16[16,32,768]{2,1,0:T(8,128)(2,1)} %pad_maximum_fusion), calls=%async_computation | async-start | bytes 1572864 | tf_op jit(solution)/shard_map/all_to_all | solution.py:60
  33.4 0.8 dynamic_slice.6
  34.2 0.8 pad_dynamic-slice_fusion
  35.0 0.7 broadcast_bitcast_fusion
  35.6 1.9 compare_and_fusion
  37.5 83.2 %all-to-all-done = bf16[16,32,768]{2,1,0:T(8,128)(2,1)S(1)} async-done(((bf16[16,32,768]{2,1,0:T(8,128)(2,1)}), bf16[16,32,768]{2,1,0:T(8,128)(2,1)S(1)}, u32[]{:S(2)}, u32[]{:S(2)}) %all-to-all-start) | async-done | bytes 786464 | tf_op jit(solution)/shard_map/all_to_all | solution.py:60
  120.7 0.1 fusion.42
  120.9 0.8 fusion.55
  121.7 0.7 pad_maximum_fusion.3
  122.4 1.9 collective-permute-start
  124.4 1.9 collective-permute-start.1
  126.3 0.1 slice_convert_fusion.1
  126.4 0.3 reshape.243
  126.7 1.3 multiply_reduce_fusion.2
  128.0 0.2 copy.157
  128.2 0.2 copy.182
  128.4 1.1 copy.147
  129.5 1.0 copy.179
  130.6 0.2 copy.181
  130.8 0.1 copy.185
  130.9 2.7 %collective-permute-done.1 = bf16[512,1,256]{2,0,1:T(8,128)(2,1)} collective-permute-done((bf16[512,1,256]{2,0,1:T(8,128)(2,1)}, bf16[512,1,256]{2,0,1:T(8,128)(2,1)}, u32[]{:S(2)}, u32[]{:S(2)}) %collective-permute-start.1) | collective-permute-done | bytes 262176 | tf_op jit(solution)/shard_map/ppermute | solution.py:18
  133.6 1.1 maximum_maximum_fusion
  134.7 3.6 %fusion.6 = (f32[2,512]{1,0:T(2,128)S(1)}, f32[1536,512,2]{1,0,2:T(8,128)S(1)}) fusion(pred[512,1536]{0,1:T(8,128)(4,1)} %compare_and_fusion, bf16[1536,1,256]{2,0,1:T(8,128)(2,1)S(1)} %maximum_maximum_fusion, f32[512,256]{1,0:T(8,128)} %copy.179, f32[256]{0:T(256)S(1)} %broadcast_bitcast_fusion, bf16[512,768]{1,0:T(8,128)(2,1)S(1)} %bitcast.220), kind=kOutput, calls=%fused_computation.11 | convolution fusion | flops 409598976 | bytes 8262656 | tf_op jit(solution)/shard_map/qhge,khe->hgqk/dot_general | solution.py:41
  138.4 2.9 %multiply_reduce_fusion.1 = (f32[512,2]{0,1:T(2,128)S(1)}, bf16[512,1,2,128]{0,3,2,1:T(8,128)(2,1)}) fusion(f32[512,1,2,128]{0,3,2,1:T(8,128)S(1)} %bitcast.227, f32[512,2]{0,1:T(2,128)S(1)} %bitcast.238, f32[1536,512,2]{1,0,2:T(8,128)S(1)} %get-tuple-element.16, pred[512,1536]{0,1:T(8,128)(4,1)S(1)} %copy-done.1, ...), kind=kOutput, calls=%fused_computation.39 | convolution fusion | flops 409598976 | bytes 8265728 | tf_op jit(solution)/shard_map/hgqk,khe->qhge/dot_general | solution.py:99
  141.2 1.8 fusion.17
  143.1 3.5 %fusion.8 = bf16[2,512,1536]{1,2,0:T(8,128)(2,1)S(1)} fusion(bf16[512,2,128]{0,2,1:T(8,128)(2,1)S(1)} %bitcast.231, f32[1536,512,2]{1,0,2:T(8,128)S(1)} %get-tuple-element.16, f32[2,512]{1,0:T(2,128)S(1)} %bitcast.239, f32[2,512]{1,0:T(2,128)S(1)} %log.9, pred[512,1536]{0,1:T(8,128)(4,1)S(1)} %copy-done.1, bf16[1536,1,256]{2,0,1:T(8,128)(2,1)S(1)} %maximum_maximum_fusion), kind=kOutput, calls=%fused_computation.13 | convolution fusion | flops 418381824 | bytes 10887168 | tf_op jit(solution)/shard_map/qhge,khe->hgqk/dot_general | solution.py:112
  146.6 0.6 multiply_reduce_fusion
  147.2 1.1 convolution_bitcast_fusion
  148.3 0.8 maximum_convert_fusion
  149.1 4.5 %collective-permute-start.2 = (bf16[512,1,256]{2,0,1:T(8,128)(2,1)}, bf16[512,1,256]{2,0,1:T(8,128)(2,1)S(1)}, u32[]{:S(2)}, u32[]{:S(2)}) collective-permute-start(bf16[512,1,256]{2,0,1:T(8,128)(2,1)} %get-tuple-element.4), channel_id=1, source_target_pairs={{16,0},{32,16},{48,32},{64,48},{80,64},{96,80},{112,96},{128,112},... | collective-permute-start | bytes 786440 | tf_op jit(solution)/shard_map/ppermute | solution.py:18
  153.6 2.4 collective-permute-start.3
  156.0 0.1 multiply_convert_fusion.1
  156.1 0.2 copy.159
  156.3 0.2 concatenate.32
  156.5 1.1 copy.152
  157.6 0.2 concatenate.31
  157.8 2.1 collective-permute-done.2
  159.8 6.0 %collective-permute-done.3 = bf16[512,1,256]{2,0,1:T(8,128)(2,1)} collective-permute-done((bf16[512,1,256]{2,0,1:T(8,128)(2,1)}, bf16[512,1,256]{2,0,1:T(8,128)(2,1)}, u32[]{:S(2)}, u32[]{:S(2)}) %collective-permute-start.3) | collective-permute-done | bytes 262176 | tf_op jit(solution)/shard_map/ppermute | solution.py:18
  165.8 1.1 fusion.44
  166.9 1.2 fusion.41
  168.2 92.9 %all_to_all.10 = bf16[16,32,768]{2,1,0:T(8,128)(2,1)S(1)} all-to-all(bf16[16,32,768]{2,1,0:T(8,128)(2,1)S(1)} %pad_maximum_fusion.1), channel_id=1, replica_groups=mesh['ctx'=64,'head'=16] {'head'}, dimensions={0} | all-to-all | bytes 1572864 | tf_op jit(solution)/shard_map/all_to_all | solution.py:150
  261.2 0.7 copy.191
  261.9 0.7 copy.192
  262.7 0.7 copy.207
  263.3 0.7 copy.208
  (20 shorter events, 0.3 us)
Async XLA Ops:
  0.6 1.1 copy-start
  3.7 117.0 %all-to-all-start = ((bf16[16,32,768]{2,1,0:T(8,128)(2,1)}), bf16[16,32,768]{2,1,0:T(8,128)(2,1)S(1)}, u32[]{:S(2)}, u32[]{:S(2)}) async-start(bf16[16,32,768]{2,1,0:T(8,128)(2,1)} %pad_maximum_fusion), calls=%async_computation | async-start | bytes 1572864 | tf_op jit(solution)/shard_map/all_to_all | solution.py:60
  122.4 8.5 %collective-permute-start = (bf16[512,1,256]{2,0,1:T(8,128)(2,1)}, bf16[512,1,256]{2,0,1:T(8,128)(2,1)}, u32[]{:S(2)}, u32[]{:S(2)}) collective-permute-start(bf16[512,1,256]{2,0,1:T(8,128)(2,1)} %pad_maximum_fusion.3), channel_id=1, source_target_pairs={{0,32},{16,48},{32,64},{48,80},{64,96},{80,112},{96,128},{112,144}... | collective-permute-start | bytes 786440 | tf_op jit(solution)/shard_map/ppermute | solution.py:18
  124.4 9.2 %collective-permute-start.1 = (bf16[512,1,256]{2,0,1:T(8,128)(2,1)}, bf16[512,1,256]{2,0,1:T(8,128)(2,1)}, u32[]{:S(2)}, u32[]{:S(2)}) collective-permute-start(bf16[512,1,256]{2,0,1:T(8,128)(2,1)} %pad_maximum_fusion.3), channel_id=1, source_target_pairs={{0,16},{16,32},{32,48},{48,64},{64,80},{80,96},{96,112},{112,128},... | collective-permute-start | bytes 786440 | tf_op jit(solution)/shard_map/ppermute | solution.py:18
  134.7 3.7 %copy-start.1 = (pred[512,1536]{0,1:T(8,128)(4,1)S(1)}, pred[512,1536]{0,1:T(8,128)(4,1)}, u32[]{:S(2)}) copy-start(pred[512,1536]{0,1:T(8,128)(4,1)} %compare_and_fusion) | copy-start | bytes 2359300
  143.1 3.5 %copy-start.2 = (f32[128]{0:T(128)S(1)}, f32[128]{0:T(128)}, u32[]{:S(2)}) copy-start(f32[128]{0:T(128)} %param.11) | copy-start | bytes 1540
  146.6 19.3 %copy-start.3 = (f32[128]{0:T(128)S(1)}, f32[128]{0:T(128)}, u32[]{:S(2)}) copy-start(f32[128]{0:T(128)} %param.12) | copy-start | bytes 1540
  149.1 10.7 %collective-permute-start.2 = (bf16[512,1,256]{2,0,1:T(8,128)(2,1)}, bf16[512,1,256]{2,0,1:T(8,128)(2,1)S(1)}, u32[]{:S(2)}, u32[]{:S(2)}) collective-permute-start(bf16[512,1,256]{2,0,1:T(8,128)(2,1)} %get-tuple-element.4), channel_id=1, source_target_pairs={{16,0},{32,16},{48,32},{64,48},{80,64},{96,80},{112,96},{128,112},... | collective-permute-start | bytes 786440 | tf_op jit(solution)/shard_map/ppermute | solution.py:18
  153.6 12.2 %collective-permute-start.3 = (bf16[512,1,256]{2,0,1:T(8,128)(2,1)}, bf16[512,1,256]{2,0,1:T(8,128)(2,1)}, u32[]{:S(2)}, u32[]{:S(2)}) collective-permute-start(bf16[512,1,256]{2,0,1:T(8,128)(2,1)} %get-tuple-element.5), channel_id=1, source_target_pairs={{32,0},{48,16},{64,32},{80,48},{96,64},{112,80},{128,96},{144,112}... | collective-permute-start | bytes 786440 | tf_op jit(solution)/shard_map/ppermute | solution.py:18

commit v7 on v6

--- a/solution.py
+++ b/solution.py
@@ -108,7 +108,7 @@
         jnp.sum(gradient_rows.astype(jnp.float32) * attended.astype(jnp.float32), axis=-1),
         (1, 2, 0),
     )
-    prob_block = jnp.where(allowed, jnp.exp(scores - log_total[..., None]), 0.0)
+    prob_block = weights / weight_sum[..., None]
     dprob = jnp.einsum(
         "qhge,khe->hgqk", gradient_rows, value_window, preferred_element_type=jnp.float32
     )

time: 265 us -> 268 us (1.011)
  the two profiles are of different devices: /device:TPU:57 before, /device:TPU:121 now
where the time goes in v7:
time: 268 us; the launch traced here: 267 us
  blocking collectives  96.5 us (36%)
  waiting for transfers between devices  88.3 us (33%)
  starting transfers between devices  44 us (16%)
  matrix products  13.5 us (5%)
  local copies, waits for them, and re-layouts  12.7 us (5%)
  other arithmetic  11.4 us (4%)
    all_to_all x1, blocking collectives, on_device(): lax.all_to_all(leaving.reshape(head_devices, token_rows, -1), 'head', spl...  96.5 us
    all_to_all x1, waiting for transfers between devices, on_device(): lax.all_to_all(packed, 'head', split_axis=0, concat_axis=0, tiled=True)  72.4 us
    all_to_all x1, starting transfers between devices, on_device(): lax.all_to_all(packed, 'head', split_axis=0, concat_axis=0, tiled=True)  27.9 us
    ppermute x4, starting transfers between devices, passed_along(): return lax.ppermute(block, axis, route)  16.1 us
    ppermute x4, waiting for transfers between devices, passed_along(): return lax.ppermute(block, axis, route)  15.9 us
  transfers between devices with their start and end apart: 5, of which 4 were waited for; matrix products, arithmetic and copies ran while one was open for 4% of the time, Pallas kernels for 0%

profile of v7, /device:TPU:121, one launch (start us, length us, event | category | flops | bytes accessed | tf_op | source)
XLA Modules:
  0.0 267.3 jit_solution(15674829229337865618)
XLA Ops:
  0.6 1.1 bitcast_bitcast_fusion
  1.8 1.0 bitcast_bitcast_fusion.2
  2.7 1.0 pad_maximum_fusion
  3.7 27.9 %all-to-all-start = ((bf16[16,32,768]{2,1,0:T(8,128)(2,1)}), bf16[16,32,768]{2,1,0:T(8,128)(2,1)S(1)}, u32[]{:S(2)}, u32[]{:S(2)}) async-start(bf16[16,32,768]{2,1,0:T(8,128)(2,1)} %pad_maximum_fusion), calls=%async_computation | async-start | bytes 1572864 | tf_op jit(solution)/shard_map/all_to_all | solution.py:60
  31.7 0.8 dynamic_slice.6
  32.4 0.8 pad_dynamic-slice_fusion
  33.2 0.7 broadcast_bitcast_fusion
  33.9 1.9 compare_and_fusion
  35.7 72.4 %all-to-all-done = bf16[16,32,768]{2,1,0:T(8,128)(2,1)S(1)} async-done(((bf16[16,32,768]{2,1,0:T(8,128)(2,1)}), bf16[16,32,768]{2,1,0:T(8,128)(2,1)S(1)}, u32[]{:S(2)}, u32[]{:S(2)}) %all-to-all-start) | async-done | bytes 786464 | tf_op jit(solution)/shard_map/all_to_all | solution.py:60
  108.2 0.1 fusion.35
  108.3 0.8 fusion.48
  109.1 0.7 pad_maximum_fusion.3
  109.9 1.9 collective-permute-start
  111.8 3.7 %collective-permute-start.1 = (bf16[512,1,256]{2,0,1:T(8,128)(2,1)}, bf16[512,1,256]{2,0,1:T(8,128)(2,1)}, u32[]{:S(2)}, u32[]{:S(2)}) collective-permute-start(bf16[512,1,256]{2,0,1:T(8,128)(2,1)} %pad_maximum_fusion.3), channel_id=1, source_target_pairs={{0,16},{16,32},{32,48},{48,64},{64,80},{80,96},{96,112},{112,128},... | collective-permute-start | bytes 786440 | tf_op jit(solution)/shard_map/ppermute | solution.py:18
  115.5 0.1 slice_convert_fusion.1
  115.6 0.3 reshape.239
  115.8 1.3 multiply_reduce_fusion.2
  117.2 0.2 copy.157
  117.4 0.2 copy.182
  117.6 1.1 copy.147
  118.7 1.0 copy.179
  119.7 1.0 copy.181
  120.7 0.8 copy.185
  121.6 6.9 %collective-permute-done.1 = bf16[512,1,256]{2,0,1:T(8,128)(2,1)} collective-permute-done((bf16[512,1,256]{2,0,1:T(8,128)(2,1)}, bf16[512,1,256]{2,0,1:T(8,128)(2,1)}, u32[]{:S(2)}, u32[]{:S(2)}) %collective-permute-start.1) | collective-permute-done | bytes 262176 | tf_op jit(solution)/shard_map/ppermute | solution.py:18
  128.5 1.1 maximum_maximum_fusion
  129.6 3.6 %fusion.9 = (f32[2,512]{1,0:T(2,128)S(1)}, f32[1536,512,2]{1,0,2:T(8,128)S(1)}) fusion(pred[512,1536]{0,1:T(8,128)(4,1)} %compare_and_fusion, bf16[1536,1,256]{2,0,1:T(8,128)(2,1)S(1)} %maximum_maximum_fusion, f32[512,256]{1,0:T(8,128)} %copy.179, f32[256]{0:T(256)S(1)} %broadcast_bitcast_fusion, bf16[512,768]{1,0:T(8,128)(2,1)S(1)} %bitcast.209), kind=kOutput, calls=%fused_computation.14 | convolution fusion | flops 409598976 | bytes 8262656 | tf_op jit(solution)/shard_map/qhge,khe->hgqk/dot_general | solution.py:41
  133.3 1.9 fusion.10
  135.2 2.9 %multiply_reduce_fusion.1 = (f32[512,2]{0,1:T(2,128)S(1)}, bf16[512,1,2,128]{0,3,2,1:T(8,128)(2,1)}) fusion(f32[512,1,2,128]{0,3,2,1:T(8,128)S(1)} %bitcast.216, f32[512,2]{0,1:T(2,128)S(1)} %bitcast.227, f32[1536,512,2]{1,0,2:T(8,128)S(1)} %get-tuple-element.16, pred[512,1536]{0,1:T(8,128)(4,1)S(1)} %copy-done.1, ...), kind=kOutput, calls=%fused_computation.34 | convolution fusion | flops 409598976 | bytes 8265728 | tf_op jit(solution)/shard_map/hgqk,khe->qhge/dot_general | solution.py:99
  138.1 3.4 %fusion.2 = bf16[2,512,1536]{1,2,0:T(8,128)(2,1)S(1)} fusion(f32[1536,512,2]{1,0,2:T(8,128)S(1)} %get-tuple-element.16, bf16[512,2,128]{0,2,1:T(8,128)(2,1)S(1)} %bitcast.220, f32[2,512]{1,0:T(2,128)S(1)} %bitcast.228, f32[2,512]{1,0:T(2,128)S(1)} %get-tuple-element.15, pred[512,1536]{0,1:T(8,128)(4,1)S(1)} %copy-done.1, ...), kind=kOutput, calls=%fused_computation.6 | convolution fusion | flops 418381824 | bytes 10887168 | tf_op jit(solution)/shard_map/qhge,khe->hgqk/dot_general | solution.py:112
  141.5 0.6 multiply_reduce_fusion
  142.1 1.1 convolution_bitcast_fusion
  143.2 0.8 maximum_convert_fusion
  144.0 8.1 %collective-permute-start.2 = (bf16[512,1,256]{2,0,1:T(8,128)(2,1)}, bf16[512,1,256]{2,0,1:T(8,128)(2,1)}, u32[]{:S(2)}, u32[]{:S(2)}) collective-permute-start(bf16[512,1,256]{2,0,1:T(8,128)(2,1)} %get-tuple-element.4), channel_id=1, source_target_pairs={{16,0},{32,16},{48,32},{64,48},{80,64},{96,80},{112,96},{128,112},... | collective-permute-start | bytes 786440 | tf_op jit(solution)/shard_map/ppermute | solution.py:18
  152.1 2.4 collective-permute-start.3
  154.5 0.1 multiply_convert_fusion.1
  154.7 0.2 copy.159
  154.8 0.2 concatenate.32
  155.0 1.1 copy.152
  156.1 0.2 concatenate.31
  156.3 0.3 collective-permute-done.2
  156.6 8.7 %collective-permute-done.3 = bf16[512,1,256]{2,0,1:T(8,128)(2,1)} collective-permute-done((bf16[512,1,256]{2,0,1:T(8,128)(2,1)}, bf16[512,1,256]{2,0,1:T(8,128)(2,1)}, u32[]{:S(2)}, u32[]{:S(2)}) %collective-permute-start.3) | collective-permute-done | bytes 262176 | tf_op jit(solution)/shard_map/ppermute | solution.py:18
  165.3 1.1 fusion.37
  166.4 1.4 fusion.34
  167.9 96.5 %all_to_all.10 = bf16[16,32,768]{2,1,0:T(8,128)(2,1)S(1)} all-to-all(bf16[16,32,768]{2,1,0:T(8,128)(2,1)S(1)} %pad_maximum_fusion.1), channel_id=1, replica_groups=mesh['ctx'=64,'head'=16] {'head'}, dimensions={0} | all-to-all | bytes 1572864 | tf_op jit(solution)/shard_map/all_to_all | solution.py:150
  264.5 0.7 copy.191
  265.3 0.7 copy.192
  266.0 0.7 copy.207
  266.7 0.7 copy.208
  (23 shorter events, 0.3 us)
Async XLA Ops:
  0.6 1.1 copy-start
  3.7 104.5 %all-to-all-start = ((bf16[16,32,768]{2,1,0:T(8,128)(2,1)}), bf16[16,32,768]{2,1,0:T(8,128)(2,1)S(1)}, u32[]{:S(2)}, u32[]{:S(2)}) async-start(bf16[16,32,768]{2,1,0:T(8,128)(2,1)} %pad_maximum_fusion), calls=%async_computation | async-start | bytes 1572864 | tf_op jit(solution)/shard_map/all_to_all | solution.py:60
  109.9 11.7 %collective-permute-start = (bf16[512,1,256]{2,0,1:T(8,128)(2,1)}, bf16[512,1,256]{2,0,1:T(8,128)(2,1)}, u32[]{:S(2)}, u32[]{:S(2)}) collective-permute-start(bf16[512,1,256]{2,0,1:T(8,128)(2,1)} %pad_maximum_fusion.3), channel_id=1, source_target_pairs={{0,32},{16,48},{32,64},{48,80},{64,96},{80,112},{96,128},{112,144}... | collective-permute-start | bytes 786440 | tf_op jit(solution)/shard_map/ppermute | solution.py:18
  111.8 16.7 %collective-permute-start.1 = (bf16[512,1,256]{2,0,1:T(8,128)(2,1)}, bf16[512,1,256]{2,0,1:T(8,128)(2,1)}, u32[]{:S(2)}, u32[]{:S(2)}) collective-permute-start(bf16[512,1,256]{2,0,1:T(8,128)(2,1)} %pad_maximum_fusion.3), channel_id=1, source_target_pairs={{0,16},{16,32},{32,48},{48,64},{64,80},{80,96},{96,112},{112,128},... | collective-permute-start | bytes 786440 | tf_op jit(solution)/shard_map/ppermute | solution.py:18
  129.6 3.7 %copy-start.1 = (pred[512,1536]{0,1:T(8,128)(4,1)S(1)}, pred[512,1536]{0,1:T(8,128)(4,1)}, u32[]{:S(2)}) copy-start(pred[512,1536]{0,1:T(8,128)(4,1)} %compare_and_fusion) | copy-start | bytes 2359300
  129.6 3.7 %copy-start.3 = (bf16[512,256]{0,1:T(8,128)(2,1)S(1)}, bf16[512,256]{0,1:T(8,128)(2,1)}, u32[]{:S(2)}) copy-start(bf16[512,256]{0,1:T(8,128)(2,1)} %copy.185) | copy-start | bytes 786436
  133.2 1.9 copy-start.2
  138.1 3.4 %copy-start.4 = (f32[128]{0:T(128)S(1)}, f32[128]{0:T(128)}, u32[]{:S(2)}) copy-start(f32[128]{0:T(128)} %param.11) | copy-start | bytes 1540
  141.5 23.8 %copy-start.5 = (f32[128]{0:T(128)S(1)}, f32[128]{0:T(128)}, u32[]{:S(2)}) copy-start(f32[128]{0:T(128)} %param.12) | copy-start | bytes 1540
  144.0 12.6 %collective-permute-start.2 = (bf16[512,1,256]{2,0,1:T(8,128)(2,1)}, bf16[512,1,256]{2,0,1:T(8,128)(2,1)}, u32[]{:S(2)}, u32[]{:S(2)}) collective-permute-start(bf16[512,1,256]{2,0,1:T(8,128)(2,1)} %get-tuple-element.4), channel_id=1, source_target_pairs={{16,0},{32,16},{48,32},{64,48},{80,64},{96,80},{112,96},{128,112},... | collective-permute-start | bytes 786440 | tf_op jit(solution)/shard_map/ppermute | solution.py:18
  152.1 13.2 %collective-permute-start.3 = (bf16[512,1,256]{2,0,1:T(8,128)(2,1)}, bf16[512,1,256]{2,0,1:T(8,128)(2,1)}, u32[]{:S(2)}, u32[]{:S(2)}) collective-permute-start(bf16[512,1,256]{2,0,1:T(8,128)(2,1)} %get-tuple-element.5), channel_id=1, source_target_pairs={{32,0},{48,16},{64,32},{80,48},{96,64},{112,80},{128,96},{144,112}... | collective-permute-start | bytes 786440 | tf_op jit(solution)/shard_map/ppermute | solution.py:18

commit v8 on v6

--- a/solution.py
+++ b/solution.py
@@ -119,22 +119,34 @@
     query_total_sum = jnp.einsum(
         "hgqk,khe->qhge", dscore, key_window, preferred_element_type=jnp.float32
     )
-    key_part = jnp.einsum(
-        "hgqk,qhge->khe", dscore, query_norm, preferred_element_type=jnp.float32
-    )
-    value_part = jnp.einsum(
-        "hgqk,qhge->khe", prob_low, gradient_rows, preferred_element_type=jnp.float32
-    )
-    key_total = key_part[REACH * row_count :]
-    value_total = value_part[REACH * row_count :]
-    grad_parts = jnp.concatenate([key_part, value_part], axis=-1)
-    for offset in range(1, REACH + 1):
-        first = (REACH - offset) * row_count
-        arrived = passed_along(
-            for_sending(grad_parts[first : first + row_count]), "ctx", -offset
+    reach_rows = REACH * row_count
+
+    def key_side(low, high):
+        key_part = jnp.einsum(
+            "hgqk,qhge->khe", dscore[..., low:high], query_norm, preferred_element_type=jnp.float32
         )
-        key_total = key_total + arrived[..., :HEAD_WIDTH]
-        value_total = value_total + arrived[..., HEAD_WIDTH:]
+        value_part = jnp.einsum(
+            "hgqk,qhge->khe",
+            prob_low[..., low:high],
+            gradient_rows,
+            preferred_element_type=jnp.float32,
+        )
+        return jnp.concatenate([key_part, value_part], axis=-1)
+
+    remote_parts = key_side(0, reach_rows)
+    arrivals = [
+        passed_along(
+            for_sending(remote_parts[(REACH - offset) * row_count : (REACH - offset + 1) * row_count]),
+            "ctx",
+            -offset,
+        )
+        for offset in range(1, REACH + 1)
+    ]
+    grad_total = key_side(reach_rows, window_rows)
+    for arrived in arrivals:
+        grad_total = grad_total + arrived
+    key_total = grad_total[..., :HEAD_WIDTH]
+    value_total = grad_total[..., HEAD_WIDTH:]
     query_gradient = norm_grad(
         query_entries, query_inv, query_gain, QUERY_SCALE, query_total_sum
     ).astype(jnp.bfloat16)

time: 265 us -> 269 us (1.015)
  the two profiles are of different devices: /device:TPU:57 before, /device:TPU:105 now
where the time goes in v8:
time: 269 us; the launch traced here: 268 us
  blocking collectives  94.8 us (35%)
  waiting for transfers between devices  79 us (29%)
  starting transfers between devices  51.9 us (19%)
  matrix products  16.2 us (6%)
  local copies, waits for them, and re-layouts  13 us (5%)
  other arithmetic  12 us (4%)
    all_to_all x1, blocking collectives, on_device(): lax.all_to_all(leaving.reshape(head_devices, token_rows, -1), 'head', spl...  94.8 us
    all_to_all x1, waiting for transfers between devices, on_device(): lax.all_to_all(packed, 'head', split_axis=0, concat_axis=0, tiled=True)  73.2 us
    all_to_all x1, starting transfers between devices, on_device(): lax.all_to_all(packed, 'head', split_axis=0, concat_axis=0, tiled=True)  27.9 us
    ppermute x4, starting transfers between devices, passed_along(): return lax.ppermute(block, axis, route)  24 us
    ppermute x4, waiting for transfers between devices, passed_along(): return lax.ppermute(block, axis, route)  5.87 us
  transfers between devices with their start and end apart: 5, of which 3 were waited for; matrix products, arithmetic and copies ran while one was open for 5% of the time, Pallas kernels for 0%

profile of v8, /device:TPU:105, one launch (start us, length us, event | category | flops | bytes accessed | tf_op | source)
XLA Modules:
  0.0 267.8 jit_solution(14175076939788527306)
XLA Ops:
  0.6 1.1 bitcast_bitcast_fusion
  1.8 1.0 bitcast_bitcast_fusion.2
  2.7 1.0 pad_maximum_fusion
  3.7 27.9 %all-to-all-start = ((bf16[16,32,768]{2,1,0:T(8,128)(2,1)}), bf16[16,32,768]{2,1,0:T(8,128)(2,1)S(1)}, u32[]{:S(2)}, u32[]{:S(2)}) async-start(bf16[16,32,768]{2,1,0:T(8,128)(2,1)} %pad_maximum_fusion), calls=%async_computation | async-start | bytes 1572864 | tf_op jit(solution)/shard_map/all_to_all | solution.py:60
  31.6 0.8 dynamic_slice.6
  32.4 0.8 pad_dynamic-slice_fusion
  33.2 0.7 broadcast_bitcast_fusion
  33.9 1.1 compare_and_fusion
  35.0 73.2 %all-to-all-done = bf16[16,32,768]{2,1,0:T(8,128)(2,1)S(1)} async-done(((bf16[16,32,768]{2,1,0:T(8,128)(2,1)}), bf16[16,32,768]{2,1,0:T(8,128)(2,1)S(1)}, u32[]{:S(2)}, u32[]{:S(2)}) %all-to-all-start) | async-done | bytes 786464 | tf_op jit(solution)/shard_map/all_to_all | solution.py:60
  108.2 0.1 fusion.49
  108.3 0.8 fusion.55
  109.1 0.7 pad_maximum_fusion.2
  109.9 3.2 %collective-permute-start = (bf16[512,1,256]{2,0,1:T(8,128)(2,1)}, bf16[512,1,256]{2,0,1:T(8,128)(2,1)}, u32[]{:S(2)}, u32[]{:S(2)}) collective-permute-start(bf16[512,1,256]{2,0,1:T(8,128)(2,1)} %pad_maximum_fusion.2), channel_id=1, source_target_pairs={{0,32},{16,48},{32,64},{48,80},{64,96},{80,112},{96,128},{112,144}... | collective-permute-start | bytes 786440 | tf_op jit(solution)/shard_map/ppermute | solution.py:18
  113.1 16.5 %collective-permute-start.1 = (bf16[512,1,256]{2,0,1:T(8,128)(2,1)}, bf16[512,1,256]{2,0,1:T(8,128)(2,1)}, u32[]{:S(2)}, u32[]{:S(2)}) collective-permute-start(bf16[512,1,256]{2,0,1:T(8,128)(2,1)} %pad_maximum_fusion.2), channel_id=1, source_target_pairs={{0,16},{16,32},{32,48},{48,64},{64,80},{80,96},{96,112},{112,128},... | collective-permute-start | bytes 786440 | tf_op jit(solution)/shard_map/ppermute | solution.py:18
  129.5 1.0 slice_convert_fusion.2
  130.5 0.3 reshape.257
  130.8 1.3 multiply_reduce_fusion.2
  132.1 0.2 copy.182
  132.3 0.2 copy.216
  132.5 1.1 copy.172
  133.7 1.0 copy.213
  134.7 1.2 copy.215
  135.9 1.8 copy.221
  137.7 1.1 maximum_maximum_fusion
  138.8 3.3 %fusion.6 = (f32[2,512]{1,0:T(2,128)S(1)}, f32[1536,512,2]{1,0,2:T(8,128)S(1)}) fusion(pred[512,1536]{0,1:T(8,128)(4,1)S(1)} %compare_and_fusion, bf16[1536,1,256]{2,0,1:T(8,128)(2,1)S(1)} %maximum_maximum_fusion, f32[512,256]{1,0:T(8,128)} %copy.213, f32[256]{0:T(256)S(1)} %broadcast_bitcast_fusion, bf16[512,768]{1,0:T(8,128)(2,1)S(1)} %bitcast.240), kind=kOutput, calls=%fused_computation.11 | convolution fusion | flops 409598976 | bytes 8262656 | tf_op jit(solution)/shard_map/qhge,khe->hgqk/dot_general | solution.py:41
  142.2 3.3 %fusion.5 = bf16[1,2,512,1536]{2,3,1,0:T(8,128)(2,1)} fusion(f32[1536,512,2]{1,0,2:T(8,128)S(1)} %get-tuple-element.14, f32[2,512]{1,0:T(2,128)S(1)} %log.9, pred[512,1536]{0,1:T(8,128)(4,1)S(1)} %compare_and_fusion), kind=kLoop, calls=%fused_computation.10 | loop fusion | flops 7864320 | bytes 10227712 | tf_op jit(solution)/shard_map/convert_element_type | solution.py:118
  145.4 2.9 %multiply_reduce_fusion.1 = (f32[512,2]{0,1:T(2,128)S(1)}, bf16[512,1,2,128]{0,3,2,1:T(8,128)(2,1)}) fusion(f32[512,1,2,128]{0,3,2,1:T(8,128)S(1)} %bitcast.250, f32[512,2]{0,1:T(2,128)S(1)} %bitcast.260, f32[1536,512,2]{1,0,2:T(8,128)S(1)} %get-tuple-element.14, pred[512,1536]{0,1:T(8,128)(4,1)S(1)} %compare_and_fusion, ...), kind=kOutput, calls=%fused_computation.45 | convolution fusion | flops 409598976 | bytes 8265728 | tf_op jit(solution)/shard_map/hgqk,khe->qhge/dot_general | solution.py:99
  148.3 3.4 %fusion = bf16[1,2,512,1536]{2,3,1,0:T(8,128)(2,1)S(1)} fusion(f32[1536,512,2]{1,0,2:T(8,128)S(1)} %get-tuple-element.14, bf16[512,2,128]{0,2,1:T(8,128)(2,1)S(1)} %bitcast.251, f32[2,512]{1,0:T(2,128)S(1)} %bitcast.261, f32[2,512]{1,0:T(2,128)S(1)} %log.9, pred[512,1536]{0,1:T(8,128)(4,1)S(1)} %compare_and_fusion, ...), kind=kOutput, calls=%fused_computation.1 | convolution fusion | flops 418381824 | bytes 10887168 | tf_op jit(solution)/shard_map/qhge,khe->hgqk/dot_general | solution.py:112
  151.7 1.5 fusion.16
  153.2 0.5 convolution_bitcast_fusion.1
  153.7 0.6 multiply_reduce_fusion
  154.5 0.2 copy.184
  154.7 0.2 concatenate.35
  154.9 2.3 fusion.17
  157.3 1.9 collective-permute-start.2
  159.2 2.4 collective-permute-start.3
  161.6 0.2 copy.177
  161.8 0.2 concatenate.34
  162.0 1.7 convolution_bitcast_fusion
  163.6 2.8 %collective-permute-done.2 = bf16[512,1,256]{2,0,1:T(8,128)(2,1)S(1)} collective-permute-done((bf16[512,1,256]{2,0,1:T(8,128)(2,1)S(1)}, bf16[512,1,256]{2,0,1:T(8,128)(2,1)S(1)}, u32[]{:S(2)}, u32[]{:S(2)}) %collective-permute-start.2) | collective-permute-done | bytes 262176 | tf_op jit(solution)/shard_map/ppermute | solution.py:18
  166.4 3.1 %collective-permute-done.3 = bf16[512,1,256]{2,0,1:T(8,128)(2,1)S(1)} collective-permute-done((bf16[512,1,256]{2,0,1:T(8,128)(2,1)S(1)}, bf16[512,1,256]{2,0,1:T(8,128)(2,1)S(1)}, u32[]{:S(2)}, u32[]{:S(2)}) %collective-permute-start.3) | collective-permute-done | bytes 262176 | tf_op jit(solution)/shard_map/ppermute | solution.py:18
  169.6 0.1 fusion.51
  169.8 0.3 fusion.48
  170.1 94.8 %all_to_all.10 = bf16[16,32,768]{2,1,0:T(8,128)(2,1)S(1)} all-to-all(bf16[16,32,768]{2,1,0:T(8,128)(2,1)S(1)} %pad_maximum_fusion.1), channel_id=1, replica_groups=mesh['ctx'=64,'head'=16] {'head'}, dimensions={0} | all-to-all | bytes 1572864 | tf_op jit(solution)/shard_map/all_to_all | solution.py:162
  265.0 0.7 copy.227
  265.7 0.7 copy.228
  266.5 0.7 copy.243
  267.1 0.7 copy.244
  (30 shorter events, 0.6 us)
Async XLA Ops:
  0.6 1.1 copy-start
  3.7 104.5 %all-to-all-start = ((bf16[16,32,768]{2,1,0:T(8,128)(2,1)}), bf16[16,32,768]{2,1,0:T(8,128)(2,1)S(1)}, u32[]{:S(2)}, u32[]{:S(2)}) async-start(bf16[16,32,768]{2,1,0:T(8,128)(2,1)} %pad_maximum_fusion), calls=%async_computation | async-start | bytes 1572864 | tf_op jit(solution)/shard_map/all_to_all | solution.py:60
  109.9 27.9 %collective-permute-start = (bf16[512,1,256]{2,0,1:T(8,128)(2,1)}, bf16[512,1,256]{2,0,1:T(8,128)(2,1)}, u32[]{:S(2)}, u32[]{:S(2)}) collective-permute-start(bf16[512,1,256]{2,0,1:T(8,128)(2,1)} %pad_maximum_fusion.2), channel_id=1, source_target_pairs={{0,32},{16,48},{32,64},{48,80},{64,96},{80,112},{96,128},{112,144}... | collective-permute-start | bytes 786440 | tf_op jit(solution)/shard_map/ppermute | solution.py:18
  113.1 24.7 %collective-permute-start.1 = (bf16[512,1,256]{2,0,1:T(8,128)(2,1)}, bf16[512,1,256]{2,0,1:T(8,128)(2,1)}, u32[]{:S(2)}, u32[]{:S(2)}) collective-permute-start(bf16[512,1,256]{2,0,1:T(8,128)(2,1)} %pad_maximum_fusion.2), channel_id=1, source_target_pairs={{0,16},{16,32},{32,48},{48,64},{64,80},{80,96},{96,112},{112,128},... | collective-permute-start | bytes 786440 | tf_op jit(solution)/shard_map/ppermute | solution.py:18
  145.4 2.9 %copy-start.1 = (bf16[512,256]{0,1:T(8,128)(2,1)S(1)}, bf16[512,256]{0,1:T(8,128)(2,1)}, u32[]{:S(2)}) copy-start(bf16[512,256]{0,1:T(8,128)(2,1)} %copy.221) | copy-start | bytes 786436
  148.3 3.4 %copy-start.5 = (f32[128]{0:T(128)S(1)}, f32[128]{0:T(128)}, u32[]{:S(2)}) copy-start(f32[128]{0:T(128)} %param.11) | copy-start | bytes 1540
  153.7 3.5 %copy-start.3 = (bf16[1024,1,128]{2,0,1:T(8,128)(2,1)S(1)}, bf16[1024,1,128]{2,0,1:T(8,128)(2,1)}, u32[]{:S(2)}) copy-start(bf16[1024,1,128]{2,0,1:T(8,128)(2,1)} %fusion.16) | copy-start | bytes 786436
  153.7 7.9 %copy-start.2 = (bf16[512,1,2,128]{0,3,2,1:T(8,128)(2,1)S(1)}, bf16[512,1,2,128]{0,3,2,1:T(8,128)(2,1)}, u32[]{:S(2)}) copy-start(bf16[512,1,2,128]{0,3,2,1:T(8,128)(2,1)} %get-tuple-element.16) | copy-start | bytes 786436
  154.4 15.2 %copy-start.4 = (f32[128]{0:T(128)S(1)}, f32[128]{0:T(128)}, u32[]{:S(2)}) copy-start(f32[128]{0:T(128)} %param.12) | copy-start | bytes 1540
  157.3 9.1 %collective-permute-start.2 = (bf16[512,1,256]{2,0,1:T(8,128)(2,1)S(1)}, bf16[512,1,256]{2,0,1:T(8,128)(2,1)S(1)}, u32[]{:S(2)}, u32[]{:S(2)}) collective-permute-start(bf16[512,1,256]{2,0,1:T(8,128)(2,1)S(1)} %get-tuple-element.11), channel_id=1, source_target_pairs={{16,0},{32,16},{48,32},{64,48},{80,64},{96,80},{112,96},{128,112},... | collective-permute-start | bytes 786440 | tf_op jit(solution)/shard_map/ppermute | solution.py:18
  159.2 10.3 %collective-permute-start.3 = (bf16[512,1,256]{2,0,1:T(8,128)(2,1)S(1)}, bf16[512,1,256]{2,0,1:T(8,128)(2,1)S(1)}, u32[]{:S(2)}, u32[]{:S(2)}) collective-permute-start(bf16[512,1,256]{2,0,1:T(8,128)(2,1)S(1)} %get-tuple-element.12), channel_id=1, source_target_pairs={{32,0},{48,16},{64,32},{80,48},{96,64},{112,80},{128,96},{144,112}... | collective-permute-start | bytes 786440 | tf_op jit(solution)/shard_map/ppermute | solution.py:18

commit v9 on v6

--- a/solution.py
+++ b/solution.py
@@ -80,12 +80,12 @@
     row_start = ctx_place * row_count
     query_docs = lax.dynamic_slice_in_dim(doc_ids, row_start, row_count, 0)
     query_pos = row_start + jnp.arange(row_count, dtype=jnp.int32)
-    own_pair = jnp.concatenate([key_norm_factor, value_entries], axis=-1)
+    own_pair = jnp.concatenate([key_loc.reshape(row_count, kv_heads, HEAD_WIDTH), value_entries], axis=-1)
     pairs = [own_pair] + [
         passed_along(own_pair, "ctx", offset) for offset in range(1, REACH + 1)
     ]
     window = jnp.concatenate(pairs[::-1], axis=0)
-    key_window = window[..., :HEAD_WIDTH]
+    key_window = normalize(window[..., :HEAD_WIDTH].astype(jnp.float32), key_gain, 1.0)[1]
     value_window = window[..., HEAD_WIDTH:]
     window_rows = (REACH + 1) * row_count
     key_pos = row_start - REACH * row_count + jnp.arange(window_rows, dtype=jnp.int32)

time: 265 us -> 264 us (level)
  waiting for transfers between devices: 94 us -> 100 us
  other arithmetic: 11.2 us -> 5.4 us
    ppermute x4, waiting for transfers between devices: 10.7 us -> 14.9 us  [passed_along(): return lax.ppermute(block, axis, route)]
    unnamed x10 -> x16, local copies, waits for them, and re-layouts: 0.13 us -> 4.23 us
  transfers between devices with their start and end apart: 5 -> 5, of which waited for: 4 -> 5; matrix products, arithmetic and copies ran while one was open for 4% -> 1% of each run, Pallas kernels for 0% -> 0%
where the time goes in v9:
time: 264 us; the launch traced here: 263 us
  waiting for transfers between devices  100 us (38%)
  blocking collectives  92.9 us (35%)
  starting transfers between devices  40.5 us (15%)
  matrix products  13.4 us (5%)
  local copies, waits for them, and re-layouts  9.95 us (4%)
  other arithmetic  5.4 us (2%)
    all_to_all x1, blocking collectives, on_device(): lax.all_to_all(leaving.reshape(head_devices, token_rows, -1), 'head', spl...  92.9 us
    all_to_all x1, waiting for transfers between devices, on_device(): lax.all_to_all(packed, 'head', split_axis=0, concat_axis=0, tiled=True)  85.2 us
    all_to_all x1, starting transfers between devices, on_device(): lax.all_to_all(packed, 'head', split_axis=0, concat_axis=0, tiled=True)  29.9 us
    ppermute x4, waiting for transfers between devices, passed_along(): return lax.ppermute(block, axis, route)  14.9 us
    ppermute x4, starting transfers between devices, passed_along(): return lax.ppermute(block, axis, route)  10.7 us
  transfers between devices with their start and end apart: 5, of which 5 were waited for; matrix products, arithmetic and copies ran while one was open for 1% of the time, Pallas kernels for 0%

profile of v9, /device:TPU:57, one launch (start us, length us, event | category | flops | bytes accessed | tf_op | source)
XLA Modules:
  0.0 263.3 jit_solution(10455053270779947272)
XLA Ops:
  0.7 1.0 copy.111
  1.7 1.0 copy.114
  2.7 0.9 copy.112
  3.6 0.9 copy.113
  4.6 1.1 copy.69
  5.8 29.9 %all-to-all-start = ((bf16[16,32,768]{2,1,0:T(8,128)(2,1)}), bf16[16,32,768]{2,1,0:T(8,128)(2,1)S(1)}, u32[]{:S(2)}, u32[]{:S(2)}) async-start(bf16[16,32,768]{2,1,0:T(8,128)(2,1)} %copy.69), calls=%async_computation | async-start | bytes 1572864 | tf_op jit(solution)/shard_map/all_to_all | solution.py:60
  35.7 0.1 pad_dynamic-slice_fusion
  35.8 1.9 compare_and_fusion
  37.7 85.2 %all-to-all-done = bf16[16,32,768]{2,1,0:T(8,128)(2,1)S(1)} async-done(((bf16[16,32,768]{2,1,0:T(8,128)(2,1)}), bf16[16,32,768]{2,1,0:T(8,128)(2,1)S(1)}, u32[]{:S(2)}, u32[]{:S(2)}) %all-to-all-start) | async-done | bytes 786464 | tf_op jit(solution)/shard_map/all_to_all | solution.py:60
  122.9 0.1 copy.104
  123.1 0.1 copy.105
  123.2 0.7 pad_maximum_fusion.3
  123.9 1.9 collective-permute-start
  125.8 1.9 collective-permute-start.1
  127.8 0.1 slice_convert_fusion.1
  127.9 0.2 copy.72
  128.2 0.2 copy.101
  128.5 0.2 copy.81
  128.7 0.1 copy.78
  128.8 2.9 %collective-permute-done = bf16[512,1,256]{0,2,1:T(8,128)(2,1)} collective-permute-done((bf16[512,1,256]{0,2,1:T(8,128)(2,1)}, bf16[512,1,256]{0,2,1:T(8,128)(2,1)}, u32[]{:S(2)}, u32[]{:S(2)}) %collective-permute-start) | collective-permute-done | bytes 262176 | tf_op jit(solution)/shard_map/ppermute | solution.py:18
  131.7 3.3 %collective-permute-done.1 = bf16[512,1,256]{0,2,1:T(8,128)(2,1)} collective-permute-done((bf16[512,1,256]{0,2,1:T(8,128)(2,1)}, bf16[512,1,256]{0,2,1:T(8,128)(2,1)}, u32[]{:S(2)}, u32[]{:S(2)}) %collective-permute-start.1) | collective-permute-done | bytes 262176 | tf_op jit(solution)/shard_map/ppermute | solution.py:18
  135.1 1.1 maximum_maximum_fusion
  136.1 0.1 fusion.32
  136.3 3.6 %fusion.6 = (f32[2,512]{1,0:T(2,128)S(1)}, f32[1536,512,2]{1,0,2:T(8,128)S(1)}) fusion(pred[512,1536]{0,1:T(8,128)(4,1)} %compare_and_fusion, f32[128]{0:T(128)S(1)} %copy-done.2, f32[1536]{0:T(1024)S(1)} %add_rsqrt_fusion, bf16[1536,1,256]{0,2,1:T(8,128)(2,1)S(1)} %maximum_maximum_fusion, f32[512,256]{1,0:T(8,128)S(1)} %copy.101, ...), kind=kOutput, calls=%fused_computation.11 | convolution fusion | flops 410385408 | bytes 8271360 | tf_op jit(solution)/shard_map/qhge,khe->hgqk/dot_general | solution.py:41
  139.9 2.2 multiply_reduce_fusion.1
  142.1 2.3 fusion.17
  144.3 3.6 %fusion.8 = bf16[2,512,1536]{1,2,0:T(8,128)(2,1)S(1)} fusion(bf16[512,2,128]{0,2,1:T(8,128)(2,1)S(1)} %bitcast.231, f32[1536,512,2]{1,0,2:T(8,128)S(1)} %get-tuple-element.18, f32[2,512]{1,0:T(2,128)S(1)} %bitcast.239, f32[2,512]{1,0:T(2,128)S(1)} %log.9, pred[512,1536]{0,1:T(8,128)(4,1)S(1)} %copy-done, bf16[1536,1,256]{0,2,1:T(8,128)(2,1)S(1)} %maximum_maximum_fusion), kind=kOutput, calls=%fused_computation.13 | convolution fusion | flops 418381824 | bytes 10887168 | tf_op jit(solution)/shard_map/qhge,khe->hgqk/dot_general | solution.py:112
  147.9 0.7 multiply_reduce_fusion
  148.6 1.2 convolution_bitcast_fusion
  149.7 0.8 maximum_convert_fusion
  150.5 4.5 %collective-permute-start.2 = (bf16[512,1,256]{0,2,1:T(8,128)(2,1)}, bf16[512,1,256]{0,2,1:T(8,128)(2,1)S(1)}, u32[]{:S(2)}, u32[]{:S(2)}) collective-permute-start(bf16[512,1,256]{0,2,1:T(8,128)(2,1)} %get-tuple-element.4), channel_id=1, source_target_pairs={{16,0},{32,16},{48,32},{64,48},{80,64},{96,80},{112,96},{128,112},... | collective-permute-start | bytes 786440 | tf_op jit(solution)/shard_map/ppermute | solution.py:18
  155.0 2.4 collective-permute-start.3
  157.4 0.1 multiply_convert_fusion.1
  157.5 0.2 copy.83
  157.7 0.2 concatenate.32
  157.9 0.2 copy.77
  158.0 0.2 concatenate.31
  158.2 3.0 %collective-permute-done.2 = bf16[512,1,256]{0,2,1:T(8,128)(2,1)S(1)} collective-permute-done((bf16[512,1,256]{0,2,1:T(8,128)(2,1)}, bf16[512,1,256]{0,2,1:T(8,128)(2,1)S(1)}, u32[]{:S(2)}, u32[]{:S(2)}) %collective-permute-start.2) | collective-permute-done | bytes 262176 | tf_op jit(solution)/shard_map/ppermute | solution.py:18
  161.3 5.7 %collective-permute-done.3 = bf16[512,1,256]{0,2,1:T(8,128)(2,1)S(1)} collective-permute-done((bf16[512,1,256]{0,2,1:T(8,128)(2,1)S(1)}, bf16[512,1,256]{0,2,1:T(8,128)(2,1)S(1)}, u32[]{:S(2)}, u32[]{:S(2)}) %collective-permute-start.3) | collective-permute-done | bytes 262176 | tf_op jit(solution)/shard_map/ppermute | solution.py:18
  166.9 0.1 fusion.45
  167.1 0.1 fusion.43
  167.2 0.1 copy.87
  167.3 0.1 copy.88
  167.5 92.9 %all_to_all.10 = bf16[16,32,768]{2,1,0:T(8,128)(2,1)S(1)} all-to-all(bf16[16,32,768]{2,1,0:T(8,128)(2,1)S(1)} %pad_maximum_fusion.1), channel_id=1, replica_groups=mesh['ctx'=64,'head'=16] {'head'}, dimensions={0} | all-to-all | bytes 1572864 | tf_op jit(solution)/shard_map/all_to_all | solution.py:150
  260.5 0.7 copy.107
  261.3 0.7 copy.108
  262.0 0.7 copy.123
  262.7 0.7 copy.124
  (25 shorter events, 0.6 us)
Async XLA Ops:
  0.6 35.0 %copy-start.1 = (s32[32768]{0:T(1024)S(1)}, s32[32768]{0:T(1024)}, u32[]{:S(2)}) copy-start(s32[32768]{0:T(1024)} %param.13) | copy-start | bytes 393220
  0.6 35.2 %copy-start.3 = (f32[128]{0:T(128)S(1)}, f32[128]{0:T(128)}, u32[]{:S(2)}) copy-start(f32[128]{0:T(128)} %param.11) | copy-start | bytes 1540
  5.8 130.5 %copy-start.2 = (f32[128]{0:T(128)S(1)}, f32[128]{0:T(128)}, u32[]{:S(2)}) copy-start(f32[128]{0:T(128)} %param.12) | copy-start | bytes 1540
  5.8 117.2 %all-to-all-start = ((bf16[16,32,768]{2,1,0:T(8,128)(2,1)}), bf16[16,32,768]{2,1,0:T(8,128)(2,1)S(1)}, u32[]{:S(2)}, u32[]{:S(2)}) async-start(bf16[16,32,768]{2,1,0:T(8,128)(2,1)} %copy.69), calls=%async_computation | async-start | bytes 1572864 | tf_op jit(solution)/shard_map/all_to_all | solution.py:60
  123.9 7.8 %collective-permute-start = (bf16[512,1,256]{0,2,1:T(8,128)(2,1)}, bf16[512,1,256]{0,2,1:T(8,128)(2,1)}, u32[]{:S(2)}, u32[]{:S(2)}) collective-permute-start(bf16[512,1,256]{0,2,1:T(8,128)(2,1)} %pad_maximum_fusion.3), channel_id=1, source_target_pairs={{0,32},{16,48},{32,64},{48,80},{64,96},{80,112},{96,128},{112,144}... | collective-permute-start | bytes 786440 | tf_op jit(solution)/shard_map/ppermute | solution.py:18
  125.8 9.2 %collective-permute-start.1 = (bf16[512,1,256]{0,2,1:T(8,128)(2,1)}, bf16[512,1,256]{0,2,1:T(8,128)(2,1)}, u32[]{:S(2)}, u32[]{:S(2)}) collective-permute-start(bf16[512,1,256]{0,2,1:T(8,128)(2,1)} %pad_maximum_fusion.3), channel_id=1, source_target_pairs={{0,16},{16,32},{32,48},{48,64},{64,80},{80,96},{96,112},{112,128},... | collective-permute-start | bytes 786440 | tf_op jit(solution)/shard_map/ppermute | solution.py:18
  136.3 3.6 %copy-start = (pred[512,1536]{0,1:T(8,128)(4,1)S(1)}, pred[512,1536]{0,1:T(8,128)(4,1)}, u32[]{:S(2)}) copy-start(pred[512,1536]{0,1:T(8,128)(4,1)} %compare_and_fusion) | copy-start | bytes 2359300
  150.5 10.7 %collective-permute-start.2 = (bf16[512,1,256]{0,2,1:T(8,128)(2,1)}, bf16[512,1,256]{0,2,1:T(8,128)(2,1)S(1)}, u32[]{:S(2)}, u32[]{:S(2)}) collective-permute-start(bf16[512,1,256]{0,2,1:T(8,128)(2,1)} %get-tuple-element.4), channel_id=1, source_target_pairs={{16,0},{32,16},{48,32},{64,48},{80,64},{96,80},{112,96},{128,112},... | collective-permute-start | bytes 786440 | tf_op jit(solution)/shard_map/ppermute | solution.py:18
  155.0 11.9 %collective-permute-start.3 = (bf16[512,1,256]{0,2,1:T(8,128)(2,1)S(1)}, bf16[512,1,256]{0,2,1:T(8,128)(2,1)S(1)}, u32[]{:S(2)}, u32[]{:S(2)}) collective-permute-start(bf16[512,1,256]{0,2,1:T(8,128)(2,1)S(1)} %get-tuple-element.5), channel_id=1, source_target_pairs={{32,0},{48,16},{64,32},{80,48},{96,64},{112,80},{128,96},{144,112}... | collective-permute-start | bytes 786440 | tf_op jit(solution)/shard_map/ppermute | solution.py:18

commit v10 on v9

--- a/solution.py
+++ b/solution.py
@@ -53,7 +53,7 @@
     packed = jnp.concatenate(
         [
             jnp.swapaxes(part.reshape(token_rows, head_devices, -1), 0, 1)
-            for part in (query_matrix, key_matrix, value_matrix, output_gradient)
+            for part in (key_matrix, value_matrix, query_matrix, output_gradient)
         ],
         axis=-1,
     )
@@ -61,9 +61,9 @@
     arrived = arrived.reshape(token_rows * head_devices, -1)
     widths = [query_matrix.shape[1] // head_devices, key_matrix.shape[1] // head_devices]
     cuts = [widths[0], widths[0] + widths[1], widths[0] + 2 * widths[1]]
-    query_loc = arrived[:, : cuts[0]]
-    key_loc = arrived[:, cuts[0] : cuts[1]]
-    value_loc = arrived[:, cuts[1] : cuts[2]]
+    key_loc = arrived[:, : widths[1]]
+    value_loc = arrived[:, widths[1] : 2 * widths[1]]
+    query_loc = arrived[:, 2 * widths[1] : cuts[2]]
     grad_loc = arrived[:, cuts[2] :]
     row_count = query_loc.shape[0]
     kv_heads = key_loc.shape[1] // HEAD_WIDTH
@@ -80,7 +80,7 @@
     row_start = ctx_place * row_count
     query_docs = lax.dynamic_slice_in_dim(doc_ids, row_start, row_count, 0)
     query_pos = row_start + jnp.arange(row_count, dtype=jnp.int32)
-    own_pair = jnp.concatenate([key_loc.reshape(row_count, kv_heads, HEAD_WIDTH), value_entries], axis=-1)
+    own_pair = arrived[:, : 2 * widths[1]].reshape(row_count, kv_heads, 2 * HEAD_WIDTH)
     pairs = [own_pair] + [
         passed_along(own_pair, "ctx", offset) for offset in range(1, REACH + 1)
     ]

time: 264 us -> 263 us (level)
  the two profiles are of different devices: /device:TPU:57 before, /device:TPU:99 now
where the time goes in v10:
time: 263 us; the launch traced here: 262 us
  blocking collectives  92.9 us (35%)
  waiting for transfers between devices  87.5 us (33%)
  starting transfers between devices  52.2 us (20%)
  matrix products  13.3 us (5%)
  local copies, waits for them, and re-layouts  10.5 us (4%)
  other arithmetic  4.72 us (2%)
    all_to_all x1, blocking collectives, on_device(): lax.all_to_all(leaving.reshape(head_devices, token_rows, -1), 'head', spl...  92.9 us
    all_to_all x1, waiting for transfers between devices, on_device(): lax.all_to_all(packed, 'head', split_axis=0, concat_axis=0, tiled=True)  72.2 us
    all_to_all x1, starting transfers between devices, on_device(): lax.all_to_all(packed, 'head', split_axis=0, concat_axis=0, tiled=True)  28.2 us
    ppermute x4, starting transfers between devices, passed_along(): return lax.ppermute(block, axis, route)  24 us
    ppermute x4, waiting for transfers between devices, passed_along(): return lax.ppermute(block, axis, route)  15.4 us
  transfers between devices with their start and end apart: 5, of which 4 were waited for; matrix products, arithmetic and copies ran while one was open for 2% of the time, Pallas kernels for 0%

profile of v10, /device:TPU:99, one launch (start us, length us, event | category | flops | bytes accessed | tf_op | source)
XLA Modules:
  0.0 262.2 jit_solution(9428905673384393925)
XLA Ops:
  0.7 1.0 copy.114
  1.7 1.0 copy.113
  2.7 0.9 copy.112
  3.6 0.9 copy.111
  4.6 1.1 copy.69
  5.8 28.2 %all-to-all-start = ((bf16[16,32,768]{2,1,0:T(8,128)(2,1)}), bf16[16,32,768]{2,1,0:T(8,128)(2,1)S(1)}, u32[]{:S(2)}, u32[]{:S(2)}) async-start(bf16[16,32,768]{2,1,0:T(8,128)(2,1)} %copy.69), calls=%async_computation | async-start | bytes 1572864 | tf_op jit(solution)/shard_map/all_to_all | solution.py:60
  34.1 0.1 pad_dynamic-slice_fusion
  34.2 0.6 broadcast_bitcast_fusion
  34.7 1.9 compare_and_fusion
  36.6 72.2 %all-to-all-done = bf16[16,32,768]{2,1,0:T(8,128)(2,1)S(1)} async-done(((bf16[16,32,768]{2,1,0:T(8,128)(2,1)}), bf16[16,32,768]{2,1,0:T(8,128)(2,1)S(1)}, u32[]{:S(2)}, u32[]{:S(2)}) %all-to-all-start) | async-done | bytes 786464 | tf_op jit(solution)/shard_map/all_to_all | solution.py:60
  108.8 0.1 slice_convert_fusion.1
  108.9 0.1 copy.104
  109.0 16.6 %collective-permute-start.1 = (bf16[512,1,256]{0,2,1:T(8,128)(2,1)S(1)}, bf16[512,1,256]{0,2,1:T(8,128)(2,1)}, u32[]{:S(2)}, u32[]{:S(2)}) collective-permute-start(bf16[512,1,256]{0,2,1:T(8,128)(2,1)S(1)} %bitcast.216), channel_id=1, source_target_pairs={{0,16},{16,32},{32,48},{48,64},{64,80},{80,96},{96,112},{112,128},... | collective-permute-start | bytes 786440 | tf_op jit(solution)/shard_map/ppermute | solution.py:18
  125.7 3.2 %collective-permute-start = (bf16[512,1,256]{0,2,1:T(8,128)(2,1)S(1)}, bf16[512,1,256]{0,2,1:T(8,128)(2,1)}, u32[]{:S(2)}, u32[]{:S(2)}) collective-permute-start(bf16[512,1,256]{0,2,1:T(8,128)(2,1)S(1)} %bitcast.217), channel_id=1, source_target_pairs={{0,32},{16,48},{32,64},{48,80},{64,96},{80,112},{96,128},{112,144}... | collective-permute-start | bytes 786440 | tf_op jit(solution)/shard_map/ppermute | solution.py:18
  128.9 0.1 copy.105
  129.0 0.2 copy.71
  129.4 0.1 copy.77
  129.6 0.2 copy.101
  129.8 0.2 copy.80
  130.0 7.4 %collective-permute-done = bf16[512,1,256]{0,2,1:T(8,128)(2,1)} collective-permute-done((bf16[512,1,256]{0,2,1:T(8,128)(2,1)S(1)}, bf16[512,1,256]{0,2,1:T(8,128)(2,1)}, u32[]{:S(2)}, u32[]{:S(2)}) %collective-permute-start) | collective-permute-done | bytes 262176 | tf_op jit(solution)/shard_map/ppermute | solution.py:18
  137.4 1.1 pad_maximum_fusion.1
  138.5 0.1 fusion.32
  138.6 3.6 %fusion.6 = (f32[2,512]{1,0:T(2,128)S(1)}, f32[1536,512,2]{1,0,2:T(8,128)S(1)}) fusion(pred[512,1536]{0,1:T(8,128)(4,1)} %compare_and_fusion, f32[128]{0:T(128)S(1)} %copy-done.2, f32[1536]{0:T(1024)S(1)} %add_rsqrt_fusion, bf16[1536,1,256]{0,2,1:T(8,128)(2,1)S(1)} %pad_maximum_fusion.1, f32[512,256]{1,0:T(8,128)S(1)} %copy.101, ...), kind=kOutput, calls=%fused_computation.11 | convolution fusion | flops 410385408 | bytes 8271360 | tf_op jit(solution)/shard_map/qhge,khe->hgqk/dot_general | solution.py:41
  142.2 2.2 fusion.17
  144.5 2.2 multiply_reduce_fusion.1
  146.7 3.5 %fusion.8 = bf16[2,512,1536]{1,2,0:T(8,128)(2,1)S(1)} fusion(bf16[512,2,128]{0,2,1:T(8,128)(2,1)S(1)} %bitcast.229, f32[1536,512,2]{1,0,2:T(8,128)S(1)} %get-tuple-element.17, f32[2,512]{1,0:T(2,128)S(1)} %bitcast.237, f32[2,512]{1,0:T(2,128)S(1)} %log.9, pred[512,1536]{0,1:T(8,128)(4,1)S(1)} %copy-done, bf16[1536,1,256]{0,2,1:T(8,128)(2,1)S(1)} %pad_maximum_fusion.1), kind=kOutput, calls=%fused_computation.13 | convolution fusion | flops 418381824 | bytes 10887168 | tf_op jit(solution)/shard_map/qhge,khe->hgqk/dot_general | solution.py:112
  150.2 0.7 multiply_reduce_fusion
  150.9 1.2 convolution_bitcast_fusion
  152.0 0.8 maximum_convert_fusion
  152.8 1.9 collective-permute-start.3
  154.7 2.2 collective-permute-start.2
  157.0 0.1 multiply_convert_fusion.1
  157.1 0.2 copy.82
  157.3 0.2 concatenate.28
  157.5 0.2 copy.76
  157.6 0.2 concatenate.27
  157.8 4.7 %collective-permute-done.3 = bf16[512,1,256]{0,2,1:T(8,128)(2,1)S(1)} collective-permute-done((bf16[512,1,256]{0,2,1:T(8,128)(2,1)}, bf16[512,1,256]{0,2,1:T(8,128)(2,1)S(1)}, u32[]{:S(2)}, u32[]{:S(2)}) %collective-permute-start.3) | collective-permute-done | bytes 262176 | tf_op jit(solution)/shard_map/ppermute | solution.py:18
  162.5 3.3 %collective-permute-done.2 = bf16[512,1,256]{0,2,1:T(8,128)(2,1)S(1)} collective-permute-done((bf16[512,1,256]{0,2,1:T(8,128)(2,1)S(1)}, bf16[512,1,256]{0,2,1:T(8,128)(2,1)S(1)}, u32[]{:S(2)}, u32[]{:S(2)}) %collective-permute-start.2) | collective-permute-done | bytes 262176 | tf_op jit(solution)/shard_map/ppermute | solution.py:18
  165.7 0.1 fusion.45
  165.9 0.2 fusion.43
  166.0 0.1 copy.88
  166.2 0.1 copy.87
  166.3 0.1 pad_maximum_fusion.2
  166.4 92.9 %all_to_all.10 = bf16[16,32,768]{2,1,0:T(8,128)(2,1)S(1)} all-to-all(bf16[16,32,768]{2,1,0:T(8,128)(2,1)S(1)} %pad_maximum_fusion.2), channel_id=1, replica_groups=mesh['ctx'=64,'head'=16] {'head'}, dimensions={0} | all-to-all | bytes 1572864 | tf_op jit(solution)/shard_map/all_to_all | solution.py:150
  259.4 0.7 copy.107
  260.1 0.7 copy.108
  260.8 0.7 copy.124
  261.5 0.7 copy.123
  (26 shorter events, 0.5 us)
Async XLA Ops:
  0.6 33.4 %copy-start.1 = (s32[32768]{0:T(1024)S(1)}, s32[32768]{0:T(1024)}, u32[]{:S(2)}) copy-start(s32[32768]{0:T(1024)} %param.13) | copy-start | bytes 393220
  0.6 33.5 %copy-start.3 = (f32[128]{0:T(128)S(1)}, f32[128]{0:T(128)}, u32[]{:S(2)}) copy-start(f32[128]{0:T(128)} %param.11) | copy-start | bytes 1540
  5.8 132.9 %copy-start.2 = (f32[128]{0:T(128)S(1)}, f32[128]{0:T(128)}, u32[]{:S(2)}) copy-start(f32[128]{0:T(128)} %param.12) | copy-start | bytes 1540
  5.8 103.0 %all-to-all-start = ((bf16[16,32,768]{2,1,0:T(8,128)(2,1)}), bf16[16,32,768]{2,1,0:T(8,128)(2,1)S(1)}, u32[]{:S(2)}, u32[]{:S(2)}) async-start(bf16[16,32,768]{2,1,0:T(8,128)(2,1)} %copy.69), calls=%async_computation | async-start | bytes 1572864 | tf_op jit(solution)/shard_map/all_to_all | solution.py:60
  109.0 21.0 %collective-permute-start.1 = (bf16[512,1,256]{0,2,1:T(8,128)(2,1)S(1)}, bf16[512,1,256]{0,2,1:T(8,128)(2,1)}, u32[]{:S(2)}, u32[]{:S(2)}) collective-permute-start(bf16[512,1,256]{0,2,1:T(8,128)(2,1)S(1)} %bitcast.216), channel_id=1, source_target_pairs={{0,16},{16,32},{32,48},{48,64},{64,80},{80,96},{96,112},{112,128},... | collective-permute-start | bytes 786440 | tf_op jit(solution)/shard_map/ppermute | solution.py:18
  125.7 11.7 %collective-permute-start = (bf16[512,1,256]{0,2,1:T(8,128)(2,1)S(1)}, bf16[512,1,256]{0,2,1:T(8,128)(2,1)}, u32[]{:S(2)}, u32[]{:S(2)}) collective-permute-start(bf16[512,1,256]{0,2,1:T(8,128)(2,1)S(1)} %bitcast.217), channel_id=1, source_target_pairs={{0,32},{16,48},{32,64},{48,80},{64,96},{80,112},{96,128},{112,144}... | collective-permute-start | bytes 786440 | tf_op jit(solution)/shard_map/ppermute | solution.py:18
  138.6 3.6 %copy-start = (pred[512,1536]{0,1:T(8,128)(4,1)S(1)}, pred[512,1536]{0,1:T(8,128)(4,1)}, u32[]{:S(2)}) copy-start(pred[512,1536]{0,1:T(8,128)(4,1)} %compare_and_fusion) | copy-start | bytes 2359300
  146.7 3.5 %copy-start.4 = (f32[128]{0:T(128)S(1)}, f32[128]{0:T(128)}, u32[]{:S(2)}) copy-start(f32[128]{0:T(128)} %param.11) | copy-start | bytes 1540
  152.8 9.7 %collective-permute-start.3 = (bf16[512,1,256]{0,2,1:T(8,128)(2,1)}, bf16[512,1,256]{0,2,1:T(8,128)(2,1)S(1)}, u32[]{:S(2)}, u32[]{:S(2)}) collective-permute-start(bf16[512,1,256]{0,2,1:T(8,128)(2,1)} %get-tuple-element.5), channel_id=1, source_target_pairs={{32,0},{48,16},{64,32},{80,48},{96,64},{112,80},{128,96},{144,112}... | collective-permute-start | bytes 786440 | tf_op jit(solution)/shard_map/ppermute | solution.py:18
  154.7 11.0 %collective-permute-start.2 = (bf16[512,1,256]{0,2,1:T(8,128)(2,1)S(1)}, bf16[512,1,256]{0,2,1:T(8,128)(2,1)S(1)}, u32[]{:S(2)}, u32[]{:S(2)}) collective-permute-start(bf16[512,1,256]{0,2,1:T(8,128)(2,1)S(1)} %get-tuple-element.4), channel_id=1, source_target_pairs={{16,0},{32,16},{48,32},{64,48},{80,64},{96,80},{112,96},{128,112},... | collective-permute-start | bytes 786440 | tf_op jit(solution)/shard_map/ppermute | solution.py:18
